TPU v7x, 256 devices: a whole 4x4x8 slice. The times are simulated.
256 devices in a mesh: region: 8 (over z_lo, core), tile: 32 (over x, z_hi, y).
Axes of the slice: x: 4, y: 4, z: 8 (z_hi: 2, z_lo: 4; z = z_hi * 4 + z_lo), core: 2. Of those that a mesh axis runs over, the one named last changes fastest.
Arguments:
- ens_obs: bfloat16 [32768, 512], P(('region', 'tile')), may hold values from -6 to 6
- obs_values: float32 [32768], P(('region', 'tile')), may hold values from -8 to 8
- obs_var: float32 [32768], P(('region', 'tile')), may hold values from 0.25 to 4
- edge_up: int32 [8192], P(('region', 'tile')), may hold values from 0 to 127
- edge_down: int32 [8192], P(('region', 'tile')), may hold values from 0 to 127
- loc_local: float32 [512, 4096], P(('region', 'tile')), may hold values from 0.02 to 1
- loc_edge: float32 [512, 2048], P(('region', 'tile')), may hold values from 0.02 to 1
- states: bfloat16 [2, 65536, 512], P(None, ('region', 'tile')), may hold values from -6 to 6
- box_ids: int32 [65536], P(('region', 'tile')), may hold values from 0 to 1
Outputs:
- analysis: bfloat16 [2, 65536, 512], P(None, ('region', 'tile'))
All inputs are finite; a program needn't handle non-finite values.
Results may differ from a plain program's by a relative error of at most 0.0095.
Values may be sent and summed in bfloat16 or wider, within the bound.
No kernel may reach another device: no remote copies, remote signals or barrier semaphores. Data moves between devices by JAX's collectives and lax.ppermute only.
A program may use at most 128 MiB of HBM per device.

v0:
```python
import jax
import jax.numpy as jnp
from jax import lax
from jax.sharding import PartitionSpec as P


def passed_along(block, axis, distance):
    devices = range(lax.axis_size(axis))
    route = [(i - distance, i) for i in devices if i - distance in devices]
    return lax.ppermute(block, axis, route)


def obs_terms(anomaly, obs_info, weights):
    obs_scale = weights * obs_info[:, 0].astype(jnp.float32)[None, :]
    scaled = (anomaly[None] * obs_scale[:, :, None]).astype(jnp.bfloat16)
    gram_sum = jnp.einsum("bpi,pj->bij", scaled, anomaly, preferred_element_type=jnp.float32)
    weighted = (obs_scale * obs_info[:, 1].astype(jnp.float32)[None, :]).astype(jnp.bfloat16)
    innov_sum = jnp.einsum("bp,pj->bj", weighted, anomaly, preferred_element_type=jnp.float32)
    return (gram_sum, innov_sum)


def solve_one(chol_part, rhs_part):
    return jax.scipy.linalg.cho_solve((chol_part, True), rhs_part)


def make_transform(gram_sum, innov_sum):
    members = gram_sum.shape[-1]
    identity = jnp.eye(members, dtype=jnp.float32)
    system = gram_sum + (members - 1.0) * identity
    factor = jnp.linalg.cholesky(system)
    right_sides = jnp.concatenate(
        [jnp.broadcast_to(identity, system.shape), innov_sum[:, :, None]], axis=2
    )
    solved = jax.vmap(solve_one)(factor, right_sides)
    inverse = solved[:, :, :members]
    wbar = solved[:, :, members]
    transform = 0.5 * identity + 0.5 * (members - 1.0) * inverse + wbar[:, :, None]
    return transform.astype(jnp.bfloat16)


def body(ens_obs, obs_values, obs_var, edge_up, edge_down, loc_local, loc_edge, states, box_ids):
    record_count = ens_obs.shape[0]
    members = ens_obs.shape[1]
    ymean = jnp.mean(ens_obs, axis=1, dtype=jnp.float32)
    anomaly = (ens_obs.astype(jnp.float32) - ymean[:, None]).astype(jnp.bfloat16)
    obs_info = jnp.stack([1.0 / obs_var, obs_values - ymean], axis=1).astype(jnp.bfloat16)
    lower_a, lower_i = passed_along((anomaly[edge_up], obs_info[edge_up]), "region", 1)
    upper_a, upper_i = passed_along((anomaly[edge_down], obs_info[edge_down]), "region", -1)
    edge_anom = jnp.concatenate([lower_a, upper_a], axis=0)
    edge_info = jnp.concatenate([lower_i, upper_i], axis=0)
    block_anom = jnp.concatenate([anomaly, edge_anom], axis=0)
    block_info = jnp.concatenate([obs_info, edge_info], axis=0)
    all_anom, all_info = (
        lax.all_gather(block_anom, "tile", axis=0, tiled=True),
        lax.all_gather(block_info, "tile", axis=0, tiled=True),
    )
    tile_count = lax.axis_size("tile")
    pool_rows = block_anom.shape[0]
    all_anom = all_anom.reshape(tile_count, pool_rows, members)
    all_info = all_info.reshape(tile_count, pool_rows, 2)
    gram_one, innov_one = obs_terms(
        all_anom[:, :record_count].reshape(-1, members),
        all_info[:, :record_count].reshape(-1, 2),
        loc_local,
    )
    gram_two, innov_two = obs_terms(
        all_anom[:, record_count:].reshape(-1, members),
        all_info[:, record_count:].reshape(-1, 2),
        loc_edge,
    )
    transform = make_transform(gram_one + gram_two, innov_one + innov_two)
    smean = jnp.mean(states, axis=2, dtype=jnp.float32)
    state_anomaly = (states.astype(jnp.float32) - smean[:, :, None]).astype(jnp.bfloat16)
    updates = jnp.einsum(
        "fck,bkj->bfcj", state_anomaly, transform, preferred_element_type=jnp.float32
    )
    box_range = jnp.arange(transform.shape[0], dtype=jnp.int32)
    selector = (box_ids[None, :] == box_range[:, None]).astype(jnp.float32)
    total = jnp.sum(selector[:, None, :, None] * updates, axis=0)
    return (smean[:, :, None] + total).astype(jnp.bfloat16)


def solution(mesh):
    return jax.shard_map(
        body,
        mesh=mesh,
        in_specs=(
            P(("region", "tile"), None),
            P(("region", "tile")),
            P(("region", "tile")),
            P(("region", "tile")),
            P(("region", "tile")),
            P(("region", "tile"), None),
            P(("region", "tile"), None),
            P(None, ("region", "tile"), None),
            P(("region", "tile")),
        ),
        out_specs=P(None, ("region", "tile"), None),
        check_vma=False,
    )
```

profile of v0, /device:TPU:1, one launch (start us, length us, event | category | flops | bytes accessed | tf_op | source)
XLA Modules:
  0.0 507.3 jit_solution(1882238371529107905)
XLA Ops:
  10.5 5.1 %collective-permute-start.1 = (bf16[32,512]{1,0:T(8,128)(2,1)S(1)}, bf16[32,512]{1,0:T(8,128)(2,1)S(1)}, u32[]{:S(2)}, u32[]{:S(2)}) collective-permute-start(bf16[32,512]{1,0:T(8,128)(2,1)S(1)} %gather_fusion.1), channel_id=1, source_target_pairs={{32,0},{64,32},{96,64},{128,96},{160,128},{192,160},{224,192},{33,... | collective-permute-start | bytes 98312 | tf_op jit(solution)/shard_map/ppermute | solution.py:10
  24.4 3.9 collective-permute-start.2
  36.2 111.6 %all-gather = bf16[32,192,2]{1,2,0:T(2,128)(2,1)S(1)} all-gather(bf16[1,192,2]{1,2,0:T(2,128)(2,1)S(1)} %maximum_bitcast_fusion), channel_id=1, replica_groups=mesh['region'=8,'tile'=32] {'tile'}, dimensions={0}, use_global_device_ids=true | all-gather | bytes 25344 | tf_op jit(solution)/shard_map/all_gather | solution.py:55
  148.1 6.8 %all-gather.3.cloned.1.call-done = bf16[6144,512]{1,0:T(8,128)(2,1)} async-done(((bf16[192,512]{1,0:T(8,128)(2,1)}), bf16[6144,512]{1,0:T(8,128)(2,1)}) %all-gather.3.cloned.1.call-update) | async-done | bytes 6291472 | tf_op jit(solution)/shard_map/all_gather | solution.py:54
  157.5 3.3 slice.211
  160.8 4.7 bitcast_convert_fusion.1
  165.5 2.7 bitcast_convert_fusion
  169.8 9.0 %copy.124 = f32[4096,512]{0,1:T(8,128)} copy(f32[4096,512]{1,0:T(8,128)} %bitcast_convert_fusion.1) | data formatting | bytes 16777216 | tf_op jit(solution)/shard_map/convert_element_type | solution.py:15
  178.9 5.4 %copy.129 = f32[2048,512]{0,1:T(8,128)} copy(f32[2048,512]{1,0:T(8,128)} %bitcast_convert_fusion) | data formatting | bytes 8388608 | tf_op jit(solution)/shard_map/convert_element_type | solution.py:15
  184.3 10.6 %fusion = f32[2,512,512]{1,2,0:T(8,128)} fusion(bf16[4096,512,1]{1,0,2:T(8,128)(2,1)} %bitcast.111, f32[2,4096]{1,0:T(2,128)S(1)} %broadcast_multiply_fusion, f32[4096,512]{0,1:T(8,128)} %copy.124), kind=kOutput, calls=%fused_computation.7 | convolution fusion | flops 4303355904 | bytes 14712832 | tf_op jit(solution)/shard_map/bpi,pj->bij/dot_general | solution.py:16
  194.9 6.5 %broadcast_add_fusion = (f32[2,512,512]{1,2,0:T(8,128)}, f32[2,512,512]{1,2,0:T(8,128)}) fusion(f32[512,512]{0,1:T(8,128)} %copy.133, f32[2,512,512]{1,2,0:T(8,128)} %fusion, bf16[2048,512,1]{1,0,2:T(8,128)(2,1)S(1)} %bitcast.113, f32[2,2048]{1,0:T(2,128)S(1)} %broadcast_multiply_fusion.1, f32[2048,512]{0,1:T(8,128)S(1)} %copy-done.3), kind=kOutput, calls=%fused_computation.70 | convolution fusion | flops 2152726528 | bytes 13647872 | tf_op jit(solution)/shard_map/bpi,pj->bij/dot_general | solution.py:16
  207.1 23.9 %custom-call.38 = f32[2,128,128]{2,1,0:T(8,128)S(1)} custom-call(f32[2,128,128]{2,1,0:T(8,128)S(1)} %cholesky.274), custom_call_target="Cholesky" | custom-call | tf_op jit(solution)/shard_map/jit(cholesky)/cholesky | solution.py:30
  231.3 19.7 %custom-call.39 = f32[2,1,128,128]{2,3,1,0:T(8,128)S(1)} custom-call(f32[2,1,128,128]{3,2,1,0:T(8,128)S(1)} %select_bitcast_fusion.2), custom_call_target="InvertDiagBlocksLowerTriangular" | custom-call | tf_op jit(solution)/shard_map/jit(cholesky)/cholesky | solution.py:30
  254.7 24.9 %custom-call.40 = f32[2,128,128]{2,1,0:T(8,128)} custom-call(f32[2,128,128]{2,1,0:T(8,128)} %cholesky.278), custom_call_target="Cholesky" | custom-call | tf_op jit(solution)/shard_map/jit(cholesky)/cholesky | solution.py:30
  281.2 21.3 %custom-call.41 = f32[2,1,128,128]{2,3,1,0:T(8,128)} custom-call(f32[2,1,128,128]{3,2,1,0:T(8,128)} %get-tuple-element.30), custom_call_target="InvertDiagBlocksLowerTriangular" | custom-call | tf_op jit(solution)/shard_map/jit(cholesky)/cholesky | solution.py:30
  306.0 24.9 %custom-call.42 = f32[2,128,128]{2,1,0:T(8,128)} custom-call(f32[2,128,128]{2,1,0:T(8,128)} %cholesky.283), custom_call_target="Cholesky" | custom-call | tf_op jit(solution)/shard_map/jit(cholesky)/cholesky | solution.py:30
  332.5 21.1 %custom-call.43 = f32[2,1,128,128]{2,3,1,0:T(8,128)} custom-call(f32[2,1,128,128]{3,2,1,0:T(8,128)} %get-tuple-element.28), custom_call_target="InvertDiagBlocksLowerTriangular" | custom-call | tf_op jit(solution)/shard_map/jit(cholesky)/cholesky | solution.py:30
  356.3 23.5 %custom-call.44 = f32[2,128,128]{2,1,0:T(8,128)S(1)} custom-call(f32[2,128,128]{2,1,0:T(8,128)S(1)} %convolution_subtract_fusion.6), custom_call_target="Cholesky" | custom-call | tf_op jit(solution)/shard_map/jit(cholesky)/cholesky | solution.py:30
  384.0 14.8 %while.1 = (s32[]{:T(128)}, f32[2,512,512]{2,1,0:T(8,128)}, s32[4,2]{0,1:T(2,128)S(1)}, f32[4,2,128,128]{3,2,0,1:T(8,128)}, s32[]{:T(128)}) while((s32[]{:T(128)}, f32[2,512,512]{2,1,0:T(8,128)}, s32[4,2]{0,1:T(2,128)S(1)}, f32[4,2,128,128]{3,2,0,1:T(8,128)}, s32[]{:T(128)}) %tuple.31), condition=%wide.while_cond, body=%wide.while_body.sunk | while | flops 2 | bytes 263277 | solution.py:23
  384.7 3.0 bitcast_dynamic-update-slice_fusion.2
  388.4 3.0 bitcast_dynamic-update-slice_fusion.2
  392.1 3.0 bitcast_dynamic-update-slice_fusion.2
  395.8 3.0 bitcast_dynamic-update-slice_fusion.2
  398.8 79.6 %custom-call.45 = f32[2,4,128,128]{2,3,1,0:T(8,128)S(1)} custom-call(f32[2,4,128,128]{3,2,1,0:T(8,128)} %bitcast.121), custom_call_target="InvertDiagBlocksLowerTriangular" | custom-call | tf_op jit(solution)/shard_map/vmap(jit(_cho_solve))/triangular_solve | solution.py:23
  (134 shorter events, 72.4 us)
Async XLA Ops:
  6.5 148.3 %all-gather.3.cloned.1.call-start = ((), (), s32[]{:S(2)}) async-start(), calls=%async_computation | async-start | bytes 6488064 | tf_op jit(solution)/shard_map/all_gather | solution.py:54
  10.5 7.9 %collective-permute-start.1 = (bf16[32,512]{1,0:T(8,128)(2,1)S(1)}, bf16[32,512]{1,0:T(8,128)(2,1)S(1)}, u32[]{:S(2)}, u32[]{:S(2)}) collective-permute-start(bf16[32,512]{1,0:T(8,128)(2,1)S(1)} %gather_fusion.1), channel_id=1, source_target_pairs={{32,0},{64,32},{96,64},{128,96},{160,128},{192,160},{224,192},{33,... | collective-permute-start | bytes 98312 | tf_op jit(solution)/shard_map/ppermute | solution.py:10
  16.3 15.4 %copy-start.4 = (bf16[2,256,512]{2,1,0:T(8,128)(2,1)S(1)}, bf16[2,256,512]{2,1,0:T(8,128)(2,1)}, u32[]{:S(2)}) copy-start(bf16[2,256,512]{2,1,0:T(8,128)(2,1)} %param.16) | copy-start | bytes 1572868
  16.3 3.2 collective-permute-start
  21.7 14.3 %collective-permute-start.3 = (bf16[32,2]{1,0:T(8,128)(2,1)S(1)}, bf16[32,2]{1,0:T(8,128)(2,1)S(1)}, u32[]{:S(2)}, u32[]{:S(2)}) collective-permute-start(bf16[32,2]{1,0:T(8,128)(2,1)S(1)} %gather_fusion.3), channel_id=1, source_target_pairs={{32,0},{64,32},{96,64},{128,96},{160,128},{192,160},{224,192},{33,... | collective-permute-start | bytes 392 | tf_op jit(solution)/shard_map/ppermute | solution.py:10
  24.4 11.7 %collective-permute-start.2 = (bf16[32,2]{1,0:T(8,128)(2,1)S(1)}, bf16[32,2]{1,0:T(8,128)(2,1)S(1)}, u32[]{:S(2)}, u32[]{:S(2)}) collective-permute-start(bf16[32,2]{1,0:T(8,128)(2,1)S(1)} %gather_fusion.2), channel_id=1, source_target_pairs={{0,32},{32,64},{64,96},{96,128},{128,160},{160,192},{192,224},{1,3... | collective-permute-start | bytes 392 | tf_op jit(solution)/shard_map/ppermute | solution.py:10
  29.8 3.4 copy-start.13
  34.3 113.7 %copy-start.12 = (f32[2,2048]{1,0:T(2,128)S(1)}, f32[2,2048]{1,0:T(2,128)}, u32[]{:S(2)}) copy-start(f32[2,2048]{1,0:T(2,128)} %param.15) | copy-start | bytes 49156
  34.3 113.7 %copy-start.9 = (f32[2,4096]{1,0:T(2,128)S(1)}, f32[2,4096]{1,0:T(2,128)}, u32[]{:S(2)}) copy-start(f32[2,4096]{1,0:T(2,128)} %param.14) | copy-start | bytes 98308
  157.5 10.7 %copy-start = (bf16[32,128,512]{2,1,0:T(8,128)(2,1)}, bf16[32,128,512]{2,1,0:T(8,128)(2,1)S(1)}, u32[]{:S(2)}) copy-start(bf16[32,128,512]{2,1,0:T(8,128)(2,1)S(1)} %slice.208) | copy-start | bytes 12582916
  184.3 10.6 %copy-start.3 = (f32[2048,512]{0,1:T(8,128)S(1)}, f32[2048,512]{0,1:T(8,128)}, u32[]{:S(2)}) copy-start(f32[2048,512]{0,1:T(8,128)} %copy.129) | copy-start | bytes 12582916
  205.7 1.3 copy-start.2
  231.0 21.5 %copy-start.6 = (f32[2,128,128]{2,1,0:T(8,128)}, f32[2,128,128]{2,1,0:T(8,128)S(1)}, u32[]{:S(2)}) copy-start(f32[2,128,128]{2,1,0:T(8,128)S(1)} %custom-call.38) | copy-start | bytes 393220
  303.7 76.0 %copy-start.7 = (f32[2,128,128]{2,1,0:T(8,128)S(1)}, f32[2,128,128]{2,1,0:T(8,128)}, u32[]{:S(2)}) copy-start(f32[2,128,128]{2,1,0:T(8,128)} %copy-done.6) | copy-start | bytes 393220
  381.3 2.7 copy-start.14
  384.0 95.9 %copy-start.8 = (f32[2,512,1]{1,2,0:T(1,128)S(1)}, f32[2,512,1]{1,2,0:T(1,128)}, u32[]{:S(2)}) copy-start(f32[2,512,1]{1,2,0:T(1,128)} %copy.143) | copy-start | bytes 12292
  479.9 1.6 copy-start.1
  497.0 1.0 copy-start.5
  497.0 1.0 copy-start.10
  497.0 1.0 copy-start.11
Sparse Core Ops, SparseCore 0:
  20.4 134.4 all-gather.2
where the time goes:
time: 515 us; the launch traced here: 507 us
  other arithmetic  266 us (52%)
  blocking collectives  112 us (22%)
  local copies, waits for them, and re-layouts  50.7 us (10%)
  matrix products  43.7 us (8%)
  between operations  14.4 us (3%)
  starting transfers between devices  13.2 us (3%)
  waiting for transfers between devices  7.96 us (2%)
    another operation x18, other arithmetic, make_transform(): factor = jnp.linalg.cholesky(system)  165 us
    all_gather x1, blocking collectives, body(): lax.all_gather(block_info, 'tile', axis=0, tiled=True)  112 us
    another operation x5, other arithmetic, solve_one(): return jax.scipy.linalg.cho_solve((chol_part, True), rhs_part)  83.8 us
    dot_general x2, matrix products, obs_terms(): jnp.einsum('bpi,pj->bij', scaled, anomaly, preferred_element_type=jnp.flo...  17.1 us
    another operation x14, matrix products, solve_one(): return jax.scipy.linalg.cho_solve((chol_part, True), rhs_part)  16.2 us
    another operation x12, local copies, waits for them, and re-layouts  14.8 us
    convert_element_type x2, local copies, waits for them, and re-layouts, obs_terms(): scaled = (anomaly[None] * obs_scale[:, :, None]).astype(jnp.bfloat16)  14.4 us
    ppermute x4, starting transfers between devices, passed_along(): return lax.ppermute(block, axis, route)  13.2 us
  transfers between devices with their start and end apart: 5, of which 2 were waited for; matrix products, arithmetic and copies ran while one was open for 2% of the time, Pallas kernels for 0%

commit v1 on v0

v1 whole, which is shorter than its diff:
```python
import functools

import jax
import jax.numpy as jnp
from jax import lax
from jax.experimental import pallas as pl
from jax.experimental.pallas import tpu as pltpu
from jax.sharding import Mesh
from jax.sharding import PartitionSpec as P

HI = lax.Precision.HIGHEST
ROWS_PER_STEP = 1664


def passed_along(block, axis, distance):
    devices = range(lax.axis_size(axis))
    route = [(i - distance, i) for i in devices if i - distance in devices]
    return lax.ppermute(block, axis, route)


def _gram_kernel(a_ref, s_ref, w_ref, g_ref, v_ref):
    @pl.when(pl.program_id(0) == 0)
    def _():
        g_ref[...] = jnp.zeros(g_ref.shape, jnp.float32)
        v_ref[...] = jnp.zeros(v_ref.shape, jnp.float32)

    a = a_ref[...]
    af = a.astype(jnp.float32)
    for b in range(g_ref.shape[0]):
        sc = (af * s_ref[b]).astype(jnp.bfloat16)
        g_ref[b] += lax.dot_general(sc, a, (((0,), (0,)), ((), ())),
                                    preferred_element_type=jnp.float32)
    v_ref[...] += jnp.dot(w_ref[...], a, preferred_element_type=jnp.float32)


def gram_terms(pool, scale_col, weighted):
    rows, members = pool.shape
    boxes = scale_col.shape[0]
    wrows = weighted.shape[0]
    step = ROWS_PER_STEP
    return pl.pallas_call(
        _gram_kernel,
        grid=(rows // step,),
        in_specs=[
            pl.BlockSpec((step, members), lambda i: (i, 0)),
            pl.BlockSpec((boxes, step, 1), lambda i: (0, i, 0)),
            pl.BlockSpec((wrows, step), lambda i: (0, i)),
        ],
        out_specs=[
            pl.BlockSpec((boxes, members, members), lambda i: (0, 0, 0)),
            pl.BlockSpec((wrows, members), lambda i: (0, 0)),
        ],
        out_shape=[
            jax.ShapeDtypeStruct((boxes, members, members), jnp.float32),
            jax.ShapeDtypeStruct((wrows, members), jnp.float32),
        ],
    )(pool, scale_col, weighted)


def _transform_kernel(g_ref, v_ref, t_ref, m_ref, r_ref, *, nb):
    boxes, n, _ = g_ref.shape
    ridx = lax.broadcasted_iota(jnp.int32, (n, n), 0)
    cidx = lax.broadcasted_iota(jnp.int32, (n, n), 1)
    eye = (ridx == cidx).astype(jnp.float32)
    for b in range(boxes):
        m_ref[b] = g_ref[b] + (n - 1.0) * eye
    bi = lax.broadcasted_iota(jnp.int32, (nb, nb), 0)
    bj = lax.broadcasted_iota(jnp.int32, (nb, nb), 1)
    beye = (bi == bj).astype(jnp.float32)

    def pivot(k, blocks):
        rmask = bi == k
        cmask = bj == k
        out = []
        for d in blocks:
            row = jnp.sum(jnp.where(rmask, d, 0.0), axis=0, keepdims=True)
            col = jnp.sum(jnp.where(cmask, d, 0.0), axis=1, keepdims=True)
            p = jnp.sum(jnp.where(cmask[0:1], row, 0.0), axis=1, keepdims=True)
            pinv = 1.0 / p
            rown = row * pinv
            new = d - col * rown
            new = jnp.where(rmask, rown, new)
            new = jnp.where(cmask, -col * pinv, new)
            new = jnp.where(rmask & cmask, pinv, new)
            out.append(new)
        return tuple(out)

    for kb in range(n // nb):
        s = slice(kb * nb, (kb + 1) * nb)
        dinvs = lax.fori_loop(0, nb, pivot, tuple(m_ref[b, s, s] for b in range(boxes)))
        for b in range(boxes):
            dinv = dinvs[b]
            rn = jnp.dot(dinv, m_ref[b, s, :], precision=HI, preferred_element_type=jnp.float32)
            r_ref[b] = rn
            r_ref[b, :, s] = beye + dinv
            upd = jnp.dot(m_ref[b, :, s], r_ref[b], precision=HI, preferred_element_type=jnp.float32)
            m_ref[b] = m_ref[b] - upd
            m_ref[b, s, :] = rn
            m_ref[b, s, s] = dinv
    for b in range(boxes):
        inv = m_ref[b]
        wbar = jnp.sum(inv * v_ref[b:b + 1, :], axis=1, keepdims=True)
        t_ref[b] = (0.5 * eye + (0.5 * (n - 1.0)) * inv + wbar).astype(t_ref.dtype)


def make_transform(gram, innov_rows, nb=128):
    boxes, n, _ = gram.shape
    return pl.pallas_call(
        functools.partial(_transform_kernel, nb=nb),
        out_shape=jax.ShapeDtypeStruct((boxes, n, n), jnp.bfloat16),
        scratch_shapes=[pltpu.VMEM((boxes, n, n), jnp.float32),
                        pltpu.VMEM((boxes, nb, n), jnp.float32)],
    )(gram, innov_rows)


def body(ens_obs, obs_values, obs_var, edge_up, edge_down, loc_local, loc_edge, states, box_ids):
    record_count, members = ens_obs.shape
    nx, nz, ny = lax.axis_size("tx"), lax.axis_size("tz"), lax.axis_size("ty")
    boxes = loc_local.shape[0]
    ymean = jnp.mean(ens_obs, axis=1, dtype=jnp.float32)
    anomaly = (ens_obs.astype(jnp.float32) - ymean[:, None]).astype(jnp.bfloat16)
    inv_var = (1.0 / obs_var).astype(jnp.bfloat16)
    innov = (obs_values - ymean).astype(jnp.bfloat16)
    lower_a, lower_v, lower_i = passed_along(
        (anomaly[edge_up], inv_var[edge_up], innov[edge_up]), "region", 1)
    upper_a, upper_v, upper_i = passed_along(
        (anomaly[edge_down], inv_var[edge_down], innov[edge_down]), "region", -1)
    edge_rows = lower_a.shape[0] + upper_a.shape[0]
    pool_rows = record_count + edge_rows
    block_rows = ((pool_rows + 1 + 15) // 16) * 16
    info_row = jnp.concatenate(
        [inv_var, lower_v, upper_v, innov, lower_i, upper_i,
         jnp.zeros((members - 2 * pool_rows,), jnp.bfloat16)])
    block = jnp.concatenate(
        [anomaly, lower_a, upper_a, info_row[None],
         jnp.zeros((block_rows - pool_rows - 1, members), jnp.bfloat16)], axis=0)
    half = lax.all_gather(block, "tz", axis=0)
    full = lax.all_gather(half, ("tx", "ty"), axis=0)
    info = full[:, :, pool_rows, :2 * pool_rows].astype(jnp.float32)
    inv_all = info[:, :, :pool_rows]
    innov_all = info[:, :, pool_rows:]
    local_w = loc_local.reshape(boxes, nx, nz, ny, record_count)
    edge_w = loc_edge.reshape(boxes, nx, nz, ny, edge_rows)
    weights = jnp.concatenate([local_w, edge_w], axis=4).transpose(0, 1, 3, 2, 4)
    weights = weights.reshape(boxes, nx * ny, nz, pool_rows)
    obs_scale = weights * inv_all[None]
    weighted = (obs_scale * innov_all[None]).astype(jnp.bfloat16)
    pad = ((0, 0), (0, 0), (0, 0), (0, block_rows - pool_rows))
    scale_col = jnp.pad(obs_scale, pad).reshape(boxes, -1, 1)
    weighted = jnp.pad(weighted, pad).reshape(boxes, -1)
    weighted = jnp.pad(weighted, ((0, 16 - boxes), (0, 0)))
    gram, innov_sum = gram_terms(full.reshape(-1, members), scale_col, weighted)
    transform = make_transform(gram, innov_sum)
    smean = jnp.mean(states, axis=2, dtype=jnp.float32)
    state_anomaly = (states.astype(jnp.float32) - smean[:, :, None]).astype(jnp.bfloat16)
    updates = jnp.einsum(
        "fck,bkj->bfcj", state_anomaly, transform, preferred_element_type=jnp.float32
    )
    box_range = jnp.arange(boxes, dtype=jnp.int32)
    selector = (box_ids[None, :] == box_range[:, None]).astype(jnp.float32)
    total = jnp.sum(selector[:, None, :, None] * updates, axis=0)
    return (smean[:, :, None] + total).astype(jnp.bfloat16)


def solution(mesh):
    n_region, n_tile = mesh.devices.shape
    nz = 2
    nx = 4
    ny = n_tile // (nx * nz)
    fine = Mesh(mesh.devices.reshape(n_region, nx, nz, ny), ("region", "tx", "tz", "ty"))
    flat = ("region", "tx", "tz", "ty")
    return jax.shard_map(
        body,
        mesh=fine,
        in_specs=(
            P(flat, None),
            P(flat),
            P(flat),
            P(flat),
            P(flat),
            P(flat, None),
            P(flat, None),
            P(None, flat, None),
            P(flat),
        ),
        out_specs=P(None, flat, None),
        check_vma=False,
    )
```

time: 515 us -> 238 us (0.46); the launches traced: 507 us -> 237 us
  other arithmetic: 266 us -> 5.96 us
  Pallas kernels: 0 us -> 97.7 us
  blocking collectives: 112 us -> 15 us
  waiting for transfers between devices: 7.96 us -> 72.9 us
  matrix products: 43.7 us -> 2.17 us
  local copies, waits for them, and re-layouts: 50.7 us -> 11.8 us
    another operation x26 -> x0, other arithmetic: 250 us -> none  [the longest x18 165 us: make_transform(): factor = jnp.linalg.cholesky(system)]
    pallas_call x0 -> x2, Pallas kernels: none -> 97.7 us  [the longest x1 84.9 us: make_transform(): pl.pallas_call(functools.partial(_transform_kernel, nb=nb), out_shape=jax...]
    all_gather x1, blocking collectives: 112 us -> 15 us  [body(): half = lax.all_gather(block, 'tz', axis=0)]
    all_gather x1, waiting for transfers between devices: 6.78 us -> 69.9 us  [body(): full = lax.all_gather(half, ('tx', 'ty'), axis=0)]
    another operation x20 -> x0, matrix products: 24.8 us -> none  [the longest x14 16.2 us: solve_one(): return jax.scipy.linalg.cho_solve((chol_part, True), rhs_part)]
    dot_general x4 -> x0, matrix products: 18.1 us -> none  [the longest x2 17.1 us: obs_terms(): jnp.einsum('bpi,pj->bij', scaled, anomaly, preferred_element_type=jnp.flo...]
    another operation x18 -> x0, local copies, waits for them, and re-layouts: 16.5 us -> none
    convert_element_type x3 -> x0, local copies, waits for them, and re-layouts: 15.9 us -> none  [the longest x2 14.4 us: obs_terms(): scaled = (anomaly[None] * obs_scale[:, :, None]).astype(jnp.bfloat16)]
  transfers between devices with their start and end apart: 5 -> 7, of which waited for: 2 -> 2; matrix products, arithmetic and copies ran while one was open for 2% -> 3% of each run, Pallas kernels for 0% -> 0%
where the time goes in v1:
time: 238 us; the launch traced here: 237 us
  Pallas kernels  97.7 us (41%)
  waiting for transfers between devices  72.9 us (31%)
  starting transfers between devices  18.1 us (8%)
  blocking collectives  15 us (6%)
  between operations  13.6 us (6%)
  local copies, waits for them, and re-layouts  11.8 us (5%)
  other arithmetic  5.96 us (3%)
    pallas_call x1, Pallas kernels, make_transform(): pl.pallas_call(functools.partial(_transform_kernel, nb=nb), out_shape=jax...  84.9 us
    all_gather x1, waiting for transfers between devices, body(): full = lax.all_gather(half, ('tx', 'ty'), axis=0)  69.9 us
    ppermute x6, starting transfers between devices, passed_along(): return lax.ppermute(block, axis, route)  18.1 us
    all_gather x1, blocking collectives, body(): half = lax.all_gather(block, 'tz', axis=0)  15 us
    pallas_call x1, Pallas kernels, gram_terms(): pl.pallas_call(_gram_kernel, grid=(rows // step,), in_specs=[pl.BlockSpec...  12.8 us
    reshape x1, local copies, waits for them, and re-layouts, body(): scale_col = jnp.pad(obs_scale, pad).reshape(boxes, -1, 1)  5.28 us
  transfers between devices with their start and end apart: 7, of which 2 were waited for; matrix products, arithmetic and copies ran while one was open for 3% of the time, Pallas kernels for 0%

profile of v1, /device:TPU:1, one launch (start us, length us, event | category | flops | bytes accessed | tf_op | source)
XLA Modules:
  0.0 237.3 jit_solution(16684836690553096226)
XLA Ops:
  6.5 1.0 convert_reduce_fusion.1
  7.5 0.7 compare_select_fusion.1
  8.9 0.7 gather_fusion.4
  9.6 5.1 %collective-permute-start.4 = (bf16[32]{0:T(256)(128)(2,1)S(1)}, bf16[32]{0:T(256)(128)(2,1)S(1)}, u32[]{:S(2)}, u32[]{:S(2)}) collective-permute-start(bf16[32]{0:T(256)(128)(2,1)S(1)} %gather_fusion.4), channel_id=1, source_target_pairs={{0,32},{32,64},{64,96},{96,128},{128,160},{160,192},{192,224},{1,3... | collective-permute-start | bytes 200 | tf_op jit(solution)/shard_map/ppermute | solution.py:18
  15.4 0.7 gather_fusion.5
  16.1 1.9 collective-permute-start.5
  18.0 1.0 fusion.6
  19.6 3.6 %collective-permute-start = (bf16[32,512]{1,0:T(8,128)(2,1)S(1)}, bf16[32,512]{1,0:T(8,128)(2,1)S(1)}, u32[]{:S(2)}, u32[]{:S(2)}) collective-permute-start(bf16[32,512]{1,0:T(8,128)(2,1)S(1)} %gather_fusion), channel_id=1, source_target_pairs={{0,32},{32,64},{64,96},{96,128},{128,160},{160,192},{192,224},{1,3... | collective-permute-start | bytes 98312 | tf_op jit(solution)/shard_map/ppermute | solution.py:18
  23.9 1.9 collective-permute-start.1
  25.8 0.7 divide_convert_fusion
  26.5 0.7 gather_fusion.2
  27.2 3.6 %collective-permute-start.2 = (bf16[32]{0:T(256)(128)(2,1)S(1)}, bf16[32]{0:T(256)(128)(2,1)S(1)}, u32[]{:S(2)}, u32[]{:S(2)}) collective-permute-start(bf16[32]{0:T(256)(128)(2,1)S(1)} %gather_fusion.2), channel_id=1, source_target_pairs={{0,32},{32,64},{64,96},{96,128},{128,160},{160,192},{192,224},{1,3... | collective-permute-start | bytes 200 | tf_op jit(solution)/shard_map/ppermute | solution.py:18
  30.8 0.7 gather_fusion.3
  31.6 1.9 collective-permute-start.3
  33.5 2.9 %collective-permute-done.3 = bf16[32]{0:T(256)(128)(2,1)S(1)} collective-permute-done((bf16[32]{0:T(256)(128)(2,1)S(1)}, bf16[32]{0:T(256)(128)(2,1)S(1)}, u32[]{:S(2)}, u32[]{:S(2)}) %collective-permute-start.3) | collective-permute-done | bytes 96 | tf_op jit(solution)/shard_map/ppermute | solution.py:18
  36.7 15.0 %all-gather = bf16[416,512]{1,0:T(8,128)(2,1)} all-gather(bf16[208,512]{1,0:T(8,128)(2,1)S(1)} %concatenate.10), channel_id=2, replica_groups=mesh['region'=8,'tx'=4,'tz'=2,'ty'=4] {'tz'}, dimensions={0}, use_global_device_ids=true | all-gather | bytes 638976 | tf_op jit(solution)/shard_map/all_gather | solution.py:137
  52.1 69.9 %all-gather.4.cloned.1.call-done = bf16[32,208,512]{2,1,0:T(8,128)(2,1)} async-done(((bf16[2,208,512]{2,1,0:T(8,128)(2,1)}), bf16[32,208,512]{2,1,0:T(8,128)(2,1)}) %all-gather.4.cloned.1.call-update) | async-done | bytes 6815760 | tf_op jit(solution)/shard_map/all_gather | solution.py:138
  122.1 1.0 slice_convert_fusion
  123.2 5.3 %reshape.113.s_ref = f32[2,6656,1]{2,1,0:T(8,128)} reshape(f32[2,16,2,208]{3,2,1,0:T(2,128)S(1)} %pad.12) | data formatting | bytes 106496 | tf_op jit(solution)/shard_map/reshape | solution.py:149
  128.7 0.7 pad.14.w_ref
  129.4 12.8 %shard_map.91 = (f32[2,512,512]{2,1,0:T(8,128)}, f32[16,512]{1,0:T(8,128)}) custom-call(bf16[6656,512]{1,0:T(8,128)(2,1)} %bitcast.20, f32[2,6656,1]{2,1,0:T(8,128)} %reshape.113.s_ref, bf16[16,6656]{1,0:T(8,128)(2,1)} %pad.14.w_ref), custom_call_target="tpu_custom_call" | custom-call | tf_op jit(solution)/shard_map/pallas_call | solution.py:41
  142.2 84.9 %shard_map.92 = bf16[2,512,512]{2,1,0:T(8,128)(2,1)} custom-call(f32[2,512,512]{2,1,0:T(8,128)} %get-tuple-element.7.g_ref, f32[16,512]{1,0:T(8,128)} %get-tuple-element.8.v_ref), custom_call_target="tpu_custom_call" | custom-call | tf_op jit(solution)/shard_map/pallas_call | solution.py:108
  227.1 2.2 multiply_reduce_fusion
  229.4 1.0 copy.20
  (40 shorter events, 3.7 us)
Async XLA Ops:
  6.5 115.5 %all-gather.4.cloned.1.call-start = ((), (), s32[]{:S(2)}) async-start(), calls=%async_computation | async-start | bytes 7241728 | tf_op jit(solution)/shard_map/all_gather | solution.py:138
  9.6 42.1 %copy-start.1 = (f32[2,4096]{1,0:T(2,128)S(1)}, f32[2,4096]{1,0:T(2,128)}, u32[]{:S(2)}) copy-start(f32[2,4096]{1,0:T(2,128)} %param.14) | copy-start | bytes 98308
  9.6 42.2 %copy-start.2 = (f32[2,2048]{1,0:T(2,128)S(1)}, f32[2,2048]{1,0:T(2,128)}, u32[]{:S(2)}) copy-start(f32[2,2048]{1,0:T(2,128)} %param.15) | copy-start | bytes 49156
  9.6 21.9 %collective-permute-start.4 = (bf16[32]{0:T(256)(128)(2,1)S(1)}, bf16[32]{0:T(256)(128)(2,1)S(1)}, u32[]{:S(2)}, u32[]{:S(2)}) collective-permute-start(bf16[32]{0:T(256)(128)(2,1)S(1)} %gather_fusion.4), channel_id=1, source_target_pairs={{0,32},{32,64},{64,96},{96,128},{128,160},{160,192},{192,224},{1,3... | collective-permute-start | bytes 200 | tf_op jit(solution)/shard_map/ppermute | solution.py:18
  15.4 36.6 %copy-start = (bf16[2,256,512]{2,1,0:T(8,128)(2,1)S(1)}, bf16[2,256,512]{2,1,0:T(8,128)(2,1)}, u32[]{:S(2)}) copy-start(bf16[2,256,512]{2,1,0:T(8,128)(2,1)} %param.16) | copy-start | bytes 1572868
  16.1 17.4 %collective-permute-start.5 = (bf16[32]{0:T(256)(128)(2,1)S(1)}, bf16[32]{0:T(256)(128)(2,1)S(1)}, u32[]{:S(2)}, u32[]{:S(2)}) collective-permute-start(bf16[32]{0:T(256)(128)(2,1)S(1)} %gather_fusion.5), channel_id=1, source_target_pairs={{32,0},{64,32},{96,64},{128,96},{160,128},{192,160},{224,192},{33,... | collective-permute-start | bytes 200 | tf_op jit(solution)/shard_map/ppermute | solution.py:18
  19.0 33.1 %copy-start.3 = (s32[256]{0:T(256)S(1)}, s32[256]{0:T(256)}, u32[]{:S(2)}) copy-start(s32[256]{0:T(256)} %param.17) | copy-start | bytes 3076
  19.6 16.9 %collective-permute-start = (bf16[32,512]{1,0:T(8,128)(2,1)S(1)}, bf16[32,512]{1,0:T(8,128)(2,1)S(1)}, u32[]{:S(2)}, u32[]{:S(2)}) collective-permute-start(bf16[32,512]{1,0:T(8,128)(2,1)S(1)} %gather_fusion), channel_id=1, source_target_pairs={{0,32},{32,64},{64,96},{96,128},{128,160},{160,192},{192,224},{1,3... | collective-permute-start | bytes 98312 | tf_op jit(solution)/shard_map/ppermute | solution.py:18
  23.9 12.6 %collective-permute-start.1 = (bf16[32,512]{1,0:T(8,128)(2,1)S(1)}, bf16[32,512]{1,0:T(8,128)(2,1)S(1)}, u32[]{:S(2)}, u32[]{:S(2)}) collective-permute-start(bf16[32,512]{1,0:T(8,128)(2,1)S(1)} %gather_fusion.1), channel_id=1, source_target_pairs={{32,0},{64,32},{96,64},{128,96},{160,128},{192,160},{224,192},{33,... | collective-permute-start | bytes 98312 | tf_op jit(solution)/shard_map/ppermute | solution.py:18
  27.2 6.3 %collective-permute-start.2 = (bf16[32]{0:T(256)(128)(2,1)S(1)}, bf16[32]{0:T(256)(128)(2,1)S(1)}, u32[]{:S(2)}, u32[]{:S(2)}) collective-permute-start(bf16[32]{0:T(256)(128)(2,1)S(1)} %gather_fusion.2), channel_id=1, source_target_pairs={{0,32},{32,64},{64,96},{96,128},{128,160},{160,192},{192,224},{1,3... | collective-permute-start | bytes 200 | tf_op jit(solution)/shard_map/ppermute | solution.py:18
  31.6 4.9 %collective-permute-start.3 = (bf16[32]{0:T(256)(128)(2,1)S(1)}, bf16[32]{0:T(256)(128)(2,1)S(1)}, u32[]{:S(2)}, u32[]{:S(2)}) collective-permute-start(bf16[32]{0:T(256)(128)(2,1)S(1)} %gather_fusion.3), channel_id=1, source_target_pairs={{32,0},{64,32},{96,64},{128,96},{160,128},{192,160},{224,192},{33,... | collective-permute-start | bytes 200 | tf_op jit(solution)/shard_map/ppermute | solution.py:18
Sparse Core Ops, SparseCore 0:
  51.8 70.2 all-gather.3

commit v2 on v1

--- a/solution.py
+++ b/solution.py
@@ -26,16 +26,24 @@
 
     a = a_ref[...]
     af = a.astype(jnp.float32)
+    sv = s_ref[...]
+    lanes = 128
+    eye = (lax.broadcasted_iota(jnp.int32, (lanes, lanes), 0)
+           == lax.broadcasted_iota(jnp.int32, (lanes, lanes), 1))
     for b in range(g_ref.shape[0]):
-        sc = (af * s_ref[b]).astype(jnp.bfloat16)
+        cols = [jnp.sum(jnp.where(eye, sv[b:b + 1, c * lanes:(c + 1) * lanes], 0.0),
+                        axis=1, keepdims=True)
+                for c in range(a.shape[0] // lanes)]
+        sc = (af * jnp.concatenate(cols, axis=0)).astype(jnp.bfloat16)
         g_ref[b] += lax.dot_general(sc, a, (((0,), (0,)), ((), ())),
                                     preferred_element_type=jnp.float32)
     v_ref[...] += jnp.dot(w_ref[...], a, preferred_element_type=jnp.float32)
 
 
-def gram_terms(pool, scale_col, weighted):
+def gram_terms(pool, scale_rows, weighted, gram_boxes):
     rows, members = pool.shape
-    boxes = scale_col.shape[0]
+    boxes = gram_boxes
+    srows = scale_rows.shape[0]
     wrows = weighted.shape[0]
     step = ROWS_PER_STEP
     return pl.pallas_call(
@@ -43,7 +51,7 @@
         grid=(rows // step,),
         in_specs=[
             pl.BlockSpec((step, members), lambda i: (i, 0)),
-            pl.BlockSpec((boxes, step, 1), lambda i: (0, i, 0)),
+            pl.BlockSpec((srows, step), lambda i: (0, i)),
             pl.BlockSpec((wrows, step), lambda i: (0, i)),
         ],
         out_specs=[
@@ -54,7 +62,7 @@
             jax.ShapeDtypeStruct((boxes, members, members), jnp.float32),
             jax.ShapeDtypeStruct((wrows, members), jnp.float32),
         ],
-    )(pool, scale_col, weighted)
+    )(pool, scale_rows, weighted)
 
 
 def _transform_kernel(g_ref, v_ref, t_ref, m_ref, r_ref, *, nb):
@@ -68,26 +76,35 @@
     bj = lax.broadcasted_iota(jnp.int32, (nb, nb), 1)
     beye = (bi == bj).astype(jnp.float32)
 
-    def pivot(k, blocks):
-        rmask = bi == k
-        cmask = bj == k
+    def pivot(step, blocks):
+        k = 2 * step
+        rk, rk1 = bi == k, bi == k + 1
+        lk, lk1 = bj[0:1] == k, bj[0:1] == k + 1
         out = []
         for d in blocks:
-            row = jnp.sum(jnp.where(rmask, d, 0.0), axis=0, keepdims=True)
-            col = jnp.sum(jnp.where(cmask, d, 0.0), axis=1, keepdims=True)
-            p = jnp.sum(jnp.where(cmask[0:1], row, 0.0), axis=1, keepdims=True)
-            pinv = 1.0 / p
-            rown = row * pinv
-            new = d - col * rown
-            new = jnp.where(rmask, rown, new)
-            new = jnp.where(cmask, -col * pinv, new)
-            new = jnp.where(rmask & cmask, pinv, new)
-            out.append(new)
+            r1 = jnp.sum(jnp.where(rk, d, 0.0), axis=0, keepdims=True)
+            r2 = jnp.sum(jnp.where(rk1, d, 0.0), axis=0, keepdims=True)
+            c1 = jnp.sum(jnp.where(bj == k, d, 0.0), axis=1, keepdims=True)
+            c2 = jnp.sum(jnp.where(bj == k + 1, d, 0.0), axis=1, keepdims=True)
+            a = jnp.sum(jnp.where(lk, r1, 0.0), axis=1, keepdims=True)
+            b = jnp.sum(jnp.where(lk1, r1, 0.0), axis=1, keepdims=True)
+            c = jnp.sum(jnp.where(lk, r2, 0.0), axis=1, keepdims=True)
+            e = jnp.sum(jnp.where(lk1, r2, 0.0), axis=1, keepdims=True)
+            rdet = 1.0 / (a * e - b * c)
+            q11, q12, q21, q22 = e * rdet, -b * rdet, -c * rdet, a * rdet
+            rn1 = q11 * r1 + q12 * r2
+            rn2 = q21 * r1 + q22 * r2
+            f1 = jnp.where(lk, 1.0 + q11, jnp.where(lk1, q12, rn1))
+            f2 = jnp.where(lk, q21, jnp.where(lk1, 1.0 + q22, rn2))
+            g1 = jnp.where(lk, q11, jnp.where(lk1, q12, rn1))
+            g2 = jnp.where(lk, q21, jnp.where(lk1, q22, rn2))
+            new = d - c1 * f1 - c2 * f2
+            out.append(jnp.where(rk, g1, jnp.where(rk1, g2, new)))
         return tuple(out)
 
     for kb in range(n // nb):
         s = slice(kb * nb, (kb + 1) * nb)
-        dinvs = lax.fori_loop(0, nb, pivot, tuple(m_ref[b, s, s] for b in range(boxes)))
+        dinvs = lax.fori_loop(0, nb // 2, pivot, tuple(m_ref[b, s, s] for b in range(boxes)))
         for b in range(boxes):
             dinv = dinvs[b]
             rn = jnp.dot(dinv, m_ref[b, s, :], precision=HI, preferred_element_type=jnp.float32)
@@ -146,10 +163,11 @@
     obs_scale = weights * inv_all[None]
     weighted = (obs_scale * innov_all[None]).astype(jnp.bfloat16)
     pad = ((0, 0), (0, 0), (0, 0), (0, block_rows - pool_rows))
-    scale_col = jnp.pad(obs_scale, pad).reshape(boxes, -1, 1)
+    scale_rows = jnp.pad(obs_scale, pad).reshape(boxes, -1)
+    scale_rows = jnp.pad(scale_rows, ((0, 8 - boxes), (0, 0)))
     weighted = jnp.pad(weighted, pad).reshape(boxes, -1)
     weighted = jnp.pad(weighted, ((0, 16 - boxes), (0, 0)))
-    gram, innov_sum = gram_terms(full.reshape(-1, members), scale_col, weighted)
+    gram, innov_sum = gram_terms(full.reshape(-1, members), scale_rows, weighted, boxes)
     transform = make_transform(gram, innov_sum)
     smean = jnp.mean(states, axis=2, dtype=jnp.float32)
     state_anomaly = (states.astype(jnp.float32) - smean[:, :, None]).astype(jnp.bfloat16)

time: 238 us -> 210 us (0.88)
  Pallas kernels: 97.7 us -> 74.1 us
  local copies, waits for them, and re-layouts: 11.8 us -> 7.43 us
    pallas_call x1, Pallas kernels: 84.9 us -> 57.5 us  [make_transform(): pl.pallas_call(functools.partial(_transform_kernel, nb=nb), out_shape=jax...]
    reshape x1, local copies, waits for them, and re-layouts: 5.28 us -> 0.16 us  [body(): scale_rows = jnp.pad(obs_scale, pad).reshape(boxes, -1)]
    pallas_call x1, Pallas kernels: 12.8 us -> 16.5 us  [gram_terms(): pl.pallas_call(_gram_kernel, grid=(rows // step,), in_specs=[pl.BlockSpec...]
where the time goes in v2:
time: 210 us; the launch traced here: 209 us
  Pallas kernels  74.1 us (35%)
  waiting for transfers between devices  72.9 us (35%)
  starting transfers between devices  18.1 us (9%)
  blocking collectives  15 us (7%)
  between operations  13.6 us (6%)
  local copies, waits for them, and re-layouts  7.43 us (4%)
  other arithmetic  5.96 us (3%)
  matrix products  2.17 us (1%)
    all_gather x1, waiting for transfers between devices, body(): full = lax.all_gather(half, ('tx', 'ty'), axis=0)  69.9 us
    pallas_call x1, Pallas kernels, make_transform(): pl.pallas_call(functools.partial(_transform_kernel, nb=nb), out_shape=jax...  57.5 us
    ppermute x6, starting transfers between devices, passed_along(): return lax.ppermute(block, axis, route)  18.1 us
    pallas_call x1, Pallas kernels, gram_terms(): pl.pallas_call(_gram_kernel, grid=(rows // step,), in_specs=[pl.BlockSpec...  16.5 us
    all_gather x1, blocking collectives, body(): half = lax.all_gather(block, 'tz', axis=0)  15 us
  transfers between devices with their start and end apart: 7, of which 2 were waited for; matrix products, arithmetic and copies ran while one was open for 3% of the time, Pallas kernels for 0%

profile of v2, /device:TPU:1, one launch (start us, length us, event | category | flops | bytes accessed | tf_op | source)
XLA Modules:
  0.0 209.2 jit_solution(18096616772841365022)
XLA Ops:
  6.5 1.0 convert_reduce_fusion.1
  7.5 0.7 compare_select_fusion.1
  8.9 0.7 gather_fusion.4
  9.6 5.1 %collective-permute-start.4 = (bf16[32]{0:T(256)(128)(2,1)S(1)}, bf16[32]{0:T(256)(128)(2,1)S(1)}, u32[]{:S(2)}, u32[]{:S(2)}) collective-permute-start(bf16[32]{0:T(256)(128)(2,1)S(1)} %gather_fusion.4), channel_id=1, source_target_pairs={{0,32},{32,64},{64,96},{96,128},{128,160},{160,192},{192,224},{1,3... | collective-permute-start | bytes 200 | tf_op jit(solution)/shard_map/ppermute | solution.py:18
  15.4 0.7 gather_fusion.5
  16.1 1.9 collective-permute-start.5
  18.0 1.0 fusion.6
  19.6 3.6 %collective-permute-start = (bf16[32,512]{1,0:T(8,128)(2,1)S(1)}, bf16[32,512]{1,0:T(8,128)(2,1)S(1)}, u32[]{:S(2)}, u32[]{:S(2)}) collective-permute-start(bf16[32,512]{1,0:T(8,128)(2,1)S(1)} %gather_fusion), channel_id=1, source_target_pairs={{0,32},{32,64},{64,96},{96,128},{128,160},{160,192},{192,224},{1,3... | collective-permute-start | bytes 98312 | tf_op jit(solution)/shard_map/ppermute | solution.py:18
  23.9 1.9 collective-permute-start.1
  25.8 0.7 divide_convert_fusion
  26.5 0.7 gather_fusion.2
  27.2 3.6 %collective-permute-start.2 = (bf16[32]{0:T(256)(128)(2,1)S(1)}, bf16[32]{0:T(256)(128)(2,1)S(1)}, u32[]{:S(2)}, u32[]{:S(2)}) collective-permute-start(bf16[32]{0:T(256)(128)(2,1)S(1)} %gather_fusion.2), channel_id=1, source_target_pairs={{0,32},{32,64},{64,96},{96,128},{128,160},{160,192},{192,224},{1,3... | collective-permute-start | bytes 200 | tf_op jit(solution)/shard_map/ppermute | solution.py:18
  30.8 0.7 gather_fusion.3
  31.6 1.9 collective-permute-start.3
  33.5 2.9 %collective-permute-done.3 = bf16[32]{0:T(256)(128)(2,1)S(1)} collective-permute-done((bf16[32]{0:T(256)(128)(2,1)S(1)}, bf16[32]{0:T(256)(128)(2,1)S(1)}, u32[]{:S(2)}, u32[]{:S(2)}) %collective-permute-start.3) | collective-permute-done | bytes 96 | tf_op jit(solution)/shard_map/ppermute | solution.py:18
  36.7 15.0 %all-gather = bf16[416,512]{1,0:T(8,128)(2,1)} all-gather(bf16[208,512]{1,0:T(8,128)(2,1)S(1)} %concatenate.10), channel_id=2, replica_groups=mesh['region'=8,'tx'=4,'tz'=2,'ty'=4] {'tz'}, dimensions={0}, use_global_device_ids=true | all-gather | bytes 638976 | tf_op jit(solution)/shard_map/all_gather | solution.py:154
  52.1 69.9 %all-gather.4.cloned.1.call-done = bf16[32,208,512]{2,1,0:T(8,128)(2,1)} async-done(((bf16[2,208,512]{2,1,0:T(8,128)(2,1)}), bf16[32,208,512]{2,1,0:T(8,128)(2,1)}) %all-gather.4.cloned.1.call-update) | async-done | bytes 6815760 | tf_op jit(solution)/shard_map/all_gather | solution.py:155
  122.1 1.0 slice_convert_fusion
  123.4 0.7 pad.17.s_ref
  124.3 0.7 pad.19.w_ref
  125.0 16.5 %shard_map.91 = (f32[2,512,512]{2,1,0:T(8,128)}, f32[16,512]{1,0:T(8,128)}) custom-call(bf16[6656,512]{1,0:T(8,128)(2,1)} %bitcast.20, f32[8,6656]{1,0:T(8,128)} %pad.17.s_ref, bf16[16,6656]{1,0:T(8,128)(2,1)} %pad.19.w_ref), custom_call_target="tpu_custom_call" | custom-call | tf_op jit(solution)/shard_map/pallas_call | solution.py:49
  141.5 57.5 %shard_map.92 = bf16[2,512,512]{2,1,0:T(8,128)(2,1)} custom-call(f32[2,512,512]{2,1,0:T(8,128)} %get-tuple-element.7.g_ref, f32[16,512]{1,0:T(8,128)} %get-tuple-element.8.v_ref), custom_call_target="tpu_custom_call" | custom-call | tf_op jit(solution)/shard_map/pallas_call | solution.py:125
  199.1 2.2 %multiply_reduce_fusion = f32[512,2,256]{2,0,1:T(8,128)S(1)} fusion(bf16[2,512,512]{2,1,0:T(8,128)(2,1)} %shard_map.92, f32[2,256]{1,0:T(2,128)S(1)} %compare_convert_fusion, bf16[2,256,512]{2,1,0:T(8,128)(2,1)S(1)} %copy-done, f32[2,256]{1,0:T(2,128)S(1)} %broadcast_multiply_fusion.1), kind=kOutput, calls=%fused_computation.6 | convolution fusion | flops 538443776 | bytes 2625536 | tf_op jit(solution)/shard_map/fck,bkj->bfcj/dot_general | solution.py:174
  201.3 1.0 copy.18
  (41 shorter events, 3.9 us)
Async XLA Ops:
  6.5 115.5 %all-gather.4.cloned.1.call-start = ((), (), s32[]{:S(2)}) async-start(), calls=%async_computation | async-start | bytes 7241728 | tf_op jit(solution)/shard_map/all_gather | solution.py:155
  9.6 42.1 %copy-start.1 = (f32[2,4096]{1,0:T(2,128)S(1)}, f32[2,4096]{1,0:T(2,128)}, u32[]{:S(2)}) copy-start(f32[2,4096]{1,0:T(2,128)} %param.14) | copy-start | bytes 98308
  9.6 42.2 %copy-start.2 = (f32[2,2048]{1,0:T(2,128)S(1)}, f32[2,2048]{1,0:T(2,128)}, u32[]{:S(2)}) copy-start(f32[2,2048]{1,0:T(2,128)} %param.15) | copy-start | bytes 49156
  9.6 21.9 %collective-permute-start.4 = (bf16[32]{0:T(256)(128)(2,1)S(1)}, bf16[32]{0:T(256)(128)(2,1)S(1)}, u32[]{:S(2)}, u32[]{:S(2)}) collective-permute-start(bf16[32]{0:T(256)(128)(2,1)S(1)} %gather_fusion.4), channel_id=1, source_target_pairs={{0,32},{32,64},{64,96},{96,128},{128,160},{160,192},{192,224},{1,3... | collective-permute-start | bytes 200 | tf_op jit(solution)/shard_map/ppermute | solution.py:18
  15.4 36.6 %copy-start = (bf16[2,256,512]{2,1,0:T(8,128)(2,1)S(1)}, bf16[2,256,512]{2,1,0:T(8,128)(2,1)}, u32[]{:S(2)}) copy-start(bf16[2,256,512]{2,1,0:T(8,128)(2,1)} %param.16) | copy-start | bytes 1572868
  16.1 17.4 %collective-permute-start.5 = (bf16[32]{0:T(256)(128)(2,1)S(1)}, bf16[32]{0:T(256)(128)(2,1)S(1)}, u32[]{:S(2)}, u32[]{:S(2)}) collective-permute-start(bf16[32]{0:T(256)(128)(2,1)S(1)} %gather_fusion.5), channel_id=1, source_target_pairs={{32,0},{64,32},{96,64},{128,96},{160,128},{192,160},{224,192},{33,... | collective-permute-start | bytes 200 | tf_op jit(solution)/shard_map/ppermute | solution.py:18
  19.0 33.1 %copy-start.3 = (s32[256]{0:T(256)S(1)}, s32[256]{0:T(256)}, u32[]{:S(2)}) copy-start(s32[256]{0:T(256)} %param.17) | copy-start | bytes 3076
  19.6 16.9 %collective-permute-start = (bf16[32,512]{1,0:T(8,128)(2,1)S(1)}, bf16[32,512]{1,0:T(8,128)(2,1)S(1)}, u32[]{:S(2)}, u32[]{:S(2)}) collective-permute-start(bf16[32,512]{1,0:T(8,128)(2,1)S(1)} %gather_fusion), channel_id=1, source_target_pairs={{0,32},{32,64},{64,96},{96,128},{128,160},{160,192},{192,224},{1,3... | collective-permute-start | bytes 98312 | tf_op jit(solution)/shard_map/ppermute | solution.py:18
  23.9 12.6 %collective-permute-start.1 = (bf16[32,512]{1,0:T(8,128)(2,1)S(1)}, bf16[32,512]{1,0:T(8,128)(2,1)S(1)}, u32[]{:S(2)}, u32[]{:S(2)}) collective-permute-start(bf16[32,512]{1,0:T(8,128)(2,1)S(1)} %gather_fusion.1), channel_id=1, source_target_pairs={{32,0},{64,32},{96,64},{128,96},{160,128},{192,160},{224,192},{33,... | collective-permute-start | bytes 98312 | tf_op jit(solution)/shard_map/ppermute | solution.py:18
  27.2 6.3 %collective-permute-start.2 = (bf16[32]{0:T(256)(128)(2,1)S(1)}, bf16[32]{0:T(256)(128)(2,1)S(1)}, u32[]{:S(2)}, u32[]{:S(2)}) collective-permute-start(bf16[32]{0:T(256)(128)(2,1)S(1)} %gather_fusion.2), channel_id=1, source_target_pairs={{0,32},{32,64},{64,96},{96,128},{128,160},{160,192},{192,224},{1,3... | collective-permute-start | bytes 200 | tf_op jit(solution)/shard_map/ppermute | solution.py:18
  31.6 4.9 %collective-permute-start.3 = (bf16[32]{0:T(256)(128)(2,1)S(1)}, bf16[32]{0:T(256)(128)(2,1)S(1)}, u32[]{:S(2)}, u32[]{:S(2)}) collective-permute-start(bf16[32]{0:T(256)(128)(2,1)S(1)} %gather_fusion.3), channel_id=1, source_target_pairs={{32,0},{64,32},{96,64},{128,96},{160,128},{192,160},{224,192},{33,... | collective-permute-start | bytes 200 | tf_op jit(solution)/shard_map/ppermute | solution.py:18
Sparse Core Ops, SparseCore 0:
  51.8 70.2 all-gather.3

commit v3 on v2

--- a/solution.py
+++ b/solution.py
@@ -152,22 +152,25 @@
         [anomaly, lower_a, upper_a, info_row[None],
          jnp.zeros((block_rows - pool_rows - 1, members), jnp.bfloat16)], axis=0)
     half = lax.all_gather(block, "tz", axis=0)
-    full = lax.all_gather(half, ("tx", "ty"), axis=0)
-    info = full[:, :, pool_rows, :2 * pool_rows].astype(jnp.float32)
-    inv_all = info[:, :, :pool_rows]
-    innov_all = info[:, :, pool_rows:]
+    first = lax.all_gather(lax.all_gather(half[0], "tx", axis=0), "ty", axis=0)
+    second = lax.all_gather(lax.all_gather(half[1], "ty", axis=0), "tx", axis=0)
     local_w = loc_local.reshape(boxes, nx, nz, ny, record_count)
     edge_w = loc_edge.reshape(boxes, nx, nz, ny, edge_rows)
-    weights = jnp.concatenate([local_w, edge_w], axis=4).transpose(0, 1, 3, 2, 4)
-    weights = weights.reshape(boxes, nx * ny, nz, pool_rows)
-    obs_scale = weights * inv_all[None]
-    weighted = (obs_scale * innov_all[None]).astype(jnp.bfloat16)
-    pad = ((0, 0), (0, 0), (0, 0), (0, block_rows - pool_rows))
-    scale_rows = jnp.pad(obs_scale, pad).reshape(boxes, -1)
-    scale_rows = jnp.pad(scale_rows, ((0, 8 - boxes), (0, 0)))
-    weighted = jnp.pad(weighted, pad).reshape(boxes, -1)
-    weighted = jnp.pad(weighted, ((0, 16 - boxes), (0, 0)))
-    gram, innov_sum = gram_terms(full.reshape(-1, members), scale_rows, weighted, boxes)
+    weights = jnp.concatenate([local_w, edge_w], axis=4)
+    parts = ((first, weights[:, :, 0].transpose(0, 2, 1, 3)), (second, weights[:, :, 1]))
+    gram = innov_sum = None
+    for pool, w in parts:
+        info = pool[:, :, pool_rows, :2 * pool_rows].astype(jnp.float32)
+        obs_scale = w * info[None, :, :, :pool_rows]
+        weighted = (obs_scale * info[None, :, :, pool_rows:]).astype(jnp.bfloat16)
+        pad = ((0, 0), (0, 0), (0, 0), (0, block_rows - pool_rows))
+        scale_rows = jnp.pad(obs_scale, pad).reshape(boxes, -1)
+        scale_rows = jnp.pad(scale_rows, ((0, 8 - boxes), (0, 0)))
+        weighted = jnp.pad(weighted, pad).reshape(boxes, -1)
+        weighted = jnp.pad(weighted, ((0, 16 - boxes), (0, 0)))
+        g, v = gram_terms(pool.reshape(-1, members), scale_rows, weighted, boxes)
+        gram = g if gram is None else gram + g
+        innov_sum = v if innov_sum is None else innov_sum + v
     transform = make_transform(gram, innov_sum)
     smean = jnp.mean(states, axis=2, dtype=jnp.float32)
     state_anomaly = (states.astype(jnp.float32) - smean[:, :, None]).astype(jnp.bfloat16)

time: 210 us -> 254 us (1.21)
  blocking collectives: 15 us -> 41.7 us
  waiting for transfers between devices: 72.9 us -> 80.4 us
  other arithmetic: 5.96 us -> 11.5 us
  Pallas kernels: 74.1 us -> 77 us
    all_gather x0 -> x2, blocking collectives: none -> 26.8 us  [the longest x1 13.9 us: body(): second = lax.all_gather(lax.all_gather(half[1], 'ty', axis=0), 'tx', axis=0)]
    all_gather x1 -> x2, waiting for transfers between devices: 69.9 us -> 77.4 us  [the longest x1 43.8 us: body(): first = lax.all_gather(lax.all_gather(half[0], 'tx', axis=0), 'ty', axis=0)]
    add x0 -> x2, other arithmetic: none -> 4.78 us  [the longest x1 3.4 us: body(): gram = g if gram is None else gram + g]
    pallas_call x1 -> x2, Pallas kernels: 16.5 us -> 19.5 us  [gram_terms(): pl.pallas_call(_gram_kernel, grid=(rows // step,), in_specs=[pl.BlockSpec...]
  transfers between devices with their start and end apart: 7 -> 8, of which waited for: 2 -> 3; matrix products, arithmetic and copies ran while one was open for 3% -> 3% of each run, Pallas kernels for 0% -> 0%
where the time goes in v3:
time: 254 us; the launch traced here: 253 us
  waiting for transfers between devices  80.4 us (32%)
  Pallas kernels  77 us (30%)
  blocking collectives  41.7 us (16%)
  starting transfers between devices  18 us (7%)
  between operations  13.7 us (5%)
  other arithmetic  11.5 us (5%)
  local copies, waits for them, and re-layouts  8.87 us (3%)
    pallas_call x1, Pallas kernels, make_transform(): pl.pallas_call(functools.partial(_transform_kernel, nb=nb), out_shape=jax...  57.5 us
    all_gather x1, waiting for transfers between devices, body(): first = lax.all_gather(lax.all_gather(half[0], 'tx', axis=0), 'ty', axis=0)  43.8 us
    all_gather x1, waiting for transfers between devices, body(): second = lax.all_gather(lax.all_gather(half[1], 'ty', axis=0), 'tx', axis=0)  33.6 us
    pallas_call x2, Pallas kernels, gram_terms(): pl.pallas_call(_gram_kernel, grid=(rows // step,), in_specs=[pl.BlockSpec...  19.5 us
    ppermute x6, starting transfers between devices, passed_along(): return lax.ppermute(block, axis, route)  18 us
    all_gather x1, blocking collectives, body(): half = lax.all_gather(block, 'tz', axis=0)  15 us
    all_gather x1, blocking collectives, body(): second = lax.all_gather(lax.all_gather(half[1], 'ty', axis=0), 'tx', axis=0)  13.9 us
    all_gather x1, blocking collectives, body(): first = lax.all_gather(lax.all_gather(half[0], 'tx', axis=0), 'ty', axis=0)  12.8 us
  transfers between devices with their start and end apart: 8, of which 3 were waited for; matrix products, arithmetic and copies ran while one was open for 3% of the time, Pallas kernels for 0%

profile of v3, /device:TPU:1, one launch (start us, length us, event | category | flops | bytes accessed | tf_op | source)
XLA Modules:
  0.0 253.4 jit_solution(15660467279043467858)
XLA Ops:
  7.9 1.0 convert_reduce_fusion.1
  10.2 4.9 %collective-permute-start.4 = (bf16[32]{0:T(256)(128)(2,1)S(1)}, bf16[32]{0:T(256)(128)(2,1)S(1)}, u32[]{:S(2)}, u32[]{:S(2)}) collective-permute-start(bf16[32]{0:T(256)(128)(2,1)S(1)} %gather_fusion.4), channel_id=1, source_target_pairs={{0,32},{32,64},{64,96},{96,128},{128,160},{160,192},{192,224},{1,3... | collective-permute-start | bytes 200 | tf_op jit(solution)/shard_map/ppermute | solution.py:18
  15.9 1.9 collective-permute-start.5
  17.8 1.0 fusion.6
  19.4 3.6 %collective-permute-start = (bf16[32,512]{1,0:T(8,128)(2,1)S(1)}, bf16[32,512]{1,0:T(8,128)(2,1)S(1)}, u32[]{:S(2)}, u32[]{:S(2)}) collective-permute-start(bf16[32,512]{1,0:T(8,128)(2,1)S(1)} %gather_fusion), channel_id=1, source_target_pairs={{0,32},{32,64},{64,96},{96,128},{128,160},{160,192},{192,224},{1,3... | collective-permute-start | bytes 98312 | tf_op jit(solution)/shard_map/ppermute | solution.py:18
  23.7 1.9 collective-permute-start.1
  26.3 0.7 gather_fusion.2
  27.0 3.6 %collective-permute-start.2 = (bf16[32]{0:T(256)(128)(2,1)S(1)}, bf16[32]{0:T(256)(128)(2,1)S(1)}, u32[]{:S(2)}, u32[]{:S(2)}) collective-permute-start(bf16[32]{0:T(256)(128)(2,1)S(1)} %gather_fusion.2), channel_id=1, source_target_pairs={{0,32},{32,64},{64,96},{96,128},{128,160},{160,192},{192,224},{1,3... | collective-permute-start | bytes 200 | tf_op jit(solution)/shard_map/ppermute | solution.py:18
  31.4 1.9 collective-permute-start.3
  33.3 2.9 %collective-permute-done.3 = bf16[32]{0:T(256)(128)(2,1)S(1)} collective-permute-done((bf16[32]{0:T(256)(128)(2,1)S(1)}, bf16[32]{0:T(256)(128)(2,1)S(1)}, u32[]{:S(2)}, u32[]{:S(2)}) %collective-permute-start.3) | collective-permute-done | bytes 96 | tf_op jit(solution)/shard_map/ppermute | solution.py:18
  36.5 15.0 %all-gather = bf16[416,512]{1,0:T(8,128)(2,1)S(1)} all-gather(bf16[208,512]{1,0:T(8,128)(2,1)S(1)} %concatenate.10), channel_id=2, replica_groups=mesh['region'=8,'tx'=4,'tz'=2,'ty'=4] {'tz'}, dimensions={0}, use_global_device_ids=true | all-gather | bytes 638976 | tf_op jit(solution)/shard_map/all_gather | solution.py:154
  51.6 13.9 %all-gather.4 = bf16[832,512]{1,0:T(8,128)(2,1)} all-gather(bf16[208,512]{1,0:T(8,128)(2,1)S(1)} %get-tuple-element.17), channel_id=6, replica_groups=mesh['region'=8,'tx'=4,'tz'=2,'ty'=4] {'ty'}, dimensions={0}, use_global_device_ids=true | all-gather | bytes 1064960 | tf_op jit(solution)/shard_map/all_gather | solution.py:156
  65.6 12.8 %all-gather.3 = bf16[832,512]{1,0:T(8,128)(2,1)} all-gather(bf16[208,512]{1,0:T(8,128)(2,1)S(1)} %get-tuple-element.18), channel_id=5, replica_groups=mesh['region'=8,'tx'=4,'tz'=2,'ty'=4] {'tx'}, dimensions={0}, use_global_device_ids=true | all-gather | bytes 1064960 | tf_op jit(solution)/shard_map/all_gather | solution.py:155
  78.8 33.6 %all-gather.10.cloned.1.call-done = bf16[16,208,512]{2,1,0:T(8,128)(2,1)} async-done(((bf16[4,208,512]{2,1,0:T(8,128)(2,1)}), bf16[16,208,512]{2,1,0:T(8,128)(2,1)}) %all-gather.10.cloned.1.call-update) | async-done | bytes 3407888 | tf_op jit(solution)/shard_map/all_gather | solution.py:156
  112.4 0.9 slice_convert_fusion
  115.0 43.8 %all-gather.8.cloned.1.call-done = bf16[16,208,512]{2,1,0:T(8,128)(2,1)} async-done(((bf16[4,208,512]{2,1,0:T(8,128)(2,1)}), bf16[16,208,512]{2,1,0:T(8,128)(2,1)}) %all-gather.8.cloned.1.call-update) | async-done | bytes 3407888 | tf_op jit(solution)/shard_map/all_gather | solution.py:155
  158.9 0.9 slice_convert_fusion.1
  161.5 9.7 %shard_map.92 = (f32[2,512,512]{2,1,0:T(8,128)}, f32[16,512]{1,0:T(8,128)}) custom-call(bf16[3328,512]{1,0:T(8,128)(2,1)} %bitcast.39, f32[8,3328]{1,0:T(8,128)} %pad.33.s_ref, bf16[16,3328]{1,0:T(8,128)(2,1)} %pad.35.w_ref), custom_call_target="tpu_custom_call" | custom-call | tf_op jit(solution)/shard_map/pallas_call | solution.py:49
  171.2 9.8 %shard_map.91 = (f32[2,512,512]{2,1,0:T(8,128)}, f32[16,512]{1,0:T(8,128)}) custom-call(bf16[3328,512]{1,0:T(8,128)(2,1)} %bitcast.41, f32[8,3328]{1,0:T(8,128)} %pad.29.s_ref, bf16[16,3328]{1,0:T(8,128)(2,1)} %pad.31.w_ref), custom_call_target="tpu_custom_call" | custom-call | tf_op jit(solution)/shard_map/pallas_call | solution.py:49
  181.0 1.4 add.47.v_ref
  182.4 3.4 %add.46.g_ref = f32[2,512,512]{2,1,0:T(8,128)} add(f32[2,512,512]{2,1,0:T(8,128)} %get-tuple-element.9, f32[2,512,512]{2,1,0:T(8,128)S(1)} %copy-done) | non-fusion elementwise | flops 524288 | bytes 6291456 | tf_op jit(solution)/shard_map/add | solution.py:172
  185.8 57.5 %shard_map.93 = bf16[2,512,512]{2,1,0:T(8,128)(2,1)} custom-call(f32[2,512,512]{2,1,0:T(8,128)} %add.46.g_ref, f32[16,512]{1,0:T(8,128)} %add.47.v_ref), custom_call_target="tpu_custom_call" | custom-call | tf_op jit(solution)/shard_map/pallas_call | solution.py:125
  243.3 2.2 multiply_reduce_fusion
  245.6 1.0 copy.31
  (67 shorter events, 10.2 us)
Async XLA Ops:
  6.5 105.9 %all-gather.10.cloned.1.call-start = ((), (), s32[]{:S(2)}) async-start(), calls=%async_computation.1 | async-start | bytes 4259840 | tf_op jit(solution)/shard_map/all_gather | solution.py:156
  10.2 21.1 %collective-permute-start.4 = (bf16[32]{0:T(256)(128)(2,1)S(1)}, bf16[32]{0:T(256)(128)(2,1)S(1)}, u32[]{:S(2)}, u32[]{:S(2)}) collective-permute-start(bf16[32]{0:T(256)(128)(2,1)S(1)} %gather_fusion.4), channel_id=1, source_target_pairs={{0,32},{32,64},{64,96},{96,128},{128,160},{160,192},{192,224},{1,3... | collective-permute-start | bytes 200 | tf_op jit(solution)/shard_map/ppermute | solution.py:18
  15.9 17.4 %collective-permute-start.5 = (bf16[32]{0:T(256)(128)(2,1)S(1)}, bf16[32]{0:T(256)(128)(2,1)S(1)}, u32[]{:S(2)}, u32[]{:S(2)}) collective-permute-start(bf16[32]{0:T(256)(128)(2,1)S(1)} %gather_fusion.5), channel_id=1, source_target_pairs={{32,0},{64,32},{96,64},{128,96},{160,128},{192,160},{224,192},{33,... | collective-permute-start | bytes 200 | tf_op jit(solution)/shard_map/ppermute | solution.py:18
  19.4 16.9 %collective-permute-start = (bf16[32,512]{1,0:T(8,128)(2,1)S(1)}, bf16[32,512]{1,0:T(8,128)(2,1)S(1)}, u32[]{:S(2)}, u32[]{:S(2)}) collective-permute-start(bf16[32,512]{1,0:T(8,128)(2,1)S(1)} %gather_fusion), channel_id=1, source_target_pairs={{0,32},{32,64},{64,96},{96,128},{128,160},{160,192},{192,224},{1,3... | collective-permute-start | bytes 98312 | tf_op jit(solution)/shard_map/ppermute | solution.py:18
  23.7 12.6 %collective-permute-start.1 = (bf16[32,512]{1,0:T(8,128)(2,1)S(1)}, bf16[32,512]{1,0:T(8,128)(2,1)S(1)}, u32[]{:S(2)}, u32[]{:S(2)}) collective-permute-start(bf16[32,512]{1,0:T(8,128)(2,1)S(1)} %gather_fusion.1), channel_id=1, source_target_pairs={{32,0},{64,32},{96,64},{128,96},{160,128},{192,160},{224,192},{33,... | collective-permute-start | bytes 98312 | tf_op jit(solution)/shard_map/ppermute | solution.py:18
  27.0 6.3 %collective-permute-start.2 = (bf16[32]{0:T(256)(128)(2,1)S(1)}, bf16[32]{0:T(256)(128)(2,1)S(1)}, u32[]{:S(2)}, u32[]{:S(2)}) collective-permute-start(bf16[32]{0:T(256)(128)(2,1)S(1)} %gather_fusion.2), channel_id=1, source_target_pairs={{0,32},{32,64},{64,96},{96,128},{128,160},{160,192},{192,224},{1,3... | collective-permute-start | bytes 200 | tf_op jit(solution)/shard_map/ppermute | solution.py:18
  31.4 4.9 %collective-permute-start.3 = (bf16[32]{0:T(256)(128)(2,1)S(1)}, bf16[32]{0:T(256)(128)(2,1)S(1)}, u32[]{:S(2)}, u32[]{:S(2)}) collective-permute-start(bf16[32]{0:T(256)(128)(2,1)S(1)} %gather_fusion.3), channel_id=1, source_target_pairs={{32,0},{64,32},{96,64},{128,96},{160,128},{192,160},{224,192},{33,... | collective-permute-start | bytes 200 | tf_op jit(solution)/shard_map/ppermute | solution.py:18
  51.5 26.9 %copy-start.3 = (f32[2,4096]{1,0:T(2,128)S(1)}, f32[2,4096]{1,0:T(2,128)}, u32[]{:S(2)}) copy-start(f32[2,4096]{1,0:T(2,128)} %param.14) | copy-start | bytes 98308
  51.5 27.0 %copy-start.4 = (f32[2,2048]{1,0:T(2,128)S(1)}, f32[2,2048]{1,0:T(2,128)}, u32[]{:S(2)}) copy-start(f32[2,2048]{1,0:T(2,128)} %param.15) | copy-start | bytes 49156
  51.5 27.1 %copy-start.1 = (bf16[2,256,512]{2,1,0:T(8,128)(2,1)S(1)}, bf16[2,256,512]{2,1,0:T(8,128)(2,1)}, u32[]{:S(2)}) copy-start(bf16[2,256,512]{2,1,0:T(8,128)(2,1)} %param.16) | copy-start | bytes 1572868
  51.6 27.2 %copy-start.5 = (s32[256]{0:T(256)S(1)}, s32[256]{0:T(256)}, u32[]{:S(2)}) copy-start(s32[256]{0:T(256)} %param.17) | copy-start | bytes 3076
  65.5 93.3 %all-gather.8.cloned.1.call-start = ((), (), s32[]{:S(2)}) async-start(), calls=%async_computation | async-start | bytes 4259840 | tf_op jit(solution)/shard_map/all_gather | solution.py:155
  171.2 9.8 %copy-start.2 = (f32[16,512]{1,0:T(8,128)S(1)}, f32[16,512]{1,0:T(8,128)}, u32[]{:S(2)}) copy-start(f32[16,512]{1,0:T(8,128)} %get-tuple-element.12) | copy-start | bytes 98308
  171.2 11.2 %copy-start = (f32[2,512,512]{2,1,0:T(8,128)S(1)}, f32[2,512,512]{2,1,0:T(8,128)}, u32[]{:S(2)}) copy-start(f32[2,512,512]{2,1,0:T(8,128)} %get-tuple-element.10) | copy-start | bytes 6291460
Sparse Core Ops, SparseCore 0:
  65.7 46.7 all-gather.9
  114.3 44.5 all-gather.7

commit v4 on v2

--- a/solution.py
+++ b/solution.py
@@ -138,10 +138,16 @@
     anomaly = (ens_obs.astype(jnp.float32) - ymean[:, None]).astype(jnp.bfloat16)
     inv_var = (1.0 / obs_var).astype(jnp.bfloat16)
     innov = (obs_values - ymean).astype(jnp.bfloat16)
-    lower_a, lower_v, lower_i = passed_along(
-        (anomaly[edge_up], inv_var[edge_up], innov[edge_up]), "region", 1)
-    upper_a, upper_v, upper_i = passed_along(
-        (anomaly[edge_down], inv_var[edge_down], innov[edge_down]), "region", -1)
+    def edge_payload(index):
+        info = jnp.concatenate([inv_var[index], innov[index]])
+        info = jnp.pad(info, (0, members - info.shape[0]))
+        return jnp.concatenate([anomaly[index], info[None]], axis=0)
+
+    lower = passed_along(edge_payload(edge_up), "region", 1)
+    upper = passed_along(edge_payload(edge_down), "region", -1)
+    edge = edge_up.shape[0]
+    lower_a, lower_v, lower_i = lower[:edge], lower[edge, :edge], lower[edge, edge:2 * edge]
+    upper_a, upper_v, upper_i = upper[:edge], upper[edge, :edge], upper[edge, edge:2 * edge]
     edge_rows = lower_a.shape[0] + upper_a.shape[0]
     pool_rows = record_count + edge_rows
     block_rows = ((pool_rows + 1 + 15) // 16) * 16

time: 210 us -> 198 us (0.943)
  starting transfers between devices: 18.1 us -> 7.07 us
    ppermute x6 -> x2, starting transfers between devices: 18.1 us -> 7.07 us  [passed_along(): return lax.ppermute(block, axis, route)]
    all_gather x1, waiting for transfers between devices: 69.9 us -> 73.3 us  [body(): full = lax.all_gather(half, ('tx', 'ty'), axis=0)]
  transfers between devices with their start and end apart: 7 -> 3, of which waited for: 2 -> 2; matrix products, arithmetic and copies ran while one was open for 3% -> 2% of each run, Pallas kernels for 0% -> 0%
where the time goes in v4:
time: 198 us
  waiting for transfers between devices  74.4 us (38%)
  Pallas kernels  74.1 us (37%)
  between operations  13.6 us (7%)
  blocking collectives  13.2 us (7%)
  local copies, waits for them, and re-layouts  7.6 us (4%)
  starting transfers between devices  7.07 us (4%)
  other arithmetic  5.53 us (3%)
  matrix products  2.17 us (1%)
    all_gather x1, waiting for transfers between devices, body(): full = lax.all_gather(half, ('tx', 'ty'), axis=0)  73.3 us
    pallas_call x1, Pallas kernels, make_transform(): pl.pallas_call(functools.partial(_transform_kernel, nb=nb), out_shape=jax...  57.5 us
    pallas_call x1, Pallas kernels, gram_terms(): pl.pallas_call(_gram_kernel, grid=(rows // step,), in_specs=[pl.BlockSpec...  16.5 us
    all_gather x1, blocking collectives, body(): half = lax.all_gather(block, 'tz', axis=0)  13.2 us
    ppermute x2, starting transfers between devices, passed_along(): return lax.ppermute(block, axis, route)  7.07 us
  transfers between devices with their start and end apart: 3, of which 2 were waited for; matrix products, arithmetic and copies ran while one was open for 2% of the time, Pallas kernels for 0%

profile of v4, /device:TPU:1, one launch (start us, length us, event | category | flops | bytes accessed | tf_op | source)
XLA Modules:
  0.0 197.6 jit_solution(8930449463468797358)
XLA Ops:
  6.5 1.0 convert_reduce_fusion.1
  7.5 0.7 compare_select_fusion
  8.2 0.7 subtract_convert_fusion
  8.9 0.7 gather_fusion.4
  9.6 0.7 gather_fusion.5
  10.4 1.0 fusion.6
  11.5 0.6 gather_fusion.3
  12.1 5.1 %collective-permute-start.1 = (bf16[33,512]{1,0:T(8,128)(2,1)S(1)}, bf16[33,512]{1,0:T(8,128)(2,1)S(1)}, u32[]{:S(2)}, u32[]{:S(2)}) collective-permute-start(bf16[33,512]{1,0:T(8,128)(2,1)S(1)} %pad_maximum_fusion.1), channel_id=1, source_target_pairs={{32,0},{64,32},{96,64},{128,96},{160,128},{192,160},{224,192},{33,... | collective-permute-start | bytes 101384 | tf_op jit(solution)/shard_map/ppermute | solution.py:18
  17.3 0.7 compare_select_fusion.1
  17.9 0.7 gather_fusion.1
  18.6 0.7 gather_fusion.2
  19.4 0.6 gather_fusion
  20.1 1.9 collective-permute-start
  22.1 1.1 collective-permute-done
  23.4 0.2 concatenate.26
  23.6 13.2 %all-gather = bf16[416,512]{1,0:T(8,128)(2,1)} all-gather(bf16[208,512]{1,0:T(8,128)(2,1)S(1)} %concatenate.26), channel_id=2, replica_groups=mesh['region'=8,'tx'=4,'tz'=2,'ty'=4] {'tz'}, dimensions={0}, use_global_device_ids=true | all-gather | bytes 638976 | tf_op jit(solution)/shard_map/all_gather | solution.py:160
  37.2 73.3 %all-gather.4.cloned.1.call-done = bf16[32,208,512]{2,1,0:T(8,128)(2,1)} async-done(((bf16[2,208,512]{2,1,0:T(8,128)(2,1)}), bf16[32,208,512]{2,1,0:T(8,128)(2,1)}) %all-gather.4.cloned.1.call-update) | async-done | bytes 6815760 | tf_op jit(solution)/shard_map/all_gather | solution.py:161
  110.5 1.0 slice_convert_fusion
  111.8 0.7 pad.26.s_ref
  112.7 0.7 pad.28.w_ref
  113.4 16.5 %shard_map.91 = (f32[2,512,512]{2,1,0:T(8,128)}, f32[16,512]{1,0:T(8,128)}) custom-call(bf16[6656,512]{1,0:T(8,128)(2,1)} %bitcast.28, f32[8,6656]{1,0:T(8,128)} %pad.26.s_ref, bf16[16,6656]{1,0:T(8,128)(2,1)} %pad.28.w_ref), custom_call_target="tpu_custom_call" | custom-call | tf_op jit(solution)/shard_map/pallas_call | solution.py:49
  129.9 57.5 %shard_map.92 = bf16[2,512,512]{2,1,0:T(8,128)(2,1)} custom-call(f32[2,512,512]{2,1,0:T(8,128)} %get-tuple-element.7.g_ref, f32[16,512]{1,0:T(8,128)} %get-tuple-element.8.v_ref), custom_call_target="tpu_custom_call" | custom-call | tf_op jit(solution)/shard_map/pallas_call | solution.py:125
  187.5 2.2 %multiply_reduce_fusion = f32[512,2,256]{2,0,1:T(8,128)S(1)} fusion(bf16[2,512,512]{2,1,0:T(8,128)(2,1)} %shard_map.92, f32[2,256]{1,0:T(2,128)S(1)} %compare_convert_fusion, bf16[2,256,512]{2,1,0:T(8,128)(2,1)S(1)} %copy-done, f32[2,256]{1,0:T(2,128)S(1)} %broadcast_multiply_fusion.1), kind=kOutput, calls=%fused_computation.6 | convolution fusion | flops 538443776 | bytes 2625536 | tf_op jit(solution)/shard_map/fck,bkj->bfcj/dot_general | solution.py:180
  189.8 1.0 copy.18
  (42 shorter events, 1.5 us)
Async XLA Ops:
  6.5 103.9 %all-gather.4.cloned.1.call-start = ((), (), s32[]{:S(2)}) async-start(), calls=%async_computation | async-start | bytes 7241728 | tf_op jit(solution)/shard_map/all_gather | solution.py:161
  9.6 27.2 %copy-start.1 = (f32[2,4096]{1,0:T(2,128)S(1)}, f32[2,4096]{1,0:T(2,128)}, u32[]{:S(2)}) copy-start(f32[2,4096]{1,0:T(2,128)} %param.14) | copy-start | bytes 98308
  9.6 27.2 %copy-start.2 = (f32[2,2048]{1,0:T(2,128)S(1)}, f32[2,2048]{1,0:T(2,128)}, u32[]{:S(2)}) copy-start(f32[2,2048]{1,0:T(2,128)} %param.15) | copy-start | bytes 49156
  10.3 26.7 %copy-start = (bf16[2,256,512]{2,1,0:T(8,128)(2,1)S(1)}, bf16[2,256,512]{2,1,0:T(8,128)(2,1)}, u32[]{:S(2)}) copy-start(bf16[2,256,512]{2,1,0:T(8,128)(2,1)} %param.16) | copy-start | bytes 1572868
  12.1 25.1 %copy-start.3 = (s32[256]{0:T(256)S(1)}, s32[256]{0:T(256)}, u32[]{:S(2)}) copy-start(s32[256]{0:T(256)} %param.17) | copy-start | bytes 3076
  12.1 9.9 %collective-permute-start.1 = (bf16[33,512]{1,0:T(8,128)(2,1)S(1)}, bf16[33,512]{1,0:T(8,128)(2,1)S(1)}, u32[]{:S(2)}, u32[]{:S(2)}) collective-permute-start(bf16[33,512]{1,0:T(8,128)(2,1)S(1)} %pad_maximum_fusion.1), channel_id=1, source_target_pairs={{32,0},{64,32},{96,64},{128,96},{160,128},{192,160},{224,192},{33,... | collective-permute-start | bytes 101384 | tf_op jit(solution)/shard_map/ppermute | solution.py:18
  20.1 3.1 %collective-permute-start = (bf16[33,512]{1,0:T(8,128)(2,1)S(1)}, bf16[33,512]{1,0:T(8,128)(2,1)S(1)}, u32[]{:S(2)}, u32[]{:S(2)}) collective-permute-start(bf16[33,512]{1,0:T(8,128)(2,1)S(1)} %pad_maximum_fusion), channel_id=1, source_target_pairs={{0,32},{32,64},{64,96},{96,128},{128,160},{160,192},{192,224},{1,3... | collective-permute-start | bytes 101384 | tf_op jit(solution)/shard_map/ppermute | solution.py:18
Sparse Core Ops, SparseCore 0:
  36.9 73.5 all-gather.3

commit v5 on v4

--- a/solution.py
+++ b/solution.py
@@ -16,6 +16,18 @@
     devices = range(lax.axis_size(axis))
     route = [(i - distance, i) for i in devices if i - distance in devices]
     return lax.ppermute(block, axis, route)
+
+
+def ring_gather(block, axis):
+    size = lax.axis_size(axis)
+    ahead = [(i, (i + 1) % size) for i in range(size)]
+    behind = [(i, (i - 1) % size) for i in range(size)]
+    from_prev = lax.ppermute(block, axis, ahead)
+    from_next = lax.ppermute(block, axis, behind)
+    cut = block.shape[0] // 2
+    far = jnp.concatenate([lax.ppermute(from_prev[:cut], axis, ahead),
+                           lax.ppermute(from_next[cut:], axis, behind)], axis=0)
+    return jnp.stack([block, from_prev, far, from_next], axis=0)
 
 
 def _gram_kernel(a_ref, s_ref, w_ref, g_ref, v_ref):
@@ -158,14 +170,22 @@
         [anomaly, lower_a, upper_a, info_row[None],
          jnp.zeros((block_rows - pool_rows - 1, members), jnp.bfloat16)], axis=0)
     half = lax.all_gather(block, "tz", axis=0)
-    full = lax.all_gather(half, ("tx", "ty"), axis=0)
+    first = ring_gather(ring_gather(half[0], "tx"), "ty")
+    second = ring_gather(ring_gather(half[1], "ty"), "tx")
+    full = jnp.stack([first, second.transpose(1, 0, 2, 3)], axis=2)
+    full = full.reshape(ny * nx, nz, block_rows, members)
     info = full[:, :, pool_rows, :2 * pool_rows].astype(jnp.float32)
     inv_all = info[:, :, :pool_rows]
     innov_all = info[:, :, pool_rows:]
     local_w = loc_local.reshape(boxes, nx, nz, ny, record_count)
     edge_w = loc_edge.reshape(boxes, nx, nz, ny, edge_rows)
-    weights = jnp.concatenate([local_w, edge_w], axis=4).transpose(0, 1, 3, 2, 4)
-    weights = weights.reshape(boxes, nx * ny, nz, pool_rows)
+    weights = jnp.concatenate([local_w, edge_w], axis=4)
+    x_at, y_at = lax.axis_index("tx"), lax.axis_index("ty")
+    x_src = (x_at - jnp.arange(nx)) % nx
+    y_src = (y_at - jnp.arange(ny)) % ny
+    weights = jnp.take(weights, x_src, axis=1)
+    weights = jnp.take(weights, y_src, axis=3)
+    weights = weights.transpose(0, 3, 1, 2, 4).reshape(boxes, ny * nx, nz, pool_rows)
     obs_scale = weights * inv_all[None]
     weighted = (obs_scale * innov_all[None]).astype(jnp.bfloat16)
     pad = ((0, 0), (0, 0), (0, 0), (0, block_rows - pool_rows))

time: 198 us -> 197 us (level)
  waiting for transfers between devices: 74.4 us -> 41.4 us
  starting transfers between devices: 7.07 us -> 32.4 us
  between operations: 13.6 us -> 0.47 us
  other arithmetic: 5.53 us -> 16.1 us
  local copies, waits for them, and re-layouts: 7.6 us -> 14.6 us
    all_gather x1 -> x0, waiting for transfers between devices: 73.3 us -> none  [body(): full = lax.all_gather(half, ('tx', 'ty'), axis=0)]
    ppermute x0 -> x16, waiting for transfers between devices: none -> 41.4 us  [the longest x4 23.3 us: ring_gather(): lax.ppermute(from_prev[:cut], axis, ahead)]
    ppermute x0 -> x16, starting transfers between devices: none -> 25.4 us  [the longest x4 11.1 us: ring_gather(): lax.ppermute(from_next[cut:], axis, behind)]
    another operation x0 -> x9, other arithmetic: none -> 9.65 us  [the longest x8 7.06 us: ring_gather(): return jnp.stack([block, from_prev, far, from_next], axis=0)]
    another operation x0 -> x1, local copies, waits for them, and re-layouts: none -> 3.26 us  [body(): full = jnp.stack([first, second.transpose(1, 0, 2, 3)], axis=2)]
  transfers between devices with their start and end apart: 3 -> 18, of which waited for: 2 -> 5; matrix products, arithmetic and copies ran while one was open for 2% -> 6% of each run, Pallas kernels for 0% -> 0%
where the time goes in v5:
time: 197 us; the launch traced here: 195 us
  Pallas kernels  74.2 us (38%)
  waiting for transfers between devices  41.4 us (21%)
  starting transfers between devices  32.4 us (16%)
  other arithmetic  16.1 us (8%)
  local copies, waits for them, and re-layouts  14.6 us (7%)
  blocking collectives  13.5 us (7%)
  matrix products  2.17 us (1%)
    pallas_call x1, Pallas kernels, make_transform(): pl.pallas_call(functools.partial(_transform_kernel, nb=nb), out_shape=jax...  57.6 us
    ppermute x4, waiting for transfers between devices, ring_gather(): lax.ppermute(from_prev[:cut], axis, ahead)  23.3 us
    ppermute x4, waiting for transfers between devices, ring_gather(): from_prev = lax.ppermute(block, axis, ahead)  18.1 us
    pallas_call x1, Pallas kernels, gram_terms(): pl.pallas_call(_gram_kernel, grid=(rows // step,), in_specs=[pl.BlockSpec...  16.6 us
    all_gather x1, blocking collectives, body(): half = lax.all_gather(block, 'tz', axis=0)  13.5 us
    ppermute x4, starting transfers between devices, ring_gather(): lax.ppermute(from_next[cut:], axis, behind)  11.1 us
    ppermute x4, starting transfers between devices, ring_gather(): from_next = lax.ppermute(block, axis, behind)  8.78 us
    ppermute x2, starting transfers between devices, passed_along(): return lax.ppermute(block, axis, route)  7.07 us
  transfers between devices with their start and end apart: 18, of which 5 were waited for; matrix products, arithmetic and copies ran while one was open for 6% of the time, Pallas kernels for 0%

profile of v5, /device:TPU:1, one launch (start us, length us, event | category | flops | bytes accessed | tf_op | source)
XLA Modules:
  0.0 194.8 jit_solution(7225252962785165904)
XLA Ops:
  5.5 5.1 %collective-permute-start.1 = (bf16[33,512]{1,0:T(8,128)(2,1)S(1)}, bf16[33,512]{1,0:T(8,128)(2,1)S(1)}, u32[]{:S(2)}, u32[]{:S(2)}) collective-permute-start(bf16[33,512]{1,0:T(8,128)(2,1)S(1)} %pad_maximum_fusion.8), channel_id=1, source_target_pairs={{32,0},{64,32},{96,64},{128,96},{160,128},{192,160},{224,192},{33,... | collective-permute-start | bytes 101384 | tf_op jit(solution)/shard_map/ppermute | solution.py:18
  13.5 1.9 collective-permute-start
  17.5 13.5 %all-gather = bf16[416,512]{1,0:T(8,128)(2,1)S(1)} all-gather(bf16[208,512]{1,0:T(8,128)(2,1)S(1)} %concatenate.39), channel_id=2, replica_groups=mesh['region'=8,'tx'=4,'tz'=2,'ty'=4] {'tz'}, dimensions={0}, use_global_device_ids=true | all-gather | bytes 638976 | tf_op jit(solution)/shard_map/all_gather | solution.py:172
  31.1 4.2 %collective-permute-start.2 = (bf16[208,512]{1,0:T(8,128)(2,1)S(1)}, bf16[208,512]{1,0:T(8,128)(2,1)S(1)}, u32[]{:S(2)}, u32[]{:S(2)}) collective-permute-start(bf16[208,512]{1,0:T(8,128)(2,1)S(1)} %get-tuple-element.21), channel_id=1, source_target_pairs={{0,8},{8,16},{16,24},{24,0},{1,9},{9,17},{17,25},{25,1},{2,10},{10... | collective-permute-start | bytes 638984 | tf_op jit(solution)/shard_map/ppermute | solution.py:25
  37.3 3.2 %collective-permute-done.2 = bf16[208,512]{1,0:T(8,128)(2,1)S(1)} collective-permute-done((bf16[208,512]{1,0:T(8,128)(2,1)S(1)}, bf16[208,512]{1,0:T(8,128)(2,1)S(1)}, u32[]{:S(2)}, u32[]{:S(2)}) %collective-permute-start.2) | collective-permute-done | bytes 213024 | tf_op jit(solution)/shard_map/ppermute | solution.py:25
  40.6 2.9 %collective-permute-start.5 = (bf16[104,512]{1,0:T(8,128)(2,1)S(1)}, bf16[104,512]{1,0:T(8,128)(2,1)S(1)}, u32[]{:S(2)}, u32[]{:S(2)}) collective-permute-start(bf16[104,512]{1,0:T(8,128)(2,1)S(1)} %slice.102), channel_id=1, source_target_pairs={{0,24},{8,0},{16,8},{24,16},{1,25},{9,1},{17,9},{25,17},{2,26},{10... | collective-permute-start | bytes 319496 | tf_op jit(solution)/shard_map/ppermute | solution.py:29
  44.4 2.0 %collective-permute-start.12 = (bf16[208,512]{1,0:T(8,128)(2,1)S(1)}, bf16[208,512]{1,0:T(8,128)(2,1)S(1)}, u32[]{:S(2)}, u32[]{:S(2)}) collective-permute-start(bf16[208,512]{1,0:T(8,128)(2,1)S(1)} %get-tuple-element.22), channel_id=1, source_target_pairs={{0,3},{1,0},{2,1},{3,2},{4,7},{5,4},{6,5},{7,6},{8,11},{9,8},{10,9... | collective-permute-start | bytes 638984 | tf_op jit(solution)/shard_map/ppermute | solution.py:26
  46.4 1.4 fusion.21
  47.8 2.7 %collective-permute-start.8 = (bf16[4,208,512]{2,1,0:T(8,128)(2,1)}, bf16[4,208,512]{2,1,0:T(8,128)(2,1)S(1)}, u32[]{:S(2)}, u32[]{:S(2)}) collective-permute-start(bf16[4,208,512]{2,1,0:T(8,128)(2,1)} %get-tuple-element.16), channel_id=1, source_target_pairs={{0,3},{1,0},{2,1},{3,2},{4,7},{5,4},{6,5},{7,6},{8,11},{9,8},{10,9... | collective-permute-start | bytes 2555912 | tf_op jit(solution)/shard_map/ppermute | solution.py:26
  50.5 1.5 collective-permute-done.10
  52.1 2.7 %collective-permute-start.13 = (bf16[104,512]{1,0:T(8,128)(2,1)S(1)}, bf16[104,512]{1,0:T(8,128)(2,1)S(1)}, u32[]{:S(2)}, u32[]{:S(2)}) collective-permute-start(bf16[104,512]{1,0:T(8,128)(2,1)S(1)} %slice.107), channel_id=1, source_target_pairs={{0,3},{1,0},{2,1},{3,2},{4,7},{5,4},{6,5},{7,6},{8,11},{9,8},{10,9... | collective-permute-start | bytes 319496 | tf_op jit(solution)/shard_map/ppermute | solution.py:29
  54.8 17.4 %collective-permute-done.11 = bf16[104,512]{1,0:T(8,128)(2,1)S(1)} collective-permute-done((bf16[104,512]{1,0:T(8,128)(2,1)S(1)}, bf16[104,512]{1,0:T(8,128)(2,1)S(1)}, u32[]{:S(2)}, u32[]{:S(2)}) %collective-permute-start.11) | collective-permute-done | bytes 106528 | tf_op jit(solution)/shard_map/ppermute | solution.py:28
  73.6 2.7 %collective-permute-start.16 = (bf16[4,208,512]{2,1,0:T(8,128)(2,1)}, bf16[4,208,512]{2,1,0:T(8,128)(2,1)S(1)}, u32[]{:S(2)}, u32[]{:S(2)}) collective-permute-start(bf16[4,208,512]{2,1,0:T(8,128)(2,1)} %get-tuple-element.18), channel_id=1, source_target_pairs={{0,24},{8,0},{16,8},{24,16},{1,25},{9,1},{17,9},{25,17},{2,26},{10... | collective-permute-start | bytes 2555912 | tf_op jit(solution)/shard_map/ppermute | solution.py:26
  78.7 2.7 %collective-permute-start.9 = (bf16[2,208,512]{2,1,0:T(8,128)(2,1)S(1)}, bf16[2,208,512]{2,1,0:T(8,128)(2,1)S(1)}, u32[]{:S(2)}, u32[]{:S(2)}) collective-permute-start(bf16[2,208,512]{2,1,0:T(8,128)(2,1)S(1)} %slice.104), channel_id=1, source_target_pairs={{0,3},{1,0},{2,1},{3,2},{4,7},{5,4},{6,5},{7,6},{8,11},{9,8},{10,9... | collective-permute-start | bytes 1277960 | tf_op jit(solution)/shard_map/ppermute | solution.py:29
  81.5 13.4 %collective-permute-done.14 = bf16[4,208,512]{2,1,0:T(8,128)(2,1)S(1)} collective-permute-done((bf16[4,208,512]{2,1,0:T(8,128)(2,1)}, bf16[4,208,512]{2,1,0:T(8,128)(2,1)S(1)}, u32[]{:S(2)}, u32[]{:S(2)}) %collective-permute-start.14) | collective-permute-done | bytes 852000 | tf_op jit(solution)/shard_map/ppermute | solution.py:25
  95.1 2.7 %collective-permute-start.17 = (bf16[2,208,512]{2,1,0:T(8,128)(2,1)S(1)}, bf16[2,208,512]{2,1,0:T(8,128)(2,1)S(1)}, u32[]{:S(2)}, u32[]{:S(2)}) collective-permute-start(bf16[2,208,512]{2,1,0:T(8,128)(2,1)S(1)} %slice.109), channel_id=1, source_target_pairs={{0,24},{8,0},{16,8},{24,16},{1,25},{9,1},{17,9},{25,17},{2,26},{10... | collective-permute-start | bytes 1277960 | tf_op jit(solution)/shard_map/ppermute | solution.py:29
  98.0 2.1 %pad_maximum_fusion.1 = (bf16[4,4,208,512]{3,2,1,0:T(8,128)(2,1)S(1)}, bf16[4,4,1,208,512]{4,3,1,0,2:T(8,128)(2,1)S(1)}) fusion(bf16[1,4,208,512]{3,2,1,0:T(8,128)(2,1)} %bitcast.74, bf16[1,4,208,512]{3,2,1,0:T(8,128)(2,1)S(1)} %maximum_bitcast_fusion, bf16[1,4,208,512]{3,2,1,0:T(8,128)(2,1)} %bitcast.73, bf16[1,4,208,512]{3,2,1,0:T(8,128)(2,1)} %get-tuple-element.15), kind=kLoop, calls=%fused_computation.9 | loop fusion | flops 5111808 | bytes 10223616 | tf_op jit(solution)/shard_map/stack | solution.py:30
  100.1 5.9 %collective-permute-done.15 = bf16[2,208,512]{2,1,0:T(8,128)(2,1)S(1)} collective-permute-done((bf16[2,208,512]{2,1,0:T(8,128)(2,1)S(1)}, bf16[2,208,512]{2,1,0:T(8,128)(2,1)S(1)}, u32[]{:S(2)}, u32[]{:S(2)}) %collective-permute-start.15) | collective-permute-done | bytes 426016 | tf_op jit(solution)/shard_map/ppermute | solution.py:28
  106.1 2.0 %pad_maximum_fusion.2 = (bf16[4,4,208,512]{3,2,0,1:T(8,128)(2,1)S(1)}, bf16[4,4,1,208,512]{4,3,1,0,2:T(8,128)(2,1)}) fusion(bf16[1,4,208,512]{3,2,0,1:T(8,128)(2,1)S(1)} %bitcast.76, bf16[1,4,208,512]{3,2,0,1:T(8,128)(2,1)S(1)} %maximum_bitcast_fusion.1, bf16[1,4,208,512]{3,2,0,1:T(8,128)(2,1)S(1)} %bitcast.75, bf16[1,4,208,512]{3,2,0,1:T(8,128)(2,1)S(1)} %copy-done), kind=kLoop, calls=%fused_computation.10 | loop fusion | flops 5111808 | bytes 10223616 | tf_op jit(solution)/shard_map/stack | solution.py:30
  111.4 2.6 %pad_maximum_fusion = bf16[4,4,2,208,512]{4,3,1,0,2:T(8,128)(2,1)S(1)} fusion(bf16[4,4,1,208,512]{4,3,1,0,2:T(8,128)(2,1)} %get-tuple-element.14, bf16[4,4,1,208,512]{4,3,1,0,2:T(8,128)(2,1)S(1)} %get-tuple-element.12), kind=kLoop, calls=%fused_computation.8 | loop fusion | flops 3407872 | bytes 13631488 | tf_op jit(solution)/shard_map/stack | solution.py:175
  114.0 3.3 %copy.37 = bf16[4,4,2,208,512]{4,3,2,1,0:T(8,128)(2,1)} copy(bf16[4,4,2,208,512]{4,3,1,0,2:T(8,128)(2,1)S(1)} %pad_maximum_fusion) | data formatting | bytes 13631488 | tf_op jit(solution)/shard_map/stack | solution.py:175
  117.3 16.6 %shard_map.91 = (f32[2,512,512]{2,1,0:T(8,128)}, f32[16,512]{1,0:T(8,128)}) custom-call(bf16[6656,512]{1,0:T(8,128)(2,1)} %bitcast.70, f32[8,6656]{1,0:T(8,128)} %pad.26.s_ref, bf16[16,6656]{1,0:T(8,128)(2,1)} %pad.28.w_ref), custom_call_target="tpu_custom_call" | custom-call | tf_op jit(solution)/shard_map/pallas_call | solution.py:61
  133.9 57.6 %shard_map.92 = bf16[2,512,512]{2,1,0:T(8,128)(2,1)} custom-call(f32[2,512,512]{2,1,0:T(8,128)} %get-tuple-element.7.g_ref, f32[16,512]{1,0:T(8,128)} %get-tuple-element.8.v_ref), custom_call_target="tpu_custom_call" | custom-call | tf_op jit(solution)/shard_map/pallas_call | solution.py:137
  191.5 2.2 %multiply_reduce_fusion = f32[512,2,256]{2,0,1:T(8,128)S(1)} fusion(bf16[2,512,512]{2,1,0:T(8,128)(2,1)} %shard_map.92, f32[2,256]{1,0:T(2,128)S(1)} %compare_convert_fusion, bf16[2,256,512]{2,1,0:T(8,128)(2,1)S(1)} %copy-done.7, f32[2,256]{1,0:T(2,128)S(1)} %broadcast_multiply_fusion.1), kind=kOutput, calls=%fused_computation.11 | convolution fusion | flops 538443776 | bytes 2625536 | tf_op jit(solution)/shard_map/fck,bkj->bfcj/dot_general | solution.py:200
  (113 shorter events, 21.9 us)
Async XLA Ops:
  5.5 11.6 %collective-permute-start.1 = (bf16[33,512]{1,0:T(8,128)(2,1)S(1)}, bf16[33,512]{1,0:T(8,128)(2,1)S(1)}, u32[]{:S(2)}, u32[]{:S(2)}) collective-permute-start(bf16[33,512]{1,0:T(8,128)(2,1)S(1)} %pad_maximum_fusion.8), channel_id=1, source_target_pairs={{32,0},{64,32},{96,64},{128,96},{160,128},{192,160},{224,192},{33,... | collective-permute-start | bytes 101384 | tf_op jit(solution)/shard_map/ppermute | solution.py:18
  13.5 3.7 %collective-permute-start = (bf16[33,512]{1,0:T(8,128)(2,1)S(1)}, bf16[33,512]{1,0:T(8,128)(2,1)S(1)}, u32[]{:S(2)}, u32[]{:S(2)}) collective-permute-start(bf16[33,512]{1,0:T(8,128)(2,1)S(1)} %pad_maximum_fusion.7), channel_id=1, source_target_pairs={{0,32},{32,64},{64,96},{96,128},{128,160},{160,192},{192,224},{1,3... | collective-permute-start | bytes 101384 | tf_op jit(solution)/shard_map/ppermute | solution.py:18
  31.1 9.4 %collective-permute-start.2 = (bf16[208,512]{1,0:T(8,128)(2,1)S(1)}, bf16[208,512]{1,0:T(8,128)(2,1)S(1)}, u32[]{:S(2)}, u32[]{:S(2)}) collective-permute-start(bf16[208,512]{1,0:T(8,128)(2,1)S(1)} %get-tuple-element.21), channel_id=1, source_target_pairs={{0,8},{8,16},{16,24},{24,0},{1,9},{9,17},{17,25},{25,1},{2,10},{10... | collective-permute-start | bytes 638984 | tf_op jit(solution)/shard_map/ppermute | solution.py:25
  35.3 5.2 %collective-permute-start.4 = (bf16[208,512]{1,0:T(8,128)(2,1)S(1)}, bf16[208,512]{1,0:T(8,128)(2,1)S(1)}, u32[]{:S(2)}, u32[]{:S(2)}) collective-permute-start(bf16[208,512]{1,0:T(8,128)(2,1)S(1)} %get-tuple-element.21), channel_id=1, source_target_pairs={{0,24},{8,0},{16,8},{24,16},{1,25},{9,1},{17,9},{25,17},{2,26},{10... | collective-permute-start | bytes 638984 | tf_op jit(solution)/shard_map/ppermute | solution.py:26
  40.5 5.9 %collective-permute-start.3 = (bf16[104,512]{1,0:T(8,128)(2,1)S(1)}, bf16[104,512]{1,0:T(8,128)(2,1)S(1)}, u32[]{:S(2)}, u32[]{:S(2)}) collective-permute-start(bf16[104,512]{1,0:T(8,128)(2,1)S(1)} %slice.101), channel_id=1, source_target_pairs={{0,8},{8,16},{16,24},{24,0},{1,9},{9,17},{17,25},{25,1},{2,10},{10... | collective-permute-start | bytes 319496 | tf_op jit(solution)/shard_map/ppermute | solution.py:28
  40.6 5.8 %collective-permute-start.5 = (bf16[104,512]{1,0:T(8,128)(2,1)S(1)}, bf16[104,512]{1,0:T(8,128)(2,1)S(1)}, u32[]{:S(2)}, u32[]{:S(2)}) collective-permute-start(bf16[104,512]{1,0:T(8,128)(2,1)S(1)} %slice.102), channel_id=1, source_target_pairs={{0,24},{8,0},{16,8},{24,16},{1,25},{9,1},{17,9},{25,17},{2,26},{10... | collective-permute-start | bytes 319496 | tf_op jit(solution)/shard_map/ppermute | solution.py:29
  43.6 8.4 %collective-permute-start.10 = (bf16[208,512]{1,0:T(8,128)(2,1)S(1)}, bf16[208,512]{1,0:T(8,128)(2,1)S(1)}, u32[]{:S(2)}, u32[]{:S(2)}) collective-permute-start(bf16[208,512]{1,0:T(8,128)(2,1)S(1)} %get-tuple-element.22), channel_id=1, source_target_pairs={{0,1},{1,2},{2,3},{3,0},{4,5},{5,6},{6,7},{7,4},{8,9},{9,10},{10,1... | collective-permute-start | bytes 638984 | tf_op jit(solution)/shard_map/ppermute | solution.py:25
  44.4 7.7 %collective-permute-start.12 = (bf16[208,512]{1,0:T(8,128)(2,1)S(1)}, bf16[208,512]{1,0:T(8,128)(2,1)S(1)}, u32[]{:S(2)}, u32[]{:S(2)}) collective-permute-start(bf16[208,512]{1,0:T(8,128)(2,1)S(1)} %get-tuple-element.22), channel_id=1, source_target_pairs={{0,3},{1,0},{2,1},{3,2},{4,7},{5,4},{6,5},{7,6},{8,11},{9,8},{10,9... | collective-permute-start | bytes 638984 | tf_op jit(solution)/shard_map/ppermute | solution.py:26
  47.8 33.7 %copy-start.8 = (s32[256]{0:T(256)S(1)}, s32[256]{0:T(256)}, u32[]{:S(2)}) copy-start(s32[256]{0:T(256)} %param.17) | copy-start | bytes 3076
  47.8 30.6 %collective-permute-start.6 = (bf16[4,208,512]{2,1,0:T(8,128)(2,1)}, bf16[4,208,512]{2,1,0:T(8,128)(2,1)S(1)}, u32[]{:S(2)}, u32[]{:S(2)}) collective-permute-start(bf16[4,208,512]{2,1,0:T(8,128)(2,1)} %get-tuple-element.16), channel_id=1, source_target_pairs={{0,1},{1,2},{2,3},{3,0},{4,5},{5,6},{6,7},{7,4},{8,9},{9,10},{10,1... | collective-permute-start | bytes 2555912 | tf_op jit(solution)/shard_map/ppermute | solution.py:25
  47.8 30.9 %collective-permute-start.8 = (bf16[4,208,512]{2,1,0:T(8,128)(2,1)}, bf16[4,208,512]{2,1,0:T(8,128)(2,1)S(1)}, u32[]{:S(2)}, u32[]{:S(2)}) collective-permute-start(bf16[4,208,512]{2,1,0:T(8,128)(2,1)} %get-tuple-element.16), channel_id=1, source_target_pairs={{0,3},{1,0},{2,1},{3,2},{4,7},{5,4},{6,5},{7,6},{8,11},{9,8},{10,9... | collective-permute-start | bytes 2555912 | tf_op jit(solution)/shard_map/ppermute | solution.py:26
  52.0 20.2 %collective-permute-start.11 = (bf16[104,512]{1,0:T(8,128)(2,1)S(1)}, bf16[104,512]{1,0:T(8,128)(2,1)S(1)}, u32[]{:S(2)}, u32[]{:S(2)}) collective-permute-start(bf16[104,512]{1,0:T(8,128)(2,1)S(1)} %slice.106), channel_id=1, source_target_pairs={{0,1},{1,2},{2,3},{3,0},{4,5},{5,6},{6,7},{7,4},{8,9},{9,10},{10,1... | collective-permute-start | bytes 319496 | tf_op jit(solution)/shard_map/ppermute | solution.py:28
  52.1 20.1 %collective-permute-start.13 = (bf16[104,512]{1,0:T(8,128)(2,1)S(1)}, bf16[104,512]{1,0:T(8,128)(2,1)S(1)}, u32[]{:S(2)}, u32[]{:S(2)}) collective-permute-start(bf16[104,512]{1,0:T(8,128)(2,1)S(1)} %slice.107), channel_id=1, source_target_pairs={{0,3},{1,0},{2,1},{3,2},{4,7},{5,4},{6,5},{7,6},{8,11},{9,8},{10,9... | collective-permute-start | bytes 319496 | tf_op jit(solution)/shard_map/ppermute | solution.py:29
  73.6 21.3 %collective-permute-start.14 = (bf16[4,208,512]{2,1,0:T(8,128)(2,1)}, bf16[4,208,512]{2,1,0:T(8,128)(2,1)S(1)}, u32[]{:S(2)}, u32[]{:S(2)}) collective-permute-start(bf16[4,208,512]{2,1,0:T(8,128)(2,1)} %get-tuple-element.18), channel_id=1, source_target_pairs={{0,8},{8,16},{16,24},{24,0},{1,9},{9,17},{17,25},{25,1},{2,10},{10... | collective-permute-start | bytes 2555912 | tf_op jit(solution)/shard_map/ppermute | solution.py:25
  73.6 21.4 %collective-permute-start.16 = (bf16[4,208,512]{2,1,0:T(8,128)(2,1)}, bf16[4,208,512]{2,1,0:T(8,128)(2,1)S(1)}, u32[]{:S(2)}, u32[]{:S(2)}) collective-permute-start(bf16[4,208,512]{2,1,0:T(8,128)(2,1)} %get-tuple-element.18), channel_id=1, source_target_pairs={{0,24},{8,0},{16,8},{24,16},{1,25},{9,1},{17,9},{25,17},{2,26},{10... | collective-permute-start | bytes 2555912 | tf_op jit(solution)/shard_map/ppermute | solution.py:26
  78.4 19.5 %copy-start.1 = (bf16[4,208,512]{2,1,0:T(8,128)(2,1)}, bf16[4,208,512]{2,1,0:T(8,128)(2,1)S(1)}, u32[]{:S(2)}) copy-start(bf16[4,208,512]{2,1,0:T(8,128)(2,1)S(1)} %collective-permute-done.6) | copy-start | bytes 2555908
  78.4 19.4 %collective-permute-start.7 = (bf16[2,208,512]{2,1,0:T(8,128)(2,1)S(1)}, bf16[2,208,512]{2,1,0:T(8,128)(2,1)S(1)}, u32[]{:S(2)}, u32[]{:S(2)}) collective-permute-start(bf16[2,208,512]{2,1,0:T(8,128)(2,1)S(1)} %slice.103), channel_id=1, source_target_pairs={{0,1},{1,2},{2,3},{3,0},{4,5},{5,6},{6,7},{7,4},{8,9},{9,10},{10,1... | collective-permute-start | bytes 1277960 | tf_op jit(solution)/shard_map/ppermute | solution.py:28
  78.7 19.2 %copy-start.2 = (bf16[4,208,512]{2,1,0:T(8,128)(2,1)}, bf16[4,208,512]{2,1,0:T(8,128)(2,1)S(1)}, u32[]{:S(2)}) copy-start(bf16[4,208,512]{2,1,0:T(8,128)(2,1)S(1)} %collective-permute-done.8) | copy-start | bytes 2555908
  78.7 19.1 %collective-permute-start.9 = (bf16[2,208,512]{2,1,0:T(8,128)(2,1)S(1)}, bf16[2,208,512]{2,1,0:T(8,128)(2,1)S(1)}, u32[]{:S(2)}, u32[]{:S(2)}) collective-permute-start(bf16[2,208,512]{2,1,0:T(8,128)(2,1)S(1)} %slice.104), channel_id=1, source_target_pairs={{0,3},{1,0},{2,1},{3,2},{4,7},{5,4},{6,5},{7,6},{8,11},{9,8},{10,9... | collective-permute-start | bytes 1277960 | tf_op jit(solution)/shard_map/ppermute | solution.py:29
  94.9 11.0 %collective-permute-start.15 = (bf16[2,208,512]{2,1,0:T(8,128)(2,1)S(1)}, bf16[2,208,512]{2,1,0:T(8,128)(2,1)S(1)}, u32[]{:S(2)}, u32[]{:S(2)}) collective-permute-start(bf16[2,208,512]{2,1,0:T(8,128)(2,1)S(1)} %slice.108), channel_id=1, source_target_pairs={{0,8},{8,16},{16,24},{24,0},{1,9},{9,17},{17,25},{25,1},{2,10},{10... | collective-permute-start | bytes 1277960 | tf_op jit(solution)/shard_map/ppermute | solution.py:28
  95.1 10.9 %collective-permute-start.17 = (bf16[2,208,512]{2,1,0:T(8,128)(2,1)S(1)}, bf16[2,208,512]{2,1,0:T(8,128)(2,1)S(1)}, u32[]{:S(2)}, u32[]{:S(2)}) collective-permute-start(bf16[2,208,512]{2,1,0:T(8,128)(2,1)S(1)} %slice.109), channel_id=1, source_target_pairs={{0,24},{8,0},{16,8},{24,16},{1,25},{9,1},{17,9},{25,17},{2,26},{10... | collective-permute-start | bytes 1277960 | tf_op jit(solution)/shard_map/ppermute | solution.py:29
  97.9 8.1 %copy-start = (bf16[1,4,208,512]{3,2,0,1:T(8,128)(2,1)S(1)}, bf16[1,4,208,512]{3,2,0,1:T(8,128)(2,1)}, u32[]{:S(2)}) copy-start(bf16[1,4,208,512]{3,2,0,1:T(8,128)(2,1)} %get-tuple-element.17) | copy-start | bytes 2555908
  97.9 8.1 %copy-start.4 = (bf16[4,208,512]{2,1,0:T(8,128)(2,1)S(1)}, bf16[4,208,512]{2,1,0:T(8,128)(2,1)}, u32[]{:S(2)}) copy-start(bf16[4,208,512]{2,1,0:T(8,128)(2,1)} %copy-done.3) | copy-start | bytes 2555908
  117.3 74.2 %copy-start.7 = (bf16[2,256,512]{2,1,0:T(8,128)(2,1)S(1)}, bf16[2,256,512]{2,1,0:T(8,128)(2,1)}, u32[]{:S(2)}) copy-start(bf16[2,256,512]{2,1,0:T(8,128)(2,1)} %param.16) | copy-start | bytes 1572868
  (3 other events, 14.0 us)

commit v6 on v4

--- a/solution.py
+++ b/solution.py
@@ -72,39 +72,62 @@
     eye = (ridx == cidx).astype(jnp.float32)
     for b in range(boxes):
         m_ref[b] = g_ref[b] + (n - 1.0) * eye
+    width = 4
     bi = lax.broadcasted_iota(jnp.int32, (nb, nb), 0)
     bj = lax.broadcasted_iota(jnp.int32, (nb, nb), 1)
     beye = (bi == bj).astype(jnp.float32)
 
+    def mul2(x, y):
+        return [[x[i][0] * y[0][j] + x[i][1] * y[1][j] for j in range(2)] for i in range(2)]
+
+    def inv2(x):
+        r = 1.0 / (x[0][0] * x[1][1] - x[0][1] * x[1][0])
+        return [[x[1][1] * r, -x[0][1] * r], [-x[1][0] * r, x[0][0] * r]]
+
     def pivot(step, blocks):
-        k = 2 * step
-        rk, rk1 = bi == k, bi == k + 1
-        lk, lk1 = bj[0:1] == k, bj[0:1] == k + 1
+        k = width * step
+        rmask = [bi == k + m for m in range(width)]
+        lmask = [bj[0:1] == k + m for m in range(width)]
         out = []
         for d in blocks:
-            r1 = jnp.sum(jnp.where(rk, d, 0.0), axis=0, keepdims=True)
-            r2 = jnp.sum(jnp.where(rk1, d, 0.0), axis=0, keepdims=True)
-            c1 = jnp.sum(jnp.where(bj == k, d, 0.0), axis=1, keepdims=True)
-            c2 = jnp.sum(jnp.where(bj == k + 1, d, 0.0), axis=1, keepdims=True)
-            a = jnp.sum(jnp.where(lk, r1, 0.0), axis=1, keepdims=True)
-            b = jnp.sum(jnp.where(lk1, r1, 0.0), axis=1, keepdims=True)
-            c = jnp.sum(jnp.where(lk, r2, 0.0), axis=1, keepdims=True)
-            e = jnp.sum(jnp.where(lk1, r2, 0.0), axis=1, keepdims=True)
-            rdet = 1.0 / (a * e - b * c)
-            q11, q12, q21, q22 = e * rdet, -b * rdet, -c * rdet, a * rdet
-            rn1 = q11 * r1 + q12 * r2
-            rn2 = q21 * r1 + q22 * r2
-            f1 = jnp.where(lk, 1.0 + q11, jnp.where(lk1, q12, rn1))
-            f2 = jnp.where(lk, q21, jnp.where(lk1, 1.0 + q22, rn2))
-            g1 = jnp.where(lk, q11, jnp.where(lk1, q12, rn1))
-            g2 = jnp.where(lk, q21, jnp.where(lk1, q22, rn2))
-            new = d - c1 * f1 - c2 * f2
-            out.append(jnp.where(rk, g1, jnp.where(rk1, g2, new)))
+            rows = [jnp.sum(jnp.where(rmask[m], d, 0.0), axis=0, keepdims=True) for m in range(width)]
+            cols = [jnp.sum(jnp.where(bj == k + m, d, 0.0), axis=1, keepdims=True) for m in range(width)]
+            p = [[jnp.sum(jnp.where(lmask[j], rows[i], 0.0), axis=1, keepdims=True)
+                  for j in range(width)] for i in range(width)]
+            a = [[p[0][0], p[0][1]], [p[1][0], p[1][1]]]
+            b = [[p[0][2], p[0][3]], [p[1][2], p[1][3]]]
+            c = [[p[2][0], p[2][1]], [p[3][0], p[3][1]]]
+            e = [[p[2][2], p[2][3]], [p[3][2], p[3][3]]]
+            ai = inv2(a)
+            aib = mul2(ai, b)
+            cai = mul2(c, ai)
+            cab = mul2(c, aib)
+            si = inv2([[e[i][j] - cab[i][j] for j in range(2)] for i in range(2)])
+            q12 = [[-v for v in row] for row in mul2(aib, si)]
+            q21 = [[-v for v in row] for row in mul2(si, cai)]
+            q12c = mul2(q12, cai)
+            q11 = [[ai[i][j] - q12c[i][j] for j in range(2)] for i in range(2)]
+            q = [q11[0] + q12[0], q11[1] + q12[1], q21[0] + si[0], q21[1] + si[1]]
+            new = d
+            gs = []
+            for i in range(width):
+                rn = q[i][0] * rows[0]
+                for j in range(1, width):
+                    rn = rn + q[i][j] * rows[j]
+                f, g = rn, rn
+                for j in range(width):
+                    f = jnp.where(lmask[j], q[i][j] + (1.0 if i == j else 0.0), f)
+                    g = jnp.where(lmask[j], q[i][j], g)
+                new = new - cols[i] * f
+                gs.append(g)
+            for i in range(width):
+                new = jnp.where(rmask[i], gs[i], new)
+            out.append(new)
         return tuple(out)
 
     for kb in range(n // nb):
         s = slice(kb * nb, (kb + 1) * nb)
-        dinvs = lax.fori_loop(0, nb // 2, pivot, tuple(m_ref[b, s, s] for b in range(boxes)))
+        dinvs = lax.fori_loop(0, nb // width, pivot, tuple(m_ref[b, s, s] for b in range(boxes)))
         for b in range(boxes):
             dinv = dinvs[b]
             rn = jnp.dot(dinv, m_ref[b, s, :], precision=HI, preferred_element_type=jnp.float32)
@@ -120,7 +143,7 @@
         t_ref[b] = (0.5 * eye + (0.5 * (n - 1.0)) * inv + wbar).astype(t_ref.dtype)
 
 
-def make_transform(gram, innov_rows, nb=128):
+def make_transform(gram, innov_rows, nb=64):
     boxes, n, _ = gram.shape
     return pl.pallas_call(
         functools.partial(_transform_kernel, nb=nb),

time: 198 us -> 190 us (0.960)
  Pallas kernels: 74.1 us -> 66.7 us
    pallas_call x1, Pallas kernels: 57.5 us -> 50.1 us  [make_transform(): pl.pallas_call(functools.partial(_transform_kernel, nb=nb), out_shape=jax...]
where the time goes in v6:
time: 190 us
  waiting for transfers between devices  74.4 us (39%)
  Pallas kernels  66.7 us (35%)
  between operations  13.6 us (7%)
  blocking collectives  13.2 us (7%)
  local copies, waits for them, and re-layouts  7.6 us (4%)
  starting transfers between devices  7.07 us (4%)
  other arithmetic  5.53 us (3%)
  matrix products  2.17 us (1%)
    all_gather x1, waiting for transfers between devices, body(): full = lax.all_gather(half, ('tx', 'ty'), axis=0)  73.3 us
    pallas_call x1, Pallas kernels, make_transform(): pl.pallas_call(functools.partial(_transform_kernel, nb=nb), out_shape=jax...  50.1 us
    pallas_call x1, Pallas kernels, gram_terms(): pl.pallas_call(_gram_kernel, grid=(rows // step,), in_specs=[pl.BlockSpec...  16.5 us
    all_gather x1, blocking collectives, body(): half = lax.all_gather(block, 'tz', axis=0)  13.2 us
    ppermute x2, starting transfers between devices, passed_along(): return lax.ppermute(block, axis, route)  7.07 us
  transfers between devices with their start and end apart: 3, of which 2 were waited for; matrix products, arithmetic and copies ran while one was open for 2% of the time, Pallas kernels for 0%

profile of v6, /device:TPU:1, one launch (start us, length us, event | category | flops | bytes accessed | tf_op | source)
XLA Modules:
  0.0 190.2 jit_solution(11704768204360632255)
XLA Ops:
  6.5 1.0 convert_reduce_fusion.1
  7.5 0.7 compare_select_fusion
  8.2 0.7 subtract_convert_fusion
  8.9 0.7 gather_fusion.4
  9.6 0.7 gather_fusion.5
  10.4 1.0 fusion.6
  11.5 0.6 gather_fusion.3
  12.1 5.1 %collective-permute-start.1 = (bf16[33,512]{1,0:T(8,128)(2,1)S(1)}, bf16[33,512]{1,0:T(8,128)(2,1)S(1)}, u32[]{:S(2)}, u32[]{:S(2)}) collective-permute-start(bf16[33,512]{1,0:T(8,128)(2,1)S(1)} %pad_maximum_fusion.1), channel_id=1, source_target_pairs={{32,0},{64,32},{96,64},{128,96},{160,128},{192,160},{224,192},{33,... | collective-permute-start | bytes 101384 | tf_op jit(solution)/shard_map/ppermute | solution.py:18
  17.3 0.7 compare_select_fusion.1
  17.9 0.7 gather_fusion.1
  18.6 0.7 gather_fusion.2
  19.4 0.6 gather_fusion
  20.1 1.9 %collective-permute-start = (bf16[33,512]{1,0:T(8,128)(2,1)S(1)}, bf16[33,512]{1,0:T(8,128)(2,1)S(1)}, u32[]{:S(2)}, u32[]{:S(2)}) collective-permute-start(bf16[33,512]{1,0:T(8,128)(2,1)S(1)} %pad_maximum_fusion), channel_id=1, source_target_pairs={{0,32},{32,64},{64,96},{96,128},{128,160},{160,192},{192,224},{1,3... | collective-permute-start | bytes 101384 | tf_op jit(solution)/shard_map/ppermute | solution.py:18
  22.1 1.1 collective-permute-done
  23.4 0.2 concatenate.26
  23.6 13.2 %all-gather = bf16[416,512]{1,0:T(8,128)(2,1)} all-gather(bf16[208,512]{1,0:T(8,128)(2,1)S(1)} %concatenate.26), channel_id=2, replica_groups=mesh['region'=8,'tx'=4,'tz'=2,'ty'=4] {'tz'}, dimensions={0}, use_global_device_ids=true | all-gather | bytes 638976 | tf_op jit(solution)/shard_map/all_gather | solution.py:183
  37.2 73.3 %all-gather.4.cloned.1.call-done = bf16[32,208,512]{2,1,0:T(8,128)(2,1)} async-done(((bf16[2,208,512]{2,1,0:T(8,128)(2,1)}), bf16[32,208,512]{2,1,0:T(8,128)(2,1)}) %all-gather.4.cloned.1.call-update) | async-done | bytes 6815760 | tf_op jit(solution)/shard_map/all_gather | solution.py:184
  110.5 1.0 slice_convert_fusion
  111.8 0.7 pad.26.s_ref
  112.7 0.7 pad.28.w_ref
  113.4 16.5 %shard_map.91 = (f32[2,512,512]{2,1,0:T(8,128)}, f32[16,512]{1,0:T(8,128)}) custom-call(bf16[6656,512]{1,0:T(8,128)(2,1)} %bitcast.28, f32[8,6656]{1,0:T(8,128)} %pad.26.s_ref, bf16[16,6656]{1,0:T(8,128)(2,1)} %pad.28.w_ref), custom_call_target="tpu_custom_call" | custom-call | tf_op jit(solution)/shard_map/pallas_call | solution.py:49
  129.9 50.1 %shard_map.92 = bf16[2,512,512]{2,1,0:T(8,128)(2,1)} custom-call(f32[2,512,512]{2,1,0:T(8,128)} %get-tuple-element.7.g_ref, f32[16,512]{1,0:T(8,128)} %get-tuple-element.8.v_ref), custom_call_target="tpu_custom_call" | custom-call | tf_op jit(solution)/shard_map/pallas_call | solution.py:148
  180.1 2.2 %multiply_reduce_fusion = f32[512,2,256]{2,0,1:T(8,128)S(1)} fusion(bf16[2,512,512]{2,1,0:T(8,128)(2,1)} %shard_map.92, f32[2,256]{1,0:T(2,128)S(1)} %compare_convert_fusion, bf16[2,256,512]{2,1,0:T(8,128)(2,1)S(1)} %copy-done, f32[2,256]{1,0:T(2,128)S(1)} %broadcast_multiply_fusion.1), kind=kOutput, calls=%fused_computation.6 | convolution fusion | flops 538443776 | bytes 2625536 | tf_op jit(solution)/shard_map/fck,bkj->bfcj/dot_general | solution.py:203
  182.3 1.0 copy.18
  (42 shorter events, 1.5 us)
Async XLA Ops:
  6.5 103.9 %all-gather.4.cloned.1.call-start = ((), (), s32[]{:S(2)}) async-start(), calls=%async_computation | async-start | bytes 7241728 | tf_op jit(solution)/shard_map/all_gather | solution.py:184
  9.6 27.2 %copy-start.1 = (f32[2,4096]{1,0:T(2,128)S(1)}, f32[2,4096]{1,0:T(2,128)}, u32[]{:S(2)}) copy-start(f32[2,4096]{1,0:T(2,128)} %param.14) | copy-start | bytes 98308
  9.6 27.2 %copy-start.2 = (f32[2,2048]{1,0:T(2,128)S(1)}, f32[2,2048]{1,0:T(2,128)}, u32[]{:S(2)}) copy-start(f32[2,2048]{1,0:T(2,128)} %param.15) | copy-start | bytes 49156
  10.3 26.7 %copy-start = (bf16[2,256,512]{2,1,0:T(8,128)(2,1)S(1)}, bf16[2,256,512]{2,1,0:T(8,128)(2,1)}, u32[]{:S(2)}) copy-start(bf16[2,256,512]{2,1,0:T(8,128)(2,1)} %param.16) | copy-start | bytes 1572868
  12.1 25.1 %copy-start.3 = (s32[256]{0:T(256)S(1)}, s32[256]{0:T(256)}, u32[]{:S(2)}) copy-start(s32[256]{0:T(256)} %param.17) | copy-start | bytes 3076
  12.1 9.9 %collective-permute-start.1 = (bf16[33,512]{1,0:T(8,128)(2,1)S(1)}, bf16[33,512]{1,0:T(8,128)(2,1)S(1)}, u32[]{:S(2)}, u32[]{:S(2)}) collective-permute-start(bf16[33,512]{1,0:T(8,128)(2,1)S(1)} %pad_maximum_fusion.1), channel_id=1, source_target_pairs={{32,0},{64,32},{96,64},{128,96},{160,128},{192,160},{224,192},{33,... | collective-permute-start | bytes 101384 | tf_op jit(solution)/shard_map/ppermute | solution.py:18
  20.1 3.1 %collective-permute-start = (bf16[33,512]{1,0:T(8,128)(2,1)S(1)}, bf16[33,512]{1,0:T(8,128)(2,1)S(1)}, u32[]{:S(2)}, u32[]{:S(2)}) collective-permute-start(bf16[33,512]{1,0:T(8,128)(2,1)S(1)} %pad_maximum_fusion), channel_id=1, source_target_pairs={{0,32},{32,64},{64,96},{96,128},{128,160},{160,192},{192,224},{1,3... | collective-permute-start | bytes 101384 | tf_op jit(solution)/shard_map/ppermute | solution.py:18
Sparse Core Ops, SparseCore 0:
  36.9 73.5 all-gather.3

commit v7 on v6

--- a/solution.py
+++ b/solution.py
@@ -181,7 +181,9 @@
         [anomaly, lower_a, upper_a, info_row[None],
          jnp.zeros((block_rows - pool_rows - 1, members), jnp.bfloat16)], axis=0)
     half = lax.all_gather(block, "tz", axis=0)
-    full = lax.all_gather(half, ("tx", "ty"), axis=0)
+    plane = nx * ny
+    spread = jnp.broadcast_to(half[None], (plane,) + half.shape).reshape((plane * nz,) + half.shape[1:])
+    full = lax.all_to_all(spread, ("tx", "ty"), 0, 0, tiled=True).reshape((plane,) + half.shape)
     info = full[:, :, pool_rows, :2 * pool_rows].astype(jnp.float32)
     inv_all = info[:, :, :pool_rows]
     innov_all = info[:, :, pool_rows:]

time: 190 us -> 237 us (1.25)
  the two profiles are of different devices: /device:TPU:1 before, /device:TPU:156 now
where the time goes in v7:
time: 237 us; the launch traced here: 236 us
  waiting for transfers between devices  122 us (51%)
  Pallas kernels  66.7 us (28%)
  blocking collectives  17 us (7%)
  local copies, waits for them, and re-layouts  12.1 us (5%)
  starting transfers between devices  11.6 us (5%)
  other arithmetic  4.56 us (2%)
    all_to_all x1, waiting for transfers between devices, body(): lax.all_to_all(spread, ('tx', 'ty'), 0, 0, tiled=True)  121 us
    pallas_call x1, Pallas kernels, make_transform(): pl.pallas_call(functools.partial(_transform_kernel, nb=nb), out_shape=jax...  50.1 us
    all_gather x1, blocking collectives, body(): half = lax.all_gather(block, 'tz', axis=0)  17 us
    pallas_call x1, Pallas kernels, gram_terms(): pl.pallas_call(_gram_kernel, grid=(rows // step,), in_specs=[pl.BlockSpec...  16.6 us
    all_to_all x1, starting transfers between devices, body(): lax.all_to_all(spread, ('tx', 'ty'), 0, 0, tiled=True)  7.26 us
  transfers between devices with their start and end apart: 3, of which 2 were waited for; matrix products, arithmetic and copies ran while one was open for 1% of the time, Pallas kernels for 0%

profile of v7, /device:TPU:156, one launch (start us, length us, event | category | flops | bytes accessed | tf_op | source)
XLA Modules:
  0.0 236.2 jit_solution(15789325457977835631)
XLA Ops:
  0.0 1.0 convert_reduce_fusion.1
  1.0 0.7 compare_select_fusion
  1.7 0.7 subtract_convert_fusion
  2.4 0.7 gather_fusion.4
  3.1 0.7 gather_fusion.5
  3.9 1.0 fusion.6
  5.5 1.3 collective-permute-start.1
  6.8 0.7 compare_select_fusion.1
  7.5 0.7 gather_fusion.1
  8.2 0.7 gather_fusion.2
  8.9 0.6 gather_fusion
  9.6 3.0 %collective-permute-start = (bf16[33,512]{1,0:T(8,128)(2,1)S(1)}, bf16[33,512]{1,0:T(8,128)(2,1)S(1)}, u32[]{:S(2)}, u32[]{:S(2)}) collective-permute-start(bf16[33,512]{1,0:T(8,128)(2,1)S(1)} %pad_maximum_fusion), channel_id=1, source_target_pairs={{0,32},{32,64},{64,96},{96,128},{128,160},{160,192},{192,224},{1,3... | collective-permute-start | bytes 101384 | tf_op jit(solution)/shard_map/ppermute | solution.py:18
  12.7 0.8 collective-permute-done
  13.9 17.0 %all-gather = bf16[416,512]{1,0:T(8,128)(2,1)S(1)} all-gather(bf16[208,512]{1,0:T(8,128)(2,1)S(1)} %concatenate.26), channel_id=2, replica_groups=mesh['region'=8,'tx'=4,'tz'=2,'ty'=4] {'tz'}, dimensions={0}, use_global_device_ids=true | all-gather | bytes 638976 | tf_op jit(solution)/shard_map/all_gather | solution.py:183
  30.9 3.6 %broadcast_in_dim.46 = bf16[16,2,208,512]{3,2,1,0:T(8,128)(2,1)} broadcast(bf16[2,208,512]{2,1,0:T(8,128)(2,1)S(1)} %bitcast.31), dimensions={1,2,3} | broadcast | bytes 7241728 | tf_op jit(solution)/shard_map/broadcast_in_dim | solution.py:185
  34.5 7.3 %all-to-all-start = ((bf16[32,208,512]{2,1,0:T(8,128)(2,1)}), bf16[32,208,512]{2,1,0:T(8,128)(2,1)}, u32[]{:S(2)}, u32[]{:S(2)}) async-start(bf16[32,208,512]{2,1,0:T(8,128)(2,1)} %bitcast.30), calls=%async_computation | async-start | bytes 13631488 | tf_op jit(solution)/shard_map/all_to_all | solution.py:186
  42.2 121.1 %all-to-all-done = bf16[32,208,512]{2,1,0:T(8,128)(2,1)} async-done(((bf16[32,208,512]{2,1,0:T(8,128)(2,1)}), bf16[32,208,512]{2,1,0:T(8,128)(2,1)}, u32[]{:S(2)}, u32[]{:S(2)}) %all-to-all-start) | async-done | bytes 6815776 | tf_op jit(solution)/shard_map/all_to_all | solution.py:186
  163.3 1.0 slice.54
  164.6 0.7 pad.26.s_ref
  165.5 0.7 pad.28.w_ref
  166.2 16.6 %shard_map.91 = (f32[2,512,512]{2,1,0:T(8,128)}, f32[16,512]{1,0:T(8,128)}) custom-call(bf16[6656,512]{1,0:T(8,128)(2,1)} %bitcast.6.a_ref, f32[8,6656]{1,0:T(8,128)} %pad.26.s_ref, bf16[16,6656]{1,0:T(8,128)(2,1)} %pad.28.w_ref), custom_call_target="tpu_custom_call" | custom-call | tf_op jit(solution)/shard_map/pallas_call | solution.py:49
  182.8 50.1 %shard_map.92 = bf16[2,512,512]{2,1,0:T(8,128)(2,1)} custom-call(f32[2,512,512]{2,1,0:T(8,128)} %get-tuple-element.7.g_ref, f32[16,512]{1,0:T(8,128)} %get-tuple-element.8.v_ref), custom_call_target="tpu_custom_call" | custom-call | tf_op jit(solution)/shard_map/pallas_call | solution.py:148
  232.9 2.2 multiply_reduce_fusion
  235.2 1.0 copy.19
  (42 shorter events, 2.3 us)
Async XLA Ops:
  5.5 7.2 %collective-permute-start.1 = (bf16[33,512]{1,0:T(8,128)(2,1)S(1)}, bf16[33,512]{1,0:T(8,128)(2,1)S(1)}, u32[]{:S(2)}, u32[]{:S(2)}) collective-permute-start(bf16[33,512]{1,0:T(8,128)(2,1)S(1)} %pad_maximum_fusion.1), channel_id=1, source_target_pairs={{32,0},{64,32},{96,64},{128,96},{160,128},{192,160},{224,192},{33,... | collective-permute-start | bytes 101384 | tf_op jit(solution)/shard_map/ppermute | solution.py:18
  9.6 3.9 %collective-permute-start = (bf16[33,512]{1,0:T(8,128)(2,1)S(1)}, bf16[33,512]{1,0:T(8,128)(2,1)S(1)}, u32[]{:S(2)}, u32[]{:S(2)}) collective-permute-start(bf16[33,512]{1,0:T(8,128)(2,1)S(1)} %pad_maximum_fusion), channel_id=1, source_target_pairs={{0,32},{32,64},{64,96},{96,128},{128,160},{160,192},{192,224},{1,3... | collective-permute-start | bytes 101384 | tf_op jit(solution)/shard_map/ppermute | solution.py:18
  34.5 7.3 %copy-start.1 = (f32[2,4096]{1,0:T(2,128)S(1)}, f32[2,4096]{1,0:T(2,128)}, u32[]{:S(2)}) copy-start(f32[2,4096]{1,0:T(2,128)} %param.14) | copy-start | bytes 98308
  34.5 7.3 %copy-start.2 = (f32[2,2048]{1,0:T(2,128)S(1)}, f32[2,2048]{1,0:T(2,128)}, u32[]{:S(2)}) copy-start(f32[2,2048]{1,0:T(2,128)} %param.15) | copy-start | bytes 49156
  34.5 7.5 %copy-start = (bf16[2,256,512]{2,1,0:T(8,128)(2,1)S(1)}, bf16[2,256,512]{2,1,0:T(8,128)(2,1)}, u32[]{:S(2)}) copy-start(bf16[2,256,512]{2,1,0:T(8,128)(2,1)} %param.16) | copy-start | bytes 1572868
  34.5 7.7 %copy-start.3 = (s32[256]{0:T(256)S(1)}, s32[256]{0:T(256)}, u32[]{:S(2)}) copy-start(s32[256]{0:T(256)} %param.17) | copy-start | bytes 3076
  34.5 128.8 %all-to-all-start = ((bf16[32,208,512]{2,1,0:T(8,128)(2,1)}), bf16[32,208,512]{2,1,0:T(8,128)(2,1)}, u32[]{:S(2)}, u32[]{:S(2)}) async-start(bf16[32,208,512]{2,1,0:T(8,128)(2,1)} %bitcast.30), calls=%async_computation | async-start | bytes 13631488 | tf_op jit(solution)/shard_map/all_to_all | solution.py:186

commit v8 on v6

--- a/solution.py
+++ b/solution.py
@@ -9,7 +9,7 @@
 from jax.sharding import PartitionSpec as P
 
 HI = lax.Precision.HIGHEST
-ROWS_PER_STEP = 1664
+ROWS_PER_STEP = 3328
 
 
 def passed_along(block, axis, distance):
@@ -25,18 +25,10 @@
         v_ref[...] = jnp.zeros(v_ref.shape, jnp.float32)
 
     a = a_ref[...]
-    af = a.astype(jnp.float32)
-    sv = s_ref[...]
-    lanes = 128
-    eye = (lax.broadcasted_iota(jnp.int32, (lanes, lanes), 0)
-           == lax.broadcasted_iota(jnp.int32, (lanes, lanes), 1))
+    at = a.astype(jnp.float32).T
     for b in range(g_ref.shape[0]):
-        cols = [jnp.sum(jnp.where(eye, sv[b:b + 1, c * lanes:(c + 1) * lanes], 0.0),
-                        axis=1, keepdims=True)
-                for c in range(a.shape[0] // lanes)]
-        sc = (af * jnp.concatenate(cols, axis=0)).astype(jnp.bfloat16)
-        g_ref[b] += lax.dot_general(sc, a, (((0,), (0,)), ((), ())),
-                                    preferred_element_type=jnp.float32)
+        sct = (at * s_ref[b:b + 1, :]).astype(jnp.bfloat16)
+        g_ref[b] += jnp.dot(sct, a, preferred_element_type=jnp.float32)
     v_ref[...] += jnp.dot(w_ref[...], a, preferred_element_type=jnp.float32)
 
 

time: 190 us -> 185 us (0.974)
  Pallas kernels: 66.7 us -> 61.6 us
    pallas_call x1, Pallas kernels: 16.5 us -> 11.5 us  [gram_terms(): pl.pallas_call(_gram_kernel, grid=(rows // step,), in_specs=[pl.BlockSpec...]
where the time goes in v8:
time: 185 us
  waiting for transfers between devices  74.4 us (40%)
  Pallas kernels  61.6 us (33%)
  between operations  13.6 us (7%)
  blocking collectives  13.2 us (7%)
  local copies, waits for them, and re-layouts  7.6 us (4%)
  starting transfers between devices  7.07 us (4%)
  other arithmetic  5.53 us (3%)
  matrix products  2.17 us (1%)
    all_gather x1, waiting for transfers between devices, body(): full = lax.all_gather(half, ('tx', 'ty'), axis=0)  73.3 us
    pallas_call x1, Pallas kernels, make_transform(): pl.pallas_call(functools.partial(_transform_kernel, nb=nb), out_shape=jax...  50.1 us
    all_gather x1, blocking collectives, body(): half = lax.all_gather(block, 'tz', axis=0)  13.2 us
    pallas_call x1, Pallas kernels, gram_terms(): pl.pallas_call(_gram_kernel, grid=(rows // step,), in_specs=[pl.BlockSpec...  11.5 us
    ppermute x2, starting transfers between devices, passed_along(): return lax.ppermute(block, axis, route)  7.07 us
  transfers between devices with their start and end apart: 3, of which 2 were waited for; matrix products, arithmetic and copies ran while one was open for 2% of the time, Pallas kernels for 0%

profile of v8, /device:TPU:1, one launch (start us, length us, event | category | flops | bytes accessed | tf_op | source)
XLA Modules:
  0.0 185.1 jit_solution(12888718831281224229)
XLA Ops:
  6.5 1.0 convert_reduce_fusion.1
  7.5 0.7 compare_select_fusion
  8.2 0.7 subtract_convert_fusion
  8.9 0.7 gather_fusion.4
  9.6 0.7 gather_fusion.5
  10.4 1.0 fusion.6
  11.5 0.6 gather_fusion.3
  12.1 5.1 %collective-permute-start.1 = (bf16[33,512]{1,0:T(8,128)(2,1)S(1)}, bf16[33,512]{1,0:T(8,128)(2,1)S(1)}, u32[]{:S(2)}, u32[]{:S(2)}) collective-permute-start(bf16[33,512]{1,0:T(8,128)(2,1)S(1)} %pad_maximum_fusion.1), channel_id=1, source_target_pairs={{32,0},{64,32},{96,64},{128,96},{160,128},{192,160},{224,192},{33,... | collective-permute-start | bytes 101384 | tf_op jit(solution)/shard_map/ppermute | solution.py:18
  17.3 0.7 compare_select_fusion.1
  17.9 0.7 gather_fusion.1
  18.6 0.7 gather_fusion.2
  19.4 0.6 gather_fusion
  20.1 1.9 %collective-permute-start = (bf16[33,512]{1,0:T(8,128)(2,1)S(1)}, bf16[33,512]{1,0:T(8,128)(2,1)S(1)}, u32[]{:S(2)}, u32[]{:S(2)}) collective-permute-start(bf16[33,512]{1,0:T(8,128)(2,1)S(1)} %pad_maximum_fusion), channel_id=1, source_target_pairs={{0,32},{32,64},{64,96},{96,128},{128,160},{160,192},{192,224},{1,3... | collective-permute-start | bytes 101384 | tf_op jit(solution)/shard_map/ppermute | solution.py:18
  22.1 1.1 collective-permute-done
  23.4 0.2 concatenate.26
  23.6 13.2 %all-gather = bf16[416,512]{1,0:T(8,128)(2,1)} all-gather(bf16[208,512]{1,0:T(8,128)(2,1)S(1)} %concatenate.26), channel_id=2, replica_groups=mesh['region'=8,'tx'=4,'tz'=2,'ty'=4] {'tz'}, dimensions={0}, use_global_device_ids=true | all-gather | bytes 638976 | tf_op jit(solution)/shard_map/all_gather | solution.py:175
  37.2 73.3 %all-gather.4.cloned.1.call-done = bf16[32,208,512]{2,1,0:T(8,128)(2,1)} async-done(((bf16[2,208,512]{2,1,0:T(8,128)(2,1)}), bf16[32,208,512]{2,1,0:T(8,128)(2,1)}) %all-gather.4.cloned.1.call-update) | async-done | bytes 6815760 | tf_op jit(solution)/shard_map/all_gather | solution.py:176
  110.5 1.0 slice_convert_fusion
  111.8 0.7 pad.26.s_ref
  112.7 0.7 pad.28.w_ref
  113.4 11.5 %shard_map.91 = (f32[2,512,512]{2,1,0:T(8,128)}, f32[16,512]{1,0:T(8,128)}) custom-call(bf16[6656,512]{1,0:T(8,128)(2,1)} %bitcast.28, f32[8,6656]{1,0:T(8,128)} %pad.26.s_ref, bf16[16,6656]{1,0:T(8,128)(2,1)} %pad.28.w_ref), custom_call_target="tpu_custom_call" | custom-call | tf_op jit(solution)/shard_map/pallas_call | solution.py:41
  124.9 50.1 %shard_map.92 = bf16[2,512,512]{2,1,0:T(8,128)(2,1)} custom-call(f32[2,512,512]{2,1,0:T(8,128)} %get-tuple-element.7.g_ref, f32[16,512]{1,0:T(8,128)} %get-tuple-element.8.v_ref), custom_call_target="tpu_custom_call" | custom-call | tf_op jit(solution)/shard_map/pallas_call | solution.py:140
  175.0 2.2 %multiply_reduce_fusion = f32[512,2,256]{2,0,1:T(8,128)S(1)} fusion(bf16[2,512,512]{2,1,0:T(8,128)(2,1)} %shard_map.92, f32[2,256]{1,0:T(2,128)S(1)} %compare_convert_fusion, bf16[2,256,512]{2,1,0:T(8,128)(2,1)S(1)} %copy-done, f32[2,256]{1,0:T(2,128)S(1)} %broadcast_multiply_fusion.1), kind=kOutput, calls=%fused_computation.6 | convolution fusion | flops 538443776 | bytes 2625536 | tf_op jit(solution)/shard_map/fck,bkj->bfcj/dot_general | solution.py:195
  177.3 1.0 copy.18
  (42 shorter events, 1.5 us)
Async XLA Ops:
  6.5 103.9 %all-gather.4.cloned.1.call-start = ((), (), s32[]{:S(2)}) async-start(), calls=%async_computation | async-start | bytes 7241728 | tf_op jit(solution)/shard_map/all_gather | solution.py:176
  9.6 27.2 %copy-start.1 = (f32[2,4096]{1,0:T(2,128)S(1)}, f32[2,4096]{1,0:T(2,128)}, u32[]{:S(2)}) copy-start(f32[2,4096]{1,0:T(2,128)} %param.14) | copy-start | bytes 98308
  9.6 27.2 %copy-start.2 = (f32[2,2048]{1,0:T(2,128)S(1)}, f32[2,2048]{1,0:T(2,128)}, u32[]{:S(2)}) copy-start(f32[2,2048]{1,0:T(2,128)} %param.15) | copy-start | bytes 49156
  10.3 26.7 %copy-start = (bf16[2,256,512]{2,1,0:T(8,128)(2,1)S(1)}, bf16[2,256,512]{2,1,0:T(8,128)(2,1)}, u32[]{:S(2)}) copy-start(bf16[2,256,512]{2,1,0:T(8,128)(2,1)} %param.16) | copy-start | bytes 1572868
  12.1 25.1 %copy-start.3 = (s32[256]{0:T(256)S(1)}, s32[256]{0:T(256)}, u32[]{:S(2)}) copy-start(s32[256]{0:T(256)} %param.17) | copy-start | bytes 3076
  12.1 9.9 %collective-permute-start.1 = (bf16[33,512]{1,0:T(8,128)(2,1)S(1)}, bf16[33,512]{1,0:T(8,128)(2,1)S(1)}, u32[]{:S(2)}, u32[]{:S(2)}) collective-permute-start(bf16[33,512]{1,0:T(8,128)(2,1)S(1)} %pad_maximum_fusion.1), channel_id=1, source_target_pairs={{32,0},{64,32},{96,64},{128,96},{160,128},{192,160},{224,192},{33,... | collective-permute-start | bytes 101384 | tf_op jit(solution)/shard_map/ppermute | solution.py:18
  20.1 3.1 %collective-permute-start = (bf16[33,512]{1,0:T(8,128)(2,1)S(1)}, bf16[33,512]{1,0:T(8,128)(2,1)S(1)}, u32[]{:S(2)}, u32[]{:S(2)}) collective-permute-start(bf16[33,512]{1,0:T(8,128)(2,1)S(1)} %pad_maximum_fusion), channel_id=1, source_target_pairs={{0,32},{32,64},{64,96},{96,128},{128,160},{160,192},{192,224},{1,3... | collective-permute-start | bytes 101384 | tf_op jit(solution)/shard_map/ppermute | solution.py:18
Sparse Core Ops, SparseCore 0:
  36.9 73.5 all-gather.3

commit v9 on v8

--- a/solution.py
+++ b/solution.py
@@ -172,14 +172,16 @@
     block = jnp.concatenate(
         [anomaly, lower_a, upper_a, info_row[None],
          jnp.zeros((block_rows - pool_rows - 1, members), jnp.bfloat16)], axis=0)
-    half = lax.all_gather(block, "tz", axis=0)
+    half = jnp.stack([block, lax.ppermute(block, "tz", [(0, 1), (1, 0)])])
     full = lax.all_gather(half, ("tx", "ty"), axis=0)
     info = full[:, :, pool_rows, :2 * pool_rows].astype(jnp.float32)
     inv_all = info[:, :, :pool_rows]
     innov_all = info[:, :, pool_rows:]
     local_w = loc_local.reshape(boxes, nx, nz, ny, record_count)
     edge_w = loc_edge.reshape(boxes, nx, nz, ny, edge_rows)
-    weights = jnp.concatenate([local_w, edge_w], axis=4).transpose(0, 1, 3, 2, 4)
+    weights = jnp.concatenate([local_w, edge_w], axis=4)
+    weights = jnp.take(weights, (lax.axis_index("tz") + jnp.arange(nz)) % nz, axis=2)
+    weights = weights.transpose(0, 1, 3, 2, 4)
     weights = weights.reshape(boxes, nx * ny, nz, pool_rows)
     obs_scale = weights * inv_all[None]
     weighted = (obs_scale * innov_all[None]).astype(jnp.bfloat16)

time: 185 us -> 186 us (level)
  blocking collectives: 13.2 us -> 0 us
  starting transfers between devices: 7.07 us -> 13.4 us
  waiting for transfers between devices: 74.4 us -> 79.9 us
    all_gather x1 -> x0, blocking collectives: 13.2 us -> none  [body(): half = lax.all_gather(block, 'tz', axis=0)]
    ppermute x0 -> x1, starting transfers between devices: none -> 6.21 us  [body(): half = jnp.stack([block, lax.ppermute(block, 'tz', [(0, 1), (1, 0)])])]
    ppermute x0 -> x1, waiting for transfers between devices: none -> 6.21 us  [body(): half = jnp.stack([block, lax.ppermute(block, 'tz', [(0, 1), (1, 0)])])]
  transfers between devices with their start and end apart: 3 -> 4, of which waited for: 2 -> 3; matrix products, arithmetic and copies ran while one was open for 2% -> 2% of each run, Pallas kernels for 0% -> 0%
where the time goes in v9:
time: 186 us; the launch traced here: 185 us
  waiting for transfers between devices  79.9 us (43%)
  Pallas kernels  61.6 us (33%)
  between operations  13.6 us (7%)
  starting transfers between devices  13.4 us (7%)
  local copies, waits for them, and re-layouts  8.21 us (4%)
  other arithmetic  6.4 us (3%)
  matrix products  2.17 us (1%)
    all_gather x1, waiting for transfers between devices, body(): full = lax.all_gather(half, ('tx', 'ty'), axis=0)  72.5 us
    pallas_call x1, Pallas kernels, make_transform(): pl.pallas_call(functools.partial(_transform_kernel, nb=nb), out_shape=jax...  50.1 us
    pallas_call x1, Pallas kernels, gram_terms(): pl.pallas_call(_gram_kernel, grid=(rows // step,), in_specs=[pl.BlockSpec...  11.5 us
    ppermute x2, starting transfers between devices, passed_along(): return lax.ppermute(block, axis, route)  7.2 us
    ppermute x1, starting transfers between devices, body(): half = jnp.stack([block, lax.ppermute(block, 'tz', [(0, 1), (1, 0)])])  6.21 us
    ppermute x1, waiting for transfers between devices, body(): half = jnp.stack([block, lax.ppermute(block, 'tz', [(0, 1), (1, 0)])])  6.21 us
  transfers between devices with their start and end apart: 4, of which 3 were waited for; matrix products, arithmetic and copies ran while one was open for 2% of the time, Pallas kernels for 0%

profile of v9, /device:TPU:1, one launch (start us, length us, event | category | flops | bytes accessed | tf_op | source)
XLA Modules:
  0.0 185.3 jit_solution(8530601858768319448)
XLA Ops:
  6.5 1.0 convert_reduce_fusion.1
  7.5 0.7 compare_select_fusion.2
  8.2 0.7 subtract_convert_fusion
  8.9 0.7 gather_fusion.4
  9.6 0.7 gather_fusion.5
  10.4 1.0 fusion.6
  12.1 5.3 %collective-permute-start.1 = (bf16[33,512]{1,0:T(8,128)(2,1)S(1)}, bf16[33,512]{1,0:T(8,128)(2,1)S(1)}, u32[]{:S(2)}, u32[]{:S(2)}) collective-permute-start(bf16[33,512]{1,0:T(8,128)(2,1)S(1)} %pad_maximum_fusion.3), channel_id=1, source_target_pairs={{32,0},{64,32},{96,64},{128,96},{160,128},{192,160},{224,192},{33,... | collective-permute-start | bytes 101384 | tf_op jit(solution)/shard_map/ppermute | solution.py:18
  17.4 0.7 compare_select_fusion.3
  18.0 0.7 gather_fusion.1
  18.7 0.7 gather_fusion.2
  19.4 0.6 gather_fusion
  20.2 1.9 %collective-permute-start = (bf16[33,512]{1,0:T(8,128)(2,1)S(1)}, bf16[33,512]{1,0:T(8,128)(2,1)S(1)}, u32[]{:S(2)}, u32[]{:S(2)}) collective-permute-start(bf16[33,512]{1,0:T(8,128)(2,1)S(1)} %pad_maximum_fusion.2), channel_id=1, source_target_pairs={{0,32},{32,64},{64,96},{96,128},{128,160},{160,192},{192,224},{1,3... | collective-permute-start | bytes 101384 | tf_op jit(solution)/shard_map/ppermute | solution.py:18
  22.2 1.1 collective-permute-done
  23.7 6.2 %collective-permute-start.2 = (bf16[208,512]{1,0:T(8,128)(2,1)S(1)}, bf16[208,512]{1,0:T(8,128)(2,1)S(1)}, u32[]{:S(2)}, u32[]{:S(2)}) collective-permute-start(bf16[208,512]{1,0:T(8,128)(2,1)S(1)} %concatenate.26), channel_id=1, source_target_pairs={{0,4},{4,0},{1,5},{5,1},{2,6},{6,2},{3,7},{7,3},{8,12},{12,8},{9,1... | collective-permute-start | bytes 638984 | tf_op jit(solution)/shard_map/ppermute | solution.py:175
  29.9 6.2 %collective-permute-done.2 = bf16[208,512]{1,0:T(8,128)(2,1)S(1)} collective-permute-done((bf16[208,512]{1,0:T(8,128)(2,1)S(1)}, bf16[208,512]{1,0:T(8,128)(2,1)S(1)}, u32[]{:S(2)}, u32[]{:S(2)}) %collective-permute-start.2) | collective-permute-done | bytes 213024 | tf_op jit(solution)/shard_map/ppermute | solution.py:175
  36.1 0.8 pad_maximum_fusion
  38.1 72.5 %all-gather.3.cloned.1.call-done = bf16[32,208,512]{2,1,0:T(8,128)(2,1)} async-done(((bf16[2,208,512]{2,1,0:T(8,128)(2,1)}), bf16[32,208,512]{2,1,0:T(8,128)(2,1)}) %all-gather.3.cloned.1.call-update) | async-done | bytes 6815760 | tf_op jit(solution)/shard_map/all_gather | solution.py:176
  110.6 1.0 slice_convert_fusion
  112.0 0.7 pad.26.s_ref
  112.8 0.7 pad.28.w_ref
  113.6 11.5 %shard_map.91 = (f32[2,512,512]{2,1,0:T(8,128)}, f32[16,512]{1,0:T(8,128)}) custom-call(bf16[6656,512]{1,0:T(8,128)(2,1)} %bitcast.31, f32[8,6656]{1,0:T(8,128)} %pad.26.s_ref, bf16[16,6656]{1,0:T(8,128)(2,1)} %pad.28.w_ref), custom_call_target="tpu_custom_call" | custom-call | tf_op jit(solution)/shard_map/pallas_call | solution.py:41
  125.0 50.1 %shard_map.92 = bf16[2,512,512]{2,1,0:T(8,128)(2,1)} custom-call(f32[2,512,512]{2,1,0:T(8,128)} %get-tuple-element.7.g_ref, f32[16,512]{1,0:T(8,128)} %get-tuple-element.8.v_ref), custom_call_target="tpu_custom_call" | custom-call | tf_op jit(solution)/shard_map/pallas_call | solution.py:140
  175.2 2.2 %multiply_reduce_fusion = f32[512,2,256]{2,0,1:T(8,128)S(1)} fusion(bf16[2,512,512]{2,1,0:T(8,128)(2,1)} %shard_map.92, f32[2,256]{1,0:T(2,128)S(1)} %compare_convert_fusion, bf16[2,256,512]{2,1,0:T(8,128)(2,1)S(1)} %copy-done, f32[2,256]{1,0:T(2,128)S(1)} %broadcast_multiply_fusion.1), kind=kOutput, calls=%fused_computation.7 | convolution fusion | flops 538443776 | bytes 2625536 | tf_op jit(solution)/shard_map/fck,bkj->bfcj/dot_general | solution.py:197
  177.5 1.0 copy.16
  (49 shorter events, 3.0 us)
Async XLA Ops:
  6.5 104.1 %all-gather.3.cloned.1.call-start = ((), (), s32[]{:S(2)}) async-start(), calls=%async_computation | async-start | bytes 7241728 | tf_op jit(solution)/shard_map/all_gather | solution.py:176
  10.3 26.6 %copy-start.1 = (f32[2,4096]{1,0:T(2,128)S(1)}, f32[2,4096]{1,0:T(2,128)}, u32[]{:S(2)}) copy-start(f32[2,4096]{1,0:T(2,128)} %param.14) | copy-start | bytes 98308
  10.3 26.6 %copy-start.2 = (f32[2,2048]{1,0:T(2,128)S(1)}, f32[2,2048]{1,0:T(2,128)}, u32[]{:S(2)}) copy-start(f32[2,2048]{1,0:T(2,128)} %param.15) | copy-start | bytes 49156
  12.0 25.9 %copy-start = (bf16[2,256,512]{2,1,0:T(8,128)(2,1)S(1)}, bf16[2,256,512]{2,1,0:T(8,128)(2,1)}, u32[]{:S(2)}) copy-start(bf16[2,256,512]{2,1,0:T(8,128)(2,1)} %param.16) | copy-start | bytes 1572868
  12.1 10.0 %collective-permute-start.1 = (bf16[33,512]{1,0:T(8,128)(2,1)S(1)}, bf16[33,512]{1,0:T(8,128)(2,1)S(1)}, u32[]{:S(2)}, u32[]{:S(2)}) collective-permute-start(bf16[33,512]{1,0:T(8,128)(2,1)S(1)} %pad_maximum_fusion.3), channel_id=1, source_target_pairs={{32,0},{64,32},{96,64},{128,96},{160,128},{192,160},{224,192},{33,... | collective-permute-start | bytes 101384 | tf_op jit(solution)/shard_map/ppermute | solution.py:18
  18.7 19.3 %copy-start.3 = (s32[256]{0:T(256)S(1)}, s32[256]{0:T(256)}, u32[]{:S(2)}) copy-start(s32[256]{0:T(256)} %param.17) | copy-start | bytes 3076
  20.2 3.1 %collective-permute-start = (bf16[33,512]{1,0:T(8,128)(2,1)S(1)}, bf16[33,512]{1,0:T(8,128)(2,1)S(1)}, u32[]{:S(2)}, u32[]{:S(2)}) collective-permute-start(bf16[33,512]{1,0:T(8,128)(2,1)S(1)} %pad_maximum_fusion.2), channel_id=1, source_target_pairs={{0,32},{32,64},{64,96},{96,128},{128,160},{160,192},{192,224},{1,3... | collective-permute-start | bytes 101384 | tf_op jit(solution)/shard_map/ppermute | solution.py:18
  23.7 12.4 %collective-permute-start.2 = (bf16[208,512]{1,0:T(8,128)(2,1)S(1)}, bf16[208,512]{1,0:T(8,128)(2,1)S(1)}, u32[]{:S(2)}, u32[]{:S(2)}) collective-permute-start(bf16[208,512]{1,0:T(8,128)(2,1)S(1)} %concatenate.26), channel_id=1, source_target_pairs={{0,4},{4,0},{1,5},{5,1},{2,6},{6,2},{3,7},{7,3},{8,12},{12,8},{9,1... | collective-permute-start | bytes 638984 | tf_op jit(solution)/shard_map/ppermute | solution.py:175
Sparse Core Ops, SparseCore 0:
  37.0 73.5 all-gather.2

commit v10 on v8

--- a/solution.py
+++ b/solution.py
@@ -57,7 +57,7 @@
     )(pool, scale_rows, weighted)
 
 
-def _transform_kernel(g_ref, v_ref, t_ref, m_ref, r_ref, *, nb):
+def _transform_kernel(g_ref, v_ref, s_ref, box_ref, o_ref, t_ref, m_ref, r_ref, *, nb):
     boxes, n, _ = g_ref.shape
     ridx = lax.broadcasted_iota(jnp.int32, (n, n), 0)
     cidx = lax.broadcasted_iota(jnp.int32, (n, n), 1)
@@ -133,16 +133,27 @@
         inv = m_ref[b]
         wbar = jnp.sum(inv * v_ref[b:b + 1, :], axis=1, keepdims=True)
         t_ref[b] = (0.5 * eye + (0.5 * (n - 1.0)) * inv + wbar).astype(t_ref.dtype)
-
-
-def make_transform(gram, innov_rows, nb=64):
+    box = box_ref[...]
+    for f in range(s_ref.shape[0]):
+        wide = s_ref[f].astype(jnp.float32)
+        smean = jnp.sum(wide, axis=1, keepdims=True) / n
+        anomaly = (wide - smean).astype(jnp.bfloat16)
+        total = jnp.zeros(wide.shape, jnp.float32)
+        for b in range(boxes):
+            upd = jnp.dot(anomaly, t_ref[b], preferred_element_type=jnp.float32)
+            total = total + jnp.where(box == b, upd, 0.0)
+        o_ref[f] = (smean + total).astype(o_ref.dtype)
+
+
+def analysis_of(gram, innov_rows, states, box_col, nb=64):
     boxes, n, _ = gram.shape
     return pl.pallas_call(
         functools.partial(_transform_kernel, nb=nb),
-        out_shape=jax.ShapeDtypeStruct((boxes, n, n), jnp.bfloat16),
-        scratch_shapes=[pltpu.VMEM((boxes, n, n), jnp.float32),
+        out_shape=jax.ShapeDtypeStruct(states.shape, states.dtype),
+        scratch_shapes=[pltpu.VMEM((boxes, n, n), jnp.bfloat16),
+                        pltpu.VMEM((boxes, n, n), jnp.float32),
                         pltpu.VMEM((boxes, nb, n), jnp.float32)],
-    )(gram, innov_rows)
+    )(gram, innov_rows, states, box_col)
 
 
 def body(ens_obs, obs_values, obs_var, edge_up, edge_down, loc_local, loc_edge, states, box_ids):
@@ -189,16 +200,7 @@
     weighted = jnp.pad(weighted, pad).reshape(boxes, -1)
     weighted = jnp.pad(weighted, ((0, 16 - boxes), (0, 0)))
     gram, innov_sum = gram_terms(full.reshape(-1, members), scale_rows, weighted, boxes)
-    transform = make_transform(gram, innov_sum)
-    smean = jnp.mean(states, axis=2, dtype=jnp.float32)
-    state_anomaly = (states.astype(jnp.float32) - smean[:, :, None]).astype(jnp.bfloat16)
-    updates = jnp.einsum(
-        "fck,bkj->bfcj", state_anomaly, transform, preferred_element_type=jnp.float32
-    )
-    box_range = jnp.arange(boxes, dtype=jnp.int32)
-    selector = (box_ids[None, :] == box_range[:, None]).astype(jnp.float32)
-    total = jnp.sum(selector[:, None, :, None] * updates, axis=0)
-    return (smean[:, :, None] + total).astype(jnp.bfloat16)
+    return analysis_of(gram, innov_sum, states, box_ids.reshape(-1, 1))
 
 
 def solution(mesh):

time: 185 us -> 183 us (0.989)
  waiting for transfers between devices: 74.4 us -> 71.7 us
  matrix products: 2.17 us -> 0 us
  local copies, waits for them, and re-layouts: 7.6 us -> 9.53 us
    all_gather x1, waiting for transfers between devices: 73.3 us -> 70.5 us  [body(): full = lax.all_gather(half, ('tx', 'ty'), axis=0)]
    dot_general x1 -> x0, matrix products: 2.17 us -> none  [body(): jnp.einsum('fck,bkj->bfcj', state_anomaly, transform, preferred_element_t...]
  transfers between devices with their start and end apart: 3 -> 3, of which waited for: 2 -> 2; matrix products, arithmetic and copies ran while one was open for 2% -> 3% of each run, Pallas kernels for 0% -> 0%
where the time goes in v10:
time: 183 us; the launch traced here: 182 us
  waiting for transfers between devices  71.7 us (39%)
  Pallas kernels  62.2 us (34%)
  between operations  13.5 us (7%)
  blocking collectives  13.2 us (7%)
  local copies, waits for them, and re-layouts  9.53 us (5%)
  starting transfers between devices  7.07 us (4%)
  other arithmetic  5.22 us (3%)
    all_gather x1, waiting for transfers between devices, body(): full = lax.all_gather(half, ('tx', 'ty'), axis=0)  70.5 us
    pallas_call x1, Pallas kernels, analysis_of(): pl.pallas_call(functools.partial(_transform_kernel, nb=nb), out_shape=jax...  50.7 us
    all_gather x1, blocking collectives, body(): half = lax.all_gather(block, 'tz', axis=0)  13.2 us
    pallas_call x1, Pallas kernels, gram_terms(): pl.pallas_call(_gram_kernel, grid=(rows // step,), in_specs=[pl.BlockSpec...  11.5 us
    ppermute x2, starting transfers between devices, passed_along(): return lax.ppermute(block, axis, route)  7.06 us
  transfers between devices with their start and end apart: 3, of which 2 were waited for; matrix products, arithmetic and copies ran while one was open for 3% of the time, Pallas kernels for 0%

profile of v10, /device:TPU:1, one launch (start us, length us, event | category | flops | bytes accessed | tf_op | source)
XLA Modules:
  0.0 182.3 jit_solution(1417367624957220022)
XLA Ops:
  6.5 1.0 convert_reduce_fusion
  7.5 0.7 compare_select_fusion
  8.2 0.7 subtract_convert_fusion
  8.9 0.7 gather_fusion.4
  9.6 0.7 gather_fusion.5
  10.4 1.0 fusion
  11.4 0.6 gather_fusion.3
  12.0 5.1 %collective-permute-start.1 = (bf16[33,512]{1,0:T(8,128)(2,1)S(1)}, bf16[33,512]{1,0:T(8,128)(2,1)S(1)}, u32[]{:S(2)}, u32[]{:S(2)}) collective-permute-start(bf16[33,512]{1,0:T(8,128)(2,1)S(1)} %pad_maximum_fusion.1), channel_id=1, source_target_pairs={{32,0},{64,32},{96,64},{128,96},{160,128},{192,160},{224,192},{33,... | collective-permute-start | bytes 101384 | tf_op jit(solution)/shard_map/ppermute | solution.py:18
  17.2 0.7 compare_select_fusion.1
  17.9 0.7 gather_fusion.1
  18.6 0.7 gather_fusion.2
  19.3 0.6 gather_fusion
  20.0 1.9 %collective-permute-start = (bf16[33,512]{1,0:T(8,128)(2,1)S(1)}, bf16[33,512]{1,0:T(8,128)(2,1)S(1)}, u32[]{:S(2)}, u32[]{:S(2)}) collective-permute-start(bf16[33,512]{1,0:T(8,128)(2,1)S(1)} %pad_maximum_fusion), channel_id=1, source_target_pairs={{0,32},{32,64},{64,96},{96,128},{128,160},{160,192},{192,224},{1,3... | collective-permute-start | bytes 101384 | tf_op jit(solution)/shard_map/ppermute | solution.py:18
  22.0 1.1 collective-permute-done
  23.5 13.2 %all-gather = bf16[416,512]{1,0:T(8,128)(2,1)} all-gather(bf16[208,512]{1,0:T(8,128)(2,1)S(1)} %concatenate.26), channel_id=2, replica_groups=mesh['region'=8,'tx'=4,'tz'=2,'ty'=4] {'tz'}, dimensions={0}, use_global_device_ids=true | all-gather | bytes 638976 | tf_op jit(solution)/shard_map/all_gather | solution.py:186
  36.7 0.8 reshape.29
  37.5 0.8 reshape.30
  38.4 1.5 copy.16.box_ref
  39.9 70.5 %all-gather.4.cloned.1.call-done = bf16[32,208,512]{2,1,0:T(8,128)(2,1)} async-done(((bf16[2,208,512]{2,1,0:T(8,128)(2,1)}), bf16[32,208,512]{2,1,0:T(8,128)(2,1)}) %all-gather.4.cloned.1.call-update) | async-done | bytes 6815760 | tf_op jit(solution)/shard_map/all_gather | solution.py:187
  110.4 1.0 slice_convert_fusion
  111.7 0.7 pad.26.s_ref
  112.6 0.7 pad.28.w_ref
  113.3 11.5 %shard_map.91 = (f32[2,512,512]{2,1,0:T(8,128)}, f32[16,512]{1,0:T(8,128)}) custom-call(bf16[6656,512]{1,0:T(8,128)(2,1)} %bitcast.19, f32[8,6656]{1,0:T(8,128)} %pad.26.s_ref, bf16[16,6656]{1,0:T(8,128)(2,1)} %pad.28.w_ref), custom_call_target="tpu_custom_call" | custom-call | tf_op jit(solution)/shard_map/pallas_call | solution.py:41
  124.8 50.7 %shard_map.92 = bf16[2,256,512]{2,1,0:T(8,128)(2,1)} custom-call(f32[2,512,512]{2,1,0:T(8,128)} %get-tuple-element.7.g_ref, f32[16,512]{1,0:T(8,128)} %get-tuple-element.8.v_ref, bf16[2,256,512]{2,1,0:T(8,128)(2,1)} %s_ref.1, s32[256,1]{1,0:T(8,128)} %copy.16.box_ref), custom_call_target="tpu_custom_call" | custom-call | tf_op jit(solution)/shard_map/pallas_call | solution.py:150
  (29 shorter events, 1.2 us)
Async XLA Ops:
  6.5 103.9 %all-gather.4.cloned.1.call-start = ((), (), s32[]{:S(2)}) async-start(), calls=%async_computation | async-start | bytes 7241728 | tf_op jit(solution)/shard_map/all_gather | solution.py:187
  12.0 9.9 %collective-permute-start.1 = (bf16[33,512]{1,0:T(8,128)(2,1)S(1)}, bf16[33,512]{1,0:T(8,128)(2,1)S(1)}, u32[]{:S(2)}, u32[]{:S(2)}) collective-permute-start(bf16[33,512]{1,0:T(8,128)(2,1)S(1)} %pad_maximum_fusion.1), channel_id=1, source_target_pairs={{32,0},{64,32},{96,64},{128,96},{160,128},{192,160},{224,192},{33,... | collective-permute-start | bytes 101384 | tf_op jit(solution)/shard_map/ppermute | solution.py:18
  20.0 3.1 %collective-permute-start = (bf16[33,512]{1,0:T(8,128)(2,1)S(1)}, bf16[33,512]{1,0:T(8,128)(2,1)S(1)}, u32[]{:S(2)}, u32[]{:S(2)}) collective-permute-start(bf16[33,512]{1,0:T(8,128)(2,1)S(1)} %pad_maximum_fusion), channel_id=1, source_target_pairs={{0,32},{32,64},{64,96},{96,128},{128,160},{160,192},{192,224},{1,3... | collective-permute-start | bytes 101384 | tf_op jit(solution)/shard_map/ppermute | solution.py:18
Sparse Core Ops, SparseCore 0:
  36.8 73.5 all-gather.3

commit v11 on v10

--- a/solution.py
+++ b/solution.py
@@ -25,7 +25,7 @@
         v_ref[...] = jnp.zeros(v_ref.shape, jnp.float32)
 
     a = a_ref[...]
-    at = a.astype(jnp.float32).T
+    at = a.T.astype(jnp.float32)
     for b in range(g_ref.shape[0]):
         sct = (at * s_ref[b:b + 1, :]).astype(jnp.bfloat16)
         g_ref[b] += jnp.dot(sct, a, preferred_element_type=jnp.float32)
@@ -65,6 +65,9 @@
     for b in range(boxes):
         m_ref[b] = g_ref[b] + (n - 1.0) * eye
     width = 4
+    sub8 = lax.broadcasted_iota(jnp.int32, (8, nb), 0)
+    lane8 = lax.broadcasted_iota(jnp.int32, (8, nb), 1)
+    sub1 = lax.broadcasted_iota(jnp.int32, (8, 1), 0)
     bi = lax.broadcasted_iota(jnp.int32, (nb, nb), 0)
     bj = lax.broadcasted_iota(jnp.int32, (nb, nb), 1)
     beye = (bi == bj).astype(jnp.float32)
@@ -81,10 +84,14 @@
         rmask = [bi == k + m for m in range(width)]
         lmask = [bj[0:1] == k + m for m in range(width)]
         out = []
+        grp = (bi // 8) == (k // 8)
+        kk = k % 8
         for d in blocks:
-            rows = [jnp.sum(jnp.where(rmask[m], d, 0.0), axis=0, keepdims=True) for m in range(width)]
+            g8 = jnp.sum(jnp.where(grp, d, 0.0).reshape(nb // 8, 8, nb), axis=0)
+            rows = [jnp.sum(jnp.where(sub8 == kk + m, g8, 0.0), axis=0, keepdims=True) for m in range(width)]
             cols = [jnp.sum(jnp.where(bj == k + m, d, 0.0), axis=1, keepdims=True) for m in range(width)]
-            p = [[jnp.sum(jnp.where(lmask[j], rows[i], 0.0), axis=1, keepdims=True)
+            pcol = [jnp.sum(jnp.where(lane8 == k + j, g8, 0.0), axis=1, keepdims=True) for j in range(width)]
+            p = [[jnp.sum(jnp.where(sub1 == kk + i, pcol[j], 0.0), axis=0, keepdims=True)
                   for j in range(width)] for i in range(width)]
             a = [[p[0][0], p[0][1]], [p[1][0], p[1][1]]]
             b = [[p[0][2], p[0][3]], [p[1][2], p[1][3]]]

time: 183 us -> 182 us (level)
  no operation moved by 1% of the time
where the time goes in v11:
time: 182 us
  waiting for transfers between devices  71.7 us (39%)
  Pallas kernels  61.5 us (34%)
  between operations  13.5 us (7%)
  blocking collectives  13.2 us (7%)
  local copies, waits for them, and re-layouts  9.53 us (5%)
  starting transfers between devices  7.07 us (4%)
  other arithmetic  5.22 us (3%)
    all_gather x1, waiting for transfers between devices, body(): full = lax.all_gather(half, ('tx', 'ty'), axis=0)  70.5 us
    pallas_call x1, Pallas kernels, analysis_of(): pl.pallas_call(functools.partial(_transform_kernel, nb=nb), out_shape=jax...  50.1 us
    all_gather x1, blocking collectives, body(): half = lax.all_gather(block, 'tz', axis=0)  13.2 us
    pallas_call x1, Pallas kernels, gram_terms(): pl.pallas_call(_gram_kernel, grid=(rows // step,), in_specs=[pl.BlockSpec...  11.4 us
    ppermute x2, starting transfers between devices, passed_along(): return lax.ppermute(block, axis, route)  7.06 us
  transfers between devices with their start and end apart: 3, of which 2 were waited for; matrix products, arithmetic and copies ran while one was open for 3% of the time, Pallas kernels for 0%

profile of v11, /device:TPU:1, one launch (start us, length us, event | category | flops | bytes accessed | tf_op | source)
XLA Modules:
  0.0 181.7 jit_solution(12984296547836165480)
XLA Ops:
  6.5 1.0 convert_reduce_fusion
  7.5 0.7 compare_select_fusion
  8.2 0.7 subtract_convert_fusion
  8.9 0.7 gather_fusion.4
  9.6 0.7 gather_fusion.5
  10.4 1.0 fusion
  11.4 0.6 gather_fusion.3
  12.0 5.1 %collective-permute-start.1 = (bf16[33,512]{1,0:T(8,128)(2,1)S(1)}, bf16[33,512]{1,0:T(8,128)(2,1)S(1)}, u32[]{:S(2)}, u32[]{:S(2)}) collective-permute-start(bf16[33,512]{1,0:T(8,128)(2,1)S(1)} %pad_maximum_fusion.1), channel_id=1, source_target_pairs={{32,0},{64,32},{96,64},{128,96},{160,128},{192,160},{224,192},{33,... | collective-permute-start | bytes 101384 | tf_op jit(solution)/shard_map/ppermute | solution.py:18
  17.2 0.7 compare_select_fusion.1
  17.9 0.7 gather_fusion.1
  18.6 0.7 gather_fusion.2
  19.3 0.6 gather_fusion
  20.0 1.9 %collective-permute-start = (bf16[33,512]{1,0:T(8,128)(2,1)S(1)}, bf16[33,512]{1,0:T(8,128)(2,1)S(1)}, u32[]{:S(2)}, u32[]{:S(2)}) collective-permute-start(bf16[33,512]{1,0:T(8,128)(2,1)S(1)} %pad_maximum_fusion), channel_id=1, source_target_pairs={{0,32},{32,64},{64,96},{96,128},{128,160},{160,192},{192,224},{1,3... | collective-permute-start | bytes 101384 | tf_op jit(solution)/shard_map/ppermute | solution.py:18
  22.0 1.1 collective-permute-done
  23.5 13.2 %all-gather = bf16[416,512]{1,0:T(8,128)(2,1)} all-gather(bf16[208,512]{1,0:T(8,128)(2,1)S(1)} %concatenate.26), channel_id=2, replica_groups=mesh['region'=8,'tx'=4,'tz'=2,'ty'=4] {'tz'}, dimensions={0}, use_global_device_ids=true | all-gather | bytes 638976 | tf_op jit(solution)/shard_map/all_gather | solution.py:193
  36.7 0.8 reshape.29
  37.5 0.8 reshape.30
  38.4 1.5 copy.16.box_ref
  39.9 70.5 %all-gather.4.cloned.1.call-done = bf16[32,208,512]{2,1,0:T(8,128)(2,1)} async-done(((bf16[2,208,512]{2,1,0:T(8,128)(2,1)}), bf16[32,208,512]{2,1,0:T(8,128)(2,1)}) %all-gather.4.cloned.1.call-update) | async-done | bytes 6815760 | tf_op jit(solution)/shard_map/all_gather | solution.py:194
  110.4 1.0 slice_convert_fusion
  111.7 0.7 pad.26.s_ref
  112.6 0.7 pad.28.w_ref
  113.3 11.4 %shard_map.91 = (f32[2,512,512]{2,1,0:T(8,128)}, f32[16,512]{1,0:T(8,128)}) custom-call(bf16[6656,512]{1,0:T(8,128)(2,1)} %bitcast.19, f32[8,6656]{1,0:T(8,128)} %pad.26.s_ref, bf16[16,6656]{1,0:T(8,128)(2,1)} %pad.28.w_ref), custom_call_target="tpu_custom_call" | custom-call | tf_op jit(solution)/shard_map/pallas_call | solution.py:41
  124.7 50.1 %shard_map.92 = bf16[2,256,512]{2,1,0:T(8,128)(2,1)} custom-call(f32[2,512,512]{2,1,0:T(8,128)} %get-tuple-element.7.g_ref, f32[16,512]{1,0:T(8,128)} %get-tuple-element.8.v_ref, bf16[2,256,512]{2,1,0:T(8,128)(2,1)} %s_ref.1, s32[256,1]{1,0:T(8,128)} %copy.16.box_ref), custom_call_target="tpu_custom_call" | custom-call | tf_op jit(solution)/shard_map/pallas_call | solution.py:157
  (29 shorter events, 1.2 us)
Async XLA Ops:
  6.5 103.9 %all-gather.4.cloned.1.call-start = ((), (), s32[]{:S(2)}) async-start(), calls=%async_computation | async-start | bytes 7241728 | tf_op jit(solution)/shard_map/all_gather | solution.py:194
  12.0 9.9 %collective-permute-start.1 = (bf16[33,512]{1,0:T(8,128)(2,1)S(1)}, bf16[33,512]{1,0:T(8,128)(2,1)S(1)}, u32[]{:S(2)}, u32[]{:S(2)}) collective-permute-start(bf16[33,512]{1,0:T(8,128)(2,1)S(1)} %pad_maximum_fusion.1), channel_id=1, source_target_pairs={{32,0},{64,32},{96,64},{128,96},{160,128},{192,160},{224,192},{33,... | collective-permute-start | bytes 101384 | tf_op jit(solution)/shard_map/ppermute | solution.py:18
  20.0 3.1 %collective-permute-start = (bf16[33,512]{1,0:T(8,128)(2,1)S(1)}, bf16[33,512]{1,0:T(8,128)(2,1)S(1)}, u32[]{:S(2)}, u32[]{:S(2)}) collective-permute-start(bf16[33,512]{1,0:T(8,128)(2,1)S(1)} %pad_maximum_fusion), channel_id=1, source_target_pairs={{0,32},{32,64},{64,96},{96,128},{128,160},{160,192},{192,224},{1,3... | collective-permute-start | bytes 101384 | tf_op jit(solution)/shard_map/ppermute | solution.py:18
Sparse Core Ops, SparseCore 0:
  36.8 73.5 all-gather.3

commit v12 on v11

--- a/solution.py
+++ b/solution.py
@@ -176,21 +176,33 @@
         info = jnp.pad(info, (0, members - info.shape[0]))
         return jnp.concatenate([anomaly[index], info[None]], axis=0)
 
-    lower = passed_along(edge_payload(edge_up), "region", 1)
-    upper = passed_along(edge_payload(edge_down), "region", -1)
     edge = edge_up.shape[0]
-    lower_a, lower_v, lower_i = lower[:edge], lower[edge, :edge], lower[edge, edge:2 * edge]
-    upper_a, upper_v, upper_i = upper[:edge], upper[edge, :edge], upper[edge, edge:2 * edge]
-    edge_rows = lower_a.shape[0] + upper_a.shape[0]
+    n_region = lax.axis_size("region")
+    up_payload, down_payload = edge_payload(edge_up), edge_payload(edge_down)
+    cross_up = [(r * nz + t, (r + 1) * nz + (1 - t)) for r in range(n_region - 1) for t in range(nz)]
+    cross_down = [((r + 1) * nz + t, r * nz + (1 - t)) for r in range(n_region - 1) for t in range(nz)]
+    same = (passed_along(up_payload, "region", 1), passed_along(down_payload, "region", -1))
+    cross = (lax.ppermute(up_payload, ("region", "tz"), cross_up),
+             lax.ppermute(down_payload, ("region", "tz"), cross_down))
+    own_info = jnp.pad(jnp.concatenate([inv_var, innov]), (0, members - 2 * record_count))
+    own = jnp.concatenate([anomaly, own_info[None]], axis=0)
+    own_half = lax.all_gather(own, "tz", axis=0)
+    edge_rows = 2 * edge
     pool_rows = record_count + edge_rows
     block_rows = ((pool_rows + 1 + 15) // 16) * 16
-    info_row = jnp.concatenate(
-        [inv_var, lower_v, upper_v, innov, lower_i, upper_i,
-         jnp.zeros((members - 2 * pool_rows,), jnp.bfloat16)])
-    block = jnp.concatenate(
-        [anomaly, lower_a, upper_a, info_row[None],
-         jnp.zeros((block_rows - pool_rows - 1, members), jnp.bfloat16)], axis=0)
-    half = lax.all_gather(block, "tz", axis=0)
+    tz_at = lax.axis_index("tz")
+    blocks = []
+    for k in range(nz):
+        lower, upper = [jnp.where(tz_at == k, s, c) for s, c in zip(same, cross)]
+        info = own_half[k, record_count]
+        info_row = jnp.concatenate(
+            [info[:record_count], lower[edge, :edge], upper[edge, :edge],
+             info[record_count:2 * record_count], lower[edge, edge:2 * edge], upper[edge, edge:2 * edge],
+             jnp.zeros((members - 2 * pool_rows,), jnp.bfloat16)])
+        blocks.append(jnp.concatenate(
+            [own_half[k, :record_count], lower[:edge], upper[:edge], info_row[None],
+             jnp.zeros((block_rows - pool_rows - 1, members), jnp.bfloat16)], axis=0))
+    half = jnp.stack(blocks)
     full = lax.all_gather(half, ("tx", "ty"), axis=0)
     info = full[:, :, pool_rows, :2 * pool_rows].astype(jnp.float32)
     inv_all = info[:, :, :pool_rows]

time: 182 us -> 187 us (1.027)
  starting transfers between devices: 7.07 us -> 16.6 us
  blocking collectives: 13.2 us -> 9.37 us
    ppermute x0 -> x2, starting transfers between devices: none -> 8.27 us  [the longest x1 6.35 us: body(): lax.ppermute(down_payload, ('region', 'tz'), cross_down)]
    all_gather x1, blocking collectives: 13.2 us -> 9.37 us  [body(): own_half = lax.all_gather(own, 'tz', axis=0)]
  transfers between devices with their start and end apart: 3 -> 5, of which waited for: 2 -> 1; matrix products, arithmetic and copies ran while one was open for 3% -> 2% of each run, Pallas kernels for 0% -> 0%
where the time goes in v12:
time: 187 us
  waiting for transfers between devices  71.7 us (38%)
  Pallas kernels  61.6 us (33%)
  starting transfers between devices  16.6 us (9%)
  between operations  13.7 us (7%)
  blocking collectives  9.37 us (5%)
  local copies, waits for them, and re-layouts  7.85 us (4%)
  other arithmetic  6.06 us (3%)
    all_gather x1, waiting for transfers between devices, body(): full = lax.all_gather(half, ('tx', 'ty'), axis=0)  71.7 us
    pallas_call x1, Pallas kernels, analysis_of(): pl.pallas_call(functools.partial(_transform_kernel, nb=nb), out_shape=jax...  50.1 us
    pallas_call x1, Pallas kernels, gram_terms(): pl.pallas_call(_gram_kernel, grid=(rows // step,), in_specs=[pl.BlockSpec...  11.4 us
    all_gather x1, blocking collectives, body(): own_half = lax.all_gather(own, 'tz', axis=0)  9.37 us
    ppermute x2, starting transfers between devices, passed_along(): return lax.ppermute(block, axis, route)  8.33 us
    ppermute x1, starting transfers between devices, body(): lax.ppermute(down_payload, ('region', 'tz'), cross_down)  6.35 us
  transfers between devices with their start and end apart: 5, of which 1 were waited for; matrix products, arithmetic and copies ran while one was open for 2% of the time, Pallas kernels for 0%

profile of v12, /device:TPU:1, one launch (start us, length us, event | category | flops | bytes accessed | tf_op | source)
XLA Modules:
  0.0 186.8 jit_solution(12778139215707889216)
XLA Ops:
  6.5 1.0 convert_reduce_fusion
  7.6 0.7 compare_select_fusion
  8.2 0.7 compare_select_fusion.1
  8.9 0.7 broadcast_multiply_fusion.1
  9.6 0.7 gather_fusion.4
  10.3 0.7 gather_fusion.5
  11.0 1.0 fusion
  12.0 0.6 gather_fusion.3
  12.7 5.1 %collective-permute-start.2 = (bf16[33,512]{1,0:T(8,128)(2,1)S(1)}, bf16[33,512]{1,0:T(8,128)(2,1)S(1)}, u32[]{:S(2)}, u32[]{:S(2)}) collective-permute-start(bf16[33,512]{1,0:T(8,128)(2,1)S(1)} %constant_dynamic-update-slice_fusion.2), channel_id=1, source_target_pairs={{32,0},{64,32},{96,64},{128,96},{160,128},{192,160},{224,192},{33,... | collective-permute-start | bytes 101384 | tf_op jit(solution)/shard_map/ppermute | solution.py:18
  17.9 6.4 %collective-permute-start.3 = (bf16[33,512]{1,0:T(8,128)(2,1)S(1)}, bf16[33,512]{1,0:T(8,128)(2,1)S(1)}, u32[]{:S(2)}, u32[]{:S(2)}) collective-permute-start(bf16[33,512]{1,0:T(8,128)(2,1)S(1)} %constant_dynamic-update-slice_fusion.2), channel_id=1, source_target_pairs={{32,4},{36,0},{64,36},{68,32},{96,68},{100,64},{128,100},{132,96},... | collective-permute-start | bytes 101384 | tf_op jit(solution)/shard_map/ppermute | solution.py:186
  24.2 0.7 gather_fusion.1
  24.9 0.7 gather_fusion.2
  25.7 0.6 gather_fusion
  26.4 3.2 %collective-permute-start = (bf16[33,512]{1,0:T(8,128)(2,1)S(1)}, bf16[33,512]{1,0:T(8,128)(2,1)S(1)}, u32[]{:S(2)}, u32[]{:S(2)}) collective-permute-start(bf16[33,512]{1,0:T(8,128)(2,1)S(1)} %constant_dynamic-update-slice_fusion), channel_id=1, source_target_pairs={{0,32},{32,64},{64,96},{96,128},{128,160},{160,192},{192,224},{1,3... | collective-permute-start | bytes 101384 | tf_op jit(solution)/shard_map/ppermute | solution.py:18
  29.6 1.9 %collective-permute-start.1 = (bf16[33,512]{1,0:T(8,128)(2,1)S(1)}, bf16[33,512]{1,0:T(8,128)(2,1)S(1)}, u32[]{:S(2)}, u32[]{:S(2)}) collective-permute-start(bf16[33,512]{1,0:T(8,128)(2,1)S(1)} %constant_dynamic-update-slice_fusion), channel_id=1, source_target_pairs={{0,36},{4,32},{32,68},{36,64},{64,100},{68,96},{96,132},{100,128},... | collective-permute-start | bytes 101384 | tf_op jit(solution)/shard_map/ppermute | solution.py:185
  31.6 9.4 %all-gather.2 = bf16[2,129,512]{2,1,0:T(8,128)(2,1)S(1)} all-gather(bf16[1,129,512]{2,1,0:T(8,128)(2,1)S(1)} %maximum_bitcast_fusion), channel_id=2, replica_groups=mesh['region'=8,'tx'=4,'tz'=2,'ty'=4] {'tz'}, dimensions={0}, use_global_device_ids=true | all-gather | bytes 396288 | tf_op jit(solution)/shard_map/all_gather | solution.py:189
  41.9 0.8 pad_maximum_fusion
  43.0 0.8 copy.14.box_ref
  43.8 71.7 %all-gather.5.cloned.1.call-done = bf16[32,208,512]{2,1,0:T(8,128)(2,1)} async-done(((bf16[2,208,512]{2,1,0:T(8,128)(2,1)}), bf16[32,208,512]{2,1,0:T(8,128)(2,1)}) %all-gather.5.cloned.1.call-update) | async-done | bytes 6815760 | tf_op jit(solution)/shard_map/all_gather | solution.py:206
  115.5 1.0 slice_convert_fusion
  116.8 0.7 pad.31.s_ref
  117.7 0.7 pad.33.w_ref
  118.4 11.4 %shard_map.91 = (f32[2,512,512]{2,1,0:T(8,128)}, f32[16,512]{1,0:T(8,128)}) custom-call(bf16[6656,512]{1,0:T(8,128)(2,1)} %bitcast.42, f32[8,6656]{1,0:T(8,128)} %pad.31.s_ref, bf16[16,6656]{1,0:T(8,128)(2,1)} %pad.33.w_ref), custom_call_target="tpu_custom_call" | custom-call | tf_op jit(solution)/shard_map/pallas_call | solution.py:41
  129.8 50.1 %shard_map.92 = bf16[2,256,512]{2,1,0:T(8,128)(2,1)} custom-call(f32[2,512,512]{2,1,0:T(8,128)} %get-tuple-element.7.g_ref, f32[16,512]{1,0:T(8,128)} %get-tuple-element.8.v_ref, bf16[2,256,512]{2,1,0:T(8,128)(2,1)} %s_ref.1, s32[256,1]{1,0:T(8,128)} %copy.14.box_ref), custom_call_target="tpu_custom_call" | custom-call | tf_op jit(solution)/shard_map/pallas_call | solution.py:157
  (53 shorter events, 1.9 us)
Async XLA Ops:
  6.5 36.2 %copy-start = (f32[2,4096]{1,0:T(2,128)S(1)}, f32[2,4096]{1,0:T(2,128)}, u32[]{:S(2)}) copy-start(f32[2,4096]{1,0:T(2,128)} %param.14) | copy-start | bytes 98308
  6.5 36.3 %copy-start.1 = (f32[2,2048]{1,0:T(2,128)S(1)}, f32[2,2048]{1,0:T(2,128)}, u32[]{:S(2)}) copy-start(f32[2,2048]{1,0:T(2,128)} %param.15) | copy-start | bytes 49156
  6.5 36.5 %copy-start.2 = (s32[256]{0:T(256)S(1)}, s32[256]{0:T(256)}, u32[]{:S(2)}) copy-start(s32[256]{0:T(256)} %param.17) | copy-start | bytes 3076
  6.5 108.9 %all-gather.5.cloned.1.call-start = ((), (), s32[]{:S(2)}) async-start(), calls=%async_computation | async-start | bytes 7241728 | tf_op jit(solution)/shard_map/all_gather | solution.py:206
  12.7 28.4 %collective-permute-start.2 = (bf16[33,512]{1,0:T(8,128)(2,1)S(1)}, bf16[33,512]{1,0:T(8,128)(2,1)S(1)}, u32[]{:S(2)}, u32[]{:S(2)}) collective-permute-start(bf16[33,512]{1,0:T(8,128)(2,1)S(1)} %constant_dynamic-update-slice_fusion.2), channel_id=1, source_target_pairs={{32,0},{64,32},{96,64},{128,96},{160,128},{192,160},{224,192},{33,... | collective-permute-start | bytes 101384 | tf_op jit(solution)/shard_map/ppermute | solution.py:18
  17.9 23.2 %collective-permute-start.3 = (bf16[33,512]{1,0:T(8,128)(2,1)S(1)}, bf16[33,512]{1,0:T(8,128)(2,1)S(1)}, u32[]{:S(2)}, u32[]{:S(2)}) collective-permute-start(bf16[33,512]{1,0:T(8,128)(2,1)S(1)} %constant_dynamic-update-slice_fusion.2), channel_id=1, source_target_pairs={{32,4},{36,0},{64,36},{68,32},{96,68},{100,64},{128,100},{132,96},... | collective-permute-start | bytes 101384 | tf_op jit(solution)/shard_map/ppermute | solution.py:186
  26.4 14.6 %collective-permute-start = (bf16[33,512]{1,0:T(8,128)(2,1)S(1)}, bf16[33,512]{1,0:T(8,128)(2,1)S(1)}, u32[]{:S(2)}, u32[]{:S(2)}) collective-permute-start(bf16[33,512]{1,0:T(8,128)(2,1)S(1)} %constant_dynamic-update-slice_fusion), channel_id=1, source_target_pairs={{0,32},{32,64},{64,96},{96,128},{128,160},{160,192},{192,224},{1,3... | collective-permute-start | bytes 101384 | tf_op jit(solution)/shard_map/ppermute | solution.py:18
  29.6 11.4 %collective-permute-start.1 = (bf16[33,512]{1,0:T(8,128)(2,1)S(1)}, bf16[33,512]{1,0:T(8,128)(2,1)S(1)}, u32[]{:S(2)}, u32[]{:S(2)}) collective-permute-start(bf16[33,512]{1,0:T(8,128)(2,1)S(1)} %constant_dynamic-update-slice_fusion), channel_id=1, source_target_pairs={{0,36},{4,32},{32,68},{36,64},{64,100},{68,96},{96,132},{100,128},... | collective-permute-start | bytes 101384 | tf_op jit(solution)/shard_map/ppermute | solution.py:185
Sparse Core Ops, SparseCore 0:
  42.9 72.5 all-gather.4
